TPU v7x, 512 devices: a whole 4x4x16 slice. The times are simulated.
512 devices in a mesh: blk: 64 (over y, x, z_hi, core), mp: 8 (over z_lo).
Axes of the slice: x: 4, y: 4, z: 16 (z_hi: 2, z_lo: 8; z = z_hi * 8 + z_lo), core: 2. Of those that a mesh axis runs over, the one named last changes fastest.
Arguments:
- queries: bfloat16 [16384, 5120], P('blk', 'mp'), may hold values from -8.5 to 8.5
- suffix_key_rows: bfloat16 [16384, 1024], P('blk', 'mp'), may hold values from -6 to 6
- suffix_value_rows: bfloat16 [16384, 1024], P('blk', 'mp'), may hold values from -6 to 6
- shared_prefix_keys: bfloat16 [2048, 1024], P('blk', 'mp'), may hold values from -8.5 to 8.5
- shared_prefix_values: bfloat16 [2048, 1024], P('blk', 'mp'), may hold values from -6 to 6
- out_weight: bfloat16 [5120, 5120], P('mp', 'blk'), may hold values from -0.078125 to 0.078125
- lengths: int32 [16], replicated, may hold values from 1 to 4096, 16384 in all
Outputs:
- output: bfloat16 [16384, 5120], P('blk', 'mp')
Inputs may be any that keep to these rules, and one draw needn't show every extreme that they name: The lengths sum to 16384; the longest is exactly 4096.
All inputs are finite; a program needn't handle non-finite values.
Results may differ from a plain program's by a relative error of at most 0.019.
Values may be sent and summed in bfloat16 or wider, within the bound.
No kernel may reach another device: no remote copies, remote signals or barrier semaphores. Data moves between devices by JAX's collectives and lax.ppermute only.
A program may use at most 64 MiB of HBM per device.

v0:
```python
import math

import jax
import jax.numpy as jnp
from jax import lax
from jax.sharding import PartitionSpec as P

HEAD_SIZE = 128


MASKED_SCORE = -1e30


def passed_along(block, axis, distance):
    devices = range(lax.axis_size(axis))
    route = [(i - distance, i) for i in devices if i - distance in devices]
    return lax.ppermute(block, axis, route)


def per_device(
    queries,
    suffix_key_rows,
    suffix_value_rows,
    shared_prefix_keys,
    shared_prefix_values,
    out_weight,
    lengths,
):
    tok_rows = queries.shape[0]
    kv_heads = suffix_key_rows.shape[1] // HEAD_SIZE
    q_heads = queries.shape[1] // HEAD_SIZE
    heads_per_group = q_heads // kv_heads
    blocks = lax.axis_size("blk")
    cycle_reach = blocks // 4
    my_block = lax.axis_index("blk")
    score_scale = 1.0 / math.sqrt(HEAD_SIZE)
    heads_of_query = queries.reshape(tok_rows, kv_heads, heads_per_group, HEAD_SIZE)
    req_ends = jnp.cumsum(lengths)
    local_rows = jnp.arange(tok_rows, dtype=jnp.int32)
    query_pos = my_block * tok_rows + local_rows

    def owner_of(position):
        return jnp.sum((position[:, None] >= req_ends[None, :]).astype(jnp.int32), axis=1)

    query_owner = owner_of(query_pos)

    def update(carry_state, key_block, value_block, visible):
        run_max, row_total, accumulated = carry_state
        count = key_block.shape[0]
        key_heads = key_block.reshape(count, kv_heads, HEAD_SIZE)
        value_heads = value_block.reshape(count, kv_heads, HEAD_SIZE)
        scores = (
            jnp.einsum(
                "qhgd,khd->hgqk", heads_of_query, key_heads, preferred_element_type=jnp.float32
            )
            * score_scale
        )
        if visible is not None:
            scores = jnp.where(visible[None, None], scores, MASKED_SCORE)
        new_max = jnp.maximum(run_max, jnp.max(scores, axis=-1))
        weights = jnp.exp(scores - new_max[..., None])
        if visible is not None:
            weights = jnp.where(visible[None, None], weights, 0.0)
        rescale = jnp.exp(run_max - new_max)
        row_total = row_total * rescale + jnp.sum(weights, axis=-1)
        contrib = jnp.einsum(
            "hgqk,khd->hgqd",
            weights.astype(jnp.bfloat16),
            value_heads,
            preferred_element_type=jnp.float32,
        )
        accumulated = accumulated * rescale[..., None] + contrib
        return (new_max, row_total, accumulated)

    start_state = (
        jnp.full((kv_heads, heads_per_group, tok_rows), MASKED_SCORE, jnp.float32),
        jnp.zeros((kv_heads, heads_per_group, tok_rows), jnp.float32),
        jnp.zeros((kv_heads, heads_per_group, tok_rows, HEAD_SIZE), jnp.float32),
    )
    carry_state = update(
        start_state,
        lax.all_gather(shared_prefix_keys, "blk", axis=0, tiled=True),
        lax.all_gather(shared_prefix_values, "blk", axis=0, tiled=True),
        None,
    )

    def visible_from(distance):
        key_pos = (my_block - distance) * tok_rows + local_rows
        key_owner = owner_of(key_pos)
        return (
            (key_owner[None, :] == query_owner[:, None])
            & (key_pos[None, :] <= query_pos[:, None])
            & (key_pos[None, :] >= 0)
        )

    kv_pair = jnp.stack((suffix_key_rows, suffix_value_rows))
    carry_state = update(carry_state, kv_pair[0], kv_pair[1], visible_from(0))

    def advance(distance, loop_carry):
        current, moving = loop_carry
        moving = passed_along(moving, "blk", 1)
        visible = visible_from(distance)
        current = update(current, moving[0], moving[1], visible)
        return (current, moving)

    carry_state, kv_pair = lax.fori_loop(1, cycle_reach + 1, advance, (carry_state, kv_pair))
    run_max, row_total, accumulated = carry_state
    attended = accumulated / row_total[..., None]
    attn = (
        jnp.transpose(attended, (2, 0, 1, 3))
        .reshape(tok_rows, q_heads * HEAD_SIZE)
        .astype(jnp.bfloat16)
    )
    product = jnp.dot(
        attn,
        lax.all_gather(out_weight, "blk", axis=1, tiled=True),
        preferred_element_type=jnp.float32,
    )
    return lax.psum_scatter(product.astype(jnp.bfloat16), "mp", scatter_dimension=1, tiled=True)


def solution(mesh):
    placed = (
        P("blk", "mp"),
        P("blk", "mp"),
        P("blk", "mp"),
        P("blk", "mp"),
        P("blk", "mp"),
        P("mp", "blk"),
        P(),
    )
    return jax.shard_map(
        per_device, mesh=mesh, in_specs=placed, out_specs=P("blk", "mp"), check_vma=False
    )
```

profile of v0, /device:TPU:1, one launch (start us, length us, event | category | flops | bytes accessed | tf_op | source)
XLA Modules:
  0.0 751.2 jit_solution(11717746178946045109)
XLA Ops:
  9.4 197.9 %all_gather.9 = bf16[2048,128]{1,0:T(8,128)(2,1)S(1)} all-gather(bf16[32,128]{1,0:T(8,128)(2,1)} %param.12), channel_id=1, replica_groups=mesh['blk'=64,'mp'=8] {'blk'}, dimensions={0}, use_global_device_ids=true | all-gather | bytes 532480 | tf_op jit(solution)/shard_map/all_gather | solution.py:82
  207.3 148.2 %all_gather.10 = bf16[2048,128]{1,0:T(8,128)(2,1)S(1)} all-gather(bf16[32,128]{1,0:T(8,128)(2,1)S(1)} %copy-done.2), channel_id=1, replica_groups=mesh['blk'=64,'mp'=8] {'blk'}, dimensions={0}, use_global_device_ids=true | all-gather | bytes 532480 | tf_op jit(solution)/shard_map/all_gather | solution.py:83
  362.8 272.1 %while.20 = (s32[]{:T(128)}, f32[1,5,256]{2,1,0:T(8,128)S(1)}, f32[1,5,256]{2,1,0:T(8,128)S(1)}, f32[1,5,256,128]{3,2,1,0:T(8,128)S(1)}, bf16[2,256,128]{2,1,0:T...) while((s32[]{:T(128)}, f32[1,5,256]{2,1,0:T(8,128)S(1)}, ...), condition=%wide.region_10.11_spmd.clone, body=%wide.region_6.0_spmd.clone.sunk | while | flops 171328000 | bytes 6847233 | solution.py:106
  362.9 12.0 %collective-permute-start = (bf16[2,256,128]{2,1,0:T(8,128)(2,1)S(1)}, bf16[2,256,128]{2,1,0:T(8,128)(2,1)S(1)}, u32[]{:S(2)}, u32[]{:S(2)}) collective-permute-start(bf16[2,256,128]{2,1,0:T(8,128)(2,1)S(1)} %get-tuple-element.371), channel_id=1, source_target_pairs={{0,8},{8,16},{16,24},{24,32},{32,40},{40,48},{48,56},{56,64},{64,7... | collective-permute-start | bytes 393224 | tf_op jit(solution)/shard_map/while/body/eval_jaxpr/ppermute | solution.py:17
  378.1 14.5 %collective-permute-start = (bf16[2,256,128]{2,1,0:T(8,128)(2,1)S(1)}, bf16[2,256,128]{2,1,0:T(8,128)(2,1)S(1)}, u32[]{:S(2)}, u32[]{:S(2)}) collective-permute-start(bf16[2,256,128]{2,1,0:T(8,128)(2,1)S(1)} %get-tuple-element.371), channel_id=1, source_target_pairs={{0,8},{8,16},{16,24},{24,32},{32,40},{40,48},{48,56},{56,64},{64,7... | collective-permute-start | bytes 393224 | tf_op jit(solution)/shard_map/while/body/eval_jaxpr/ppermute | solution.py:17
  392.9 3.0 collective-permute-done
  397.1 13.2 %collective-permute-start = (bf16[2,256,128]{2,1,0:T(8,128)(2,1)S(1)}, bf16[2,256,128]{2,1,0:T(8,128)(2,1)S(1)}, u32[]{:S(2)}, u32[]{:S(2)}) collective-permute-start(bf16[2,256,128]{2,1,0:T(8,128)(2,1)S(1)} %get-tuple-element.371), channel_id=1, source_target_pairs={{0,8},{8,16},{16,24},{24,32},{32,40},{40,48},{48,56},{56,64},{64,7... | collective-permute-start | bytes 393224 | tf_op jit(solution)/shard_map/while/body/eval_jaxpr/ppermute | solution.py:17
  413.7 13.1 %collective-permute-start = (bf16[2,256,128]{2,1,0:T(8,128)(2,1)S(1)}, bf16[2,256,128]{2,1,0:T(8,128)(2,1)S(1)}, u32[]{:S(2)}, u32[]{:S(2)}) collective-permute-start(bf16[2,256,128]{2,1,0:T(8,128)(2,1)S(1)} %get-tuple-element.371), channel_id=1, source_target_pairs={{0,8},{8,16},{16,24},{24,32},{32,40},{40,48},{48,56},{56,64},{64,7... | collective-permute-start | bytes 393224 | tf_op jit(solution)/shard_map/while/body/eval_jaxpr/ppermute | solution.py:17
  430.0 13.1 %collective-permute-start = (bf16[2,256,128]{2,1,0:T(8,128)(2,1)S(1)}, bf16[2,256,128]{2,1,0:T(8,128)(2,1)S(1)}, u32[]{:S(2)}, u32[]{:S(2)}) collective-permute-start(bf16[2,256,128]{2,1,0:T(8,128)(2,1)S(1)} %get-tuple-element.371), channel_id=1, source_target_pairs={{0,8},{8,16},{16,24},{24,32},{32,40},{40,48},{48,56},{56,64},{64,7... | collective-permute-start | bytes 393224 | tf_op jit(solution)/shard_map/while/body/eval_jaxpr/ppermute | solution.py:17
  446.4 13.1 %collective-permute-start = (bf16[2,256,128]{2,1,0:T(8,128)(2,1)S(1)}, bf16[2,256,128]{2,1,0:T(8,128)(2,1)S(1)}, u32[]{:S(2)}, u32[]{:S(2)}) collective-permute-start(bf16[2,256,128]{2,1,0:T(8,128)(2,1)S(1)} %get-tuple-element.371), channel_id=1, source_target_pairs={{0,8},{8,16},{16,24},{24,32},{32,40},{40,48},{48,56},{56,64},{64,7... | collective-permute-start | bytes 393224 | tf_op jit(solution)/shard_map/while/body/eval_jaxpr/ppermute | solution.py:17
  462.7 13.1 %collective-permute-start = (bf16[2,256,128]{2,1,0:T(8,128)(2,1)S(1)}, bf16[2,256,128]{2,1,0:T(8,128)(2,1)S(1)}, u32[]{:S(2)}, u32[]{:S(2)}) collective-permute-start(bf16[2,256,128]{2,1,0:T(8,128)(2,1)S(1)} %get-tuple-element.371), channel_id=1, source_target_pairs={{0,8},{8,16},{16,24},{24,32},{32,40},{40,48},{48,56},{56,64},{64,7... | collective-permute-start | bytes 393224 | tf_op jit(solution)/shard_map/while/body/eval_jaxpr/ppermute | solution.py:17
  479.5 13.1 %collective-permute-start = (bf16[2,256,128]{2,1,0:T(8,128)(2,1)S(1)}, bf16[2,256,128]{2,1,0:T(8,128)(2,1)S(1)}, u32[]{:S(2)}, u32[]{:S(2)}) collective-permute-start(bf16[2,256,128]{2,1,0:T(8,128)(2,1)S(1)} %get-tuple-element.371), channel_id=1, source_target_pairs={{0,8},{8,16},{16,24},{24,32},{32,40},{40,48},{48,56},{56,64},{64,7... | collective-permute-start | bytes 393224 | tf_op jit(solution)/shard_map/while/body/eval_jaxpr/ppermute | solution.py:17
  492.9 2.6 collective-permute-done
  496.7 13.2 %collective-permute-start = (bf16[2,256,128]{2,1,0:T(8,128)(2,1)S(1)}, bf16[2,256,128]{2,1,0:T(8,128)(2,1)S(1)}, u32[]{:S(2)}, u32[]{:S(2)}) collective-permute-start(bf16[2,256,128]{2,1,0:T(8,128)(2,1)S(1)} %get-tuple-element.371), channel_id=1, source_target_pairs={{0,8},{8,16},{16,24},{24,32},{32,40},{40,48},{48,56},{56,64},{64,7... | collective-permute-start | bytes 393224 | tf_op jit(solution)/shard_map/while/body/eval_jaxpr/ppermute | solution.py:17
  514.0 13.2 %collective-permute-start = (bf16[2,256,128]{2,1,0:T(8,128)(2,1)S(1)}, bf16[2,256,128]{2,1,0:T(8,128)(2,1)S(1)}, u32[]{:S(2)}, u32[]{:S(2)}) collective-permute-start(bf16[2,256,128]{2,1,0:T(8,128)(2,1)S(1)} %get-tuple-element.371), channel_id=1, source_target_pairs={{0,8},{8,16},{16,24},{24,32},{32,40},{40,48},{48,56},{56,64},{64,7... | collective-permute-start | bytes 393224 | tf_op jit(solution)/shard_map/while/body/eval_jaxpr/ppermute | solution.py:17
  531.3 13.2 %collective-permute-start = (bf16[2,256,128]{2,1,0:T(8,128)(2,1)S(1)}, bf16[2,256,128]{2,1,0:T(8,128)(2,1)S(1)}, u32[]{:S(2)}, u32[]{:S(2)}) collective-permute-start(bf16[2,256,128]{2,1,0:T(8,128)(2,1)S(1)} %get-tuple-element.371), channel_id=1, source_target_pairs={{0,8},{8,16},{16,24},{24,32},{32,40},{40,48},{48,56},{56,64},{64,7... | collective-permute-start | bytes 393224 | tf_op jit(solution)/shard_map/while/body/eval_jaxpr/ppermute | solution.py:17
  548.6 13.2 %collective-permute-start = (bf16[2,256,128]{2,1,0:T(8,128)(2,1)S(1)}, bf16[2,256,128]{2,1,0:T(8,128)(2,1)S(1)}, u32[]{:S(2)}, u32[]{:S(2)}) collective-permute-start(bf16[2,256,128]{2,1,0:T(8,128)(2,1)S(1)} %get-tuple-element.371), channel_id=1, source_target_pairs={{0,8},{8,16},{16,24},{24,32},{32,40},{40,48},{48,56},{56,64},{64,7... | collective-permute-start | bytes 393224 | tf_op jit(solution)/shard_map/while/body/eval_jaxpr/ppermute | solution.py:17
  565.9 13.2 %collective-permute-start = (bf16[2,256,128]{2,1,0:T(8,128)(2,1)S(1)}, bf16[2,256,128]{2,1,0:T(8,128)(2,1)S(1)}, u32[]{:S(2)}, u32[]{:S(2)}) collective-permute-start(bf16[2,256,128]{2,1,0:T(8,128)(2,1)S(1)} %get-tuple-element.371), channel_id=1, source_target_pairs={{0,8},{8,16},{16,24},{24,32},{32,40},{40,48},{48,56},{56,64},{64,7... | collective-permute-start | bytes 393224 | tf_op jit(solution)/shard_map/while/body/eval_jaxpr/ppermute | solution.py:17
  583.1 13.2 %collective-permute-start = (bf16[2,256,128]{2,1,0:T(8,128)(2,1)S(1)}, bf16[2,256,128]{2,1,0:T(8,128)(2,1)S(1)}, u32[]{:S(2)}, u32[]{:S(2)}) collective-permute-start(bf16[2,256,128]{2,1,0:T(8,128)(2,1)S(1)} %get-tuple-element.371), channel_id=1, source_target_pairs={{0,8},{8,16},{16,24},{24,32},{32,40},{40,48},{48,56},{56,64},{64,7... | collective-permute-start | bytes 393224 | tf_op jit(solution)/shard_map/while/body/eval_jaxpr/ppermute | solution.py:17
  600.4 13.2 %collective-permute-start = (bf16[2,256,128]{2,1,0:T(8,128)(2,1)S(1)}, bf16[2,256,128]{2,1,0:T(8,128)(2,1)S(1)}, u32[]{:S(2)}, u32[]{:S(2)}) collective-permute-start(bf16[2,256,128]{2,1,0:T(8,128)(2,1)S(1)} %get-tuple-element.371), channel_id=1, source_target_pairs={{0,8},{8,16},{16,24},{24,32},{32,40},{40,48},{48,56},{56,64},{64,7... | collective-permute-start | bytes 393224 | tf_op jit(solution)/shard_map/while/body/eval_jaxpr/ppermute | solution.py:17
  617.7 13.2 %collective-permute-start = (bf16[2,256,128]{2,1,0:T(8,128)(2,1)S(1)}, bf16[2,256,128]{2,1,0:T(8,128)(2,1)S(1)}, u32[]{:S(2)}, u32[]{:S(2)}) collective-permute-start(bf16[2,256,128]{2,1,0:T(8,128)(2,1)S(1)} %get-tuple-element.371), channel_id=1, source_target_pairs={{0,8},{8,16},{16,24},{24,32},{32,40},{40,48},{48,56},{56,64},{64,7... | collective-permute-start | bytes 393224 | tf_op jit(solution)/shard_map/while/body/eval_jaxpr/ppermute | solution.py:17
  635.3 5.1 convolution_convert_fusion
  640.4 2.6 copy.49
  643.0 99.4 %reduce-scatter.4.cloned.1.call-done = bf16[640,256]{1,0:T(8,128)(2,1)} async-done(((bf16[5120,256]{1,0:T(8,128)(2,1)}), bf16[640,256]{1,0:T(8,128)(2,1)}) %reduce-scatter.4.cloned.1.call-update) | async-done | bytes 327696
  (222 shorter events, 66.4 us)
Async XLA Ops:
  6.5 200.8 %copy-start.2 = (bf16[32,128]{1,0:T(8,128)(2,1)S(1)}, bf16[32,128]{1,0:T(8,128)(2,1)}, u32[]{:S(2)}) copy-start(bf16[32,128]{1,0:T(8,128)(2,1)} %param.13) | copy-start | bytes 24580
  6.5 628.8 %all-gather.2.cloned.1.call-start = ((), (), s32[]{:S(2)}) async-start(), calls=%async_computation.1 | async-start | bytes 6656000 | tf_op jit(solution)/shard_map/all_gather | solution.py:116
  7.3 735.2 %reduce-scatter.4.cloned.1.call-start = ((), (), s32[]{:S(2)}) async-start(), calls=%async_computation.2 | async-start | bytes 2949120
  356.1 1.5 copy-start
  360.0 2.4 copy-start.1
  362.9 13.9 %collective-permute-start = (bf16[2,256,128]{2,1,0:T(8,128)(2,1)S(1)}, bf16[2,256,128]{2,1,0:T(8,128)(2,1)S(1)}, u32[]{:S(2)}, u32[]{:S(2)}) collective-permute-start(bf16[2,256,128]{2,1,0:T(8,128)(2,1)S(1)} %get-tuple-element.371), channel_id=1, source_target_pairs={{0,8},{8,16},{16,24},{24,32},{32,40},{40,48},{48,56},{56,64},{64,7... | collective-permute-start | bytes 393224 | tf_op jit(solution)/shard_map/while/body/eval_jaxpr/ppermute | solution.py:17
  378.1 17.8 %collective-permute-start = (bf16[2,256,128]{2,1,0:T(8,128)(2,1)S(1)}, bf16[2,256,128]{2,1,0:T(8,128)(2,1)S(1)}, u32[]{:S(2)}, u32[]{:S(2)}) collective-permute-start(bf16[2,256,128]{2,1,0:T(8,128)(2,1)S(1)} %get-tuple-element.371), channel_id=1, source_target_pairs={{0,8},{8,16},{16,24},{24,32},{32,40},{40,48},{48,56},{56,64},{64,7... | collective-permute-start | bytes 393224 | tf_op jit(solution)/shard_map/while/body/eval_jaxpr/ppermute | solution.py:17
  397.1 15.2 %collective-permute-start = (bf16[2,256,128]{2,1,0:T(8,128)(2,1)S(1)}, bf16[2,256,128]{2,1,0:T(8,128)(2,1)S(1)}, u32[]{:S(2)}, u32[]{:S(2)}) collective-permute-start(bf16[2,256,128]{2,1,0:T(8,128)(2,1)S(1)} %get-tuple-element.371), channel_id=1, source_target_pairs={{0,8},{8,16},{16,24},{24,32},{32,40},{40,48},{48,56},{56,64},{64,7... | collective-permute-start | bytes 393224 | tf_op jit(solution)/shard_map/while/body/eval_jaxpr/ppermute | solution.py:17
  413.7 15.1 %collective-permute-start = (bf16[2,256,128]{2,1,0:T(8,128)(2,1)S(1)}, bf16[2,256,128]{2,1,0:T(8,128)(2,1)S(1)}, u32[]{:S(2)}, u32[]{:S(2)}) collective-permute-start(bf16[2,256,128]{2,1,0:T(8,128)(2,1)S(1)} %get-tuple-element.371), channel_id=1, source_target_pairs={{0,8},{8,16},{16,24},{24,32},{32,40},{40,48},{48,56},{56,64},{64,7... | collective-permute-start | bytes 393224 | tf_op jit(solution)/shard_map/while/body/eval_jaxpr/ppermute | solution.py:17
  430.0 15.1 %collective-permute-start = (bf16[2,256,128]{2,1,0:T(8,128)(2,1)S(1)}, bf16[2,256,128]{2,1,0:T(8,128)(2,1)S(1)}, u32[]{:S(2)}, u32[]{:S(2)}) collective-permute-start(bf16[2,256,128]{2,1,0:T(8,128)(2,1)S(1)} %get-tuple-element.371), channel_id=1, source_target_pairs={{0,8},{8,16},{16,24},{24,32},{32,40},{40,48},{48,56},{56,64},{64,7... | collective-permute-start | bytes 393224 | tf_op jit(solution)/shard_map/while/body/eval_jaxpr/ppermute | solution.py:17
  446.4 15.0 %collective-permute-start = (bf16[2,256,128]{2,1,0:T(8,128)(2,1)S(1)}, bf16[2,256,128]{2,1,0:T(8,128)(2,1)S(1)}, u32[]{:S(2)}, u32[]{:S(2)}) collective-permute-start(bf16[2,256,128]{2,1,0:T(8,128)(2,1)S(1)} %get-tuple-element.371), channel_id=1, source_target_pairs={{0,8},{8,16},{16,24},{24,32},{32,40},{40,48},{48,56},{56,64},{64,7... | collective-permute-start | bytes 393224 | tf_op jit(solution)/shard_map/while/body/eval_jaxpr/ppermute | solution.py:17
  462.7 15.5 %collective-permute-start = (bf16[2,256,128]{2,1,0:T(8,128)(2,1)S(1)}, bf16[2,256,128]{2,1,0:T(8,128)(2,1)S(1)}, u32[]{:S(2)}, u32[]{:S(2)}) collective-permute-start(bf16[2,256,128]{2,1,0:T(8,128)(2,1)S(1)} %get-tuple-element.371), channel_id=1, source_target_pairs={{0,8},{8,16},{16,24},{24,32},{32,40},{40,48},{48,56},{56,64},{64,7... | collective-permute-start | bytes 393224 | tf_op jit(solution)/shard_map/while/body/eval_jaxpr/ppermute | solution.py:17
  479.5 16.0 %collective-permute-start = (bf16[2,256,128]{2,1,0:T(8,128)(2,1)S(1)}, bf16[2,256,128]{2,1,0:T(8,128)(2,1)S(1)}, u32[]{:S(2)}, u32[]{:S(2)}) collective-permute-start(bf16[2,256,128]{2,1,0:T(8,128)(2,1)S(1)} %get-tuple-element.371), channel_id=1, source_target_pairs={{0,8},{8,16},{16,24},{24,32},{32,40},{40,48},{48,56},{56,64},{64,7... | collective-permute-start | bytes 393224 | tf_op jit(solution)/shard_map/while/body/eval_jaxpr/ppermute | solution.py:17
  496.7 16.0 %collective-permute-start = (bf16[2,256,128]{2,1,0:T(8,128)(2,1)S(1)}, bf16[2,256,128]{2,1,0:T(8,128)(2,1)S(1)}, u32[]{:S(2)}, u32[]{:S(2)}) collective-permute-start(bf16[2,256,128]{2,1,0:T(8,128)(2,1)S(1)} %get-tuple-element.371), channel_id=1, source_target_pairs={{0,8},{8,16},{16,24},{24,32},{32,40},{40,48},{48,56},{56,64},{64,7... | collective-permute-start | bytes 393224 | tf_op jit(solution)/shard_map/while/body/eval_jaxpr/ppermute | solution.py:17
  514.0 16.0 %collective-permute-start = (bf16[2,256,128]{2,1,0:T(8,128)(2,1)S(1)}, bf16[2,256,128]{2,1,0:T(8,128)(2,1)S(1)}, u32[]{:S(2)}, u32[]{:S(2)}) collective-permute-start(bf16[2,256,128]{2,1,0:T(8,128)(2,1)S(1)} %get-tuple-element.371), channel_id=1, source_target_pairs={{0,8},{8,16},{16,24},{24,32},{32,40},{40,48},{48,56},{56,64},{64,7... | collective-permute-start | bytes 393224 | tf_op jit(solution)/shard_map/while/body/eval_jaxpr/ppermute | solution.py:17
  531.3 16.0 %collective-permute-start = (bf16[2,256,128]{2,1,0:T(8,128)(2,1)S(1)}, bf16[2,256,128]{2,1,0:T(8,128)(2,1)S(1)}, u32[]{:S(2)}, u32[]{:S(2)}) collective-permute-start(bf16[2,256,128]{2,1,0:T(8,128)(2,1)S(1)} %get-tuple-element.371), channel_id=1, source_target_pairs={{0,8},{8,16},{16,24},{24,32},{32,40},{40,48},{48,56},{56,64},{64,7... | collective-permute-start | bytes 393224 | tf_op jit(solution)/shard_map/while/body/eval_jaxpr/ppermute | solution.py:17
  548.6 16.0 %collective-permute-start = (bf16[2,256,128]{2,1,0:T(8,128)(2,1)S(1)}, bf16[2,256,128]{2,1,0:T(8,128)(2,1)S(1)}, u32[]{:S(2)}, u32[]{:S(2)}) collective-permute-start(bf16[2,256,128]{2,1,0:T(8,128)(2,1)S(1)} %get-tuple-element.371), channel_id=1, source_target_pairs={{0,8},{8,16},{16,24},{24,32},{32,40},{40,48},{48,56},{56,64},{64,7... | collective-permute-start | bytes 393224 | tf_op jit(solution)/shard_map/while/body/eval_jaxpr/ppermute | solution.py:17
  565.9 16.0 %collective-permute-start = (bf16[2,256,128]{2,1,0:T(8,128)(2,1)S(1)}, bf16[2,256,128]{2,1,0:T(8,128)(2,1)S(1)}, u32[]{:S(2)}, u32[]{:S(2)}) collective-permute-start(bf16[2,256,128]{2,1,0:T(8,128)(2,1)S(1)} %get-tuple-element.371), channel_id=1, source_target_pairs={{0,8},{8,16},{16,24},{24,32},{32,40},{40,48},{48,56},{56,64},{64,7... | collective-permute-start | bytes 393224 | tf_op jit(solution)/shard_map/while/body/eval_jaxpr/ppermute | solution.py:17
  583.1 16.0 %collective-permute-start = (bf16[2,256,128]{2,1,0:T(8,128)(2,1)S(1)}, bf16[2,256,128]{2,1,0:T(8,128)(2,1)S(1)}, u32[]{:S(2)}, u32[]{:S(2)}) collective-permute-start(bf16[2,256,128]{2,1,0:T(8,128)(2,1)S(1)} %get-tuple-element.371), channel_id=1, source_target_pairs={{0,8},{8,16},{16,24},{24,32},{32,40},{40,48},{48,56},{56,64},{64,7... | collective-permute-start | bytes 393224 | tf_op jit(solution)/shard_map/while/body/eval_jaxpr/ppermute | solution.py:17
  600.4 16.0 %collective-permute-start = (bf16[2,256,128]{2,1,0:T(8,128)(2,1)S(1)}, bf16[2,256,128]{2,1,0:T(8,128)(2,1)S(1)}, u32[]{:S(2)}, u32[]{:S(2)}) collective-permute-start(bf16[2,256,128]{2,1,0:T(8,128)(2,1)S(1)} %get-tuple-element.371), channel_id=1, source_target_pairs={{0,8},{8,16},{16,24},{24,32},{32,40},{40,48},{48,56},{56,64},{64,7... | collective-permute-start | bytes 393224 | tf_op jit(solution)/shard_map/while/body/eval_jaxpr/ppermute | solution.py:17
  617.7 16.0 %collective-permute-start = (bf16[2,256,128]{2,1,0:T(8,128)(2,1)S(1)}, bf16[2,256,128]{2,1,0:T(8,128)(2,1)S(1)}, u32[]{:S(2)}, u32[]{:S(2)}) collective-permute-start(bf16[2,256,128]{2,1,0:T(8,128)(2,1)S(1)} %get-tuple-element.371), channel_id=1, source_target_pairs={{0,8},{8,16},{16,24},{24,32},{32,40},{40,48},{48,56},{56,64},{64,7... | collective-permute-start | bytes 393224 | tf_op jit(solution)/shard_map/while/body/eval_jaxpr/ppermute | solution.py:17
Sparse Core Ops, SparseCore 0:
  11.8 168.4 all-gather.1
  643.2 99.2 reduce-scatter.3
where the time goes:
time: 756 us; the launch traced here: 751 us
  blocking collectives  346 us (46%)
  starting transfers between devices  211 us (28%)
  waiting for transfers between devices  136 us (18%)
  matrix products  24.9 us (3%)
  between operations  13.6 us (2%)
  other arithmetic  11.1 us (1%)
    ppermute x16, starting transfers between devices, passed_along(): return lax.ppermute(block, axis, route)  211 us
    all_gather x1, blocking collectives, per_device(): lax.all_gather(shared_prefix_keys, 'blk', axis=0, tiled=True)  198 us
    all_gather x1, blocking collectives, per_device(): lax.all_gather(shared_prefix_values, 'blk', axis=0, tiled=True)  148 us
    unnamed x3, waiting for transfers between devices  100 us
    ppermute x16, waiting for transfers between devices, passed_along(): return lax.ppermute(block, axis, route)  35.9 us
  transfers between devices with their start and end apart: 18, of which 17 were waited for; matrix products, arithmetic and copies ran while one was open for 4% of the time, Pallas kernels for 0%

commit v1 on v0

v1 whole, which is shorter than its diff:
```python
import math

import jax
import jax.numpy as jnp
from jax import lax
from jax.sharding import PartitionSpec as P

HEAD_SIZE = 128


MASKED_SCORE = -1e30


def shifted(block, axis, distance):
    devices = lax.axis_size(axis)
    route = [((i - distance) % devices, i) for i in range(devices)]
    return lax.ppermute(block, axis, route)


def shifted_pair(first, second, axis, distance):
    rows = first.shape[0] * first.shape[1]
    packed = jnp.concatenate(
        (first.reshape(rows, first.shape[2]), second.reshape(-1, second.shape[2])), axis=0
    )
    packed = shifted(packed, axis, distance)
    return (
        packed[:rows].reshape(first.shape),
        packed[rows:].reshape(second.shape),
    )


def per_device(
    queries,
    suffix_key_rows,
    suffix_value_rows,
    shared_prefix_keys,
    shared_prefix_values,
    out_weight,
    lengths,
):
    tok_rows = queries.shape[0]
    kv_heads = suffix_key_rows.shape[1] // HEAD_SIZE
    q_heads = queries.shape[1] // HEAD_SIZE
    heads_per_group = q_heads // kv_heads
    blocks = lax.axis_size("blk")
    my_block = lax.axis_index("blk")
    score_scale = 1.0 / math.sqrt(HEAD_SIZE)
    width = kv_heads * HEAD_SIZE

    own_kv = jnp.concatenate((suffix_key_rows, suffix_value_rows), axis=1)[None]
    prefix = jnp.concatenate((shared_prefix_keys, shared_prefix_values), axis=1)[None]
    suffix = own_kv
    distance = 1
    while 2 * distance <= blocks // 4:
        got_suffix, got_prefix = shifted_pair(suffix, prefix, "blk", distance)
        suffix = jnp.concatenate((got_suffix, suffix), axis=0)
        prefix = jnp.concatenate((got_prefix, prefix), axis=0)
        distance *= 2
    got_suffix, got_prefix = shifted_pair(own_kv, prefix, "blk", distance)
    suffix = jnp.concatenate((got_suffix, suffix), axis=0)
    prefix = jnp.concatenate((got_prefix, prefix), axis=0)
    distance *= 2
    while distance < blocks:
        prefix = jnp.concatenate((shifted(prefix, "blk", distance), prefix), axis=0)
        distance *= 2

    reach = suffix.shape[0]
    suffix = suffix.reshape(reach * tok_rows, 2 * width)
    prefix = prefix.reshape(-1, 2 * width)

    req_ends = jnp.cumsum(lengths)
    local_rows = jnp.arange(tok_rows, dtype=jnp.int32)
    query_pos = my_block * tok_rows + local_rows

    def owner_of(position):
        return jnp.sum((position[:, None] >= req_ends[None, :]).astype(jnp.int32), axis=1)

    query_owner = owner_of(query_pos)
    key_pos = (my_block - (reach - 1)) * tok_rows + jnp.arange(reach * tok_rows, dtype=jnp.int32)
    key_owner = owner_of(key_pos)
    visible = (
        (key_owner[None, :] == query_owner[:, None])
        & (key_pos[None, :] <= query_pos[:, None])
        & (key_pos[None, :] >= 0)
    )

    heads_of_query = queries.reshape(tok_rows, kv_heads, heads_per_group, HEAD_SIZE)

    def one_head(kv_head):
        cols = slice(kv_head * HEAD_SIZE, (kv_head + 1) * HEAD_SIZE)
        vcols = slice(width + kv_head * HEAD_SIZE, width + (kv_head + 1) * HEAD_SIZE)
        q = heads_of_query[:, kv_head]
        pre_scores = (
            jnp.einsum("qgd,kd->gqk", q, prefix[:, cols], preferred_element_type=jnp.float32)
            * score_scale
        )
        suf_scores = (
            jnp.einsum("qgd,kd->gqk", q, suffix[:, cols], preferred_element_type=jnp.float32)
            * score_scale
        )
        suf_scores = jnp.where(visible[None], suf_scores, MASKED_SCORE)
        peak = jnp.maximum(jnp.max(pre_scores, axis=-1), jnp.max(suf_scores, axis=-1))
        pre_weights = jnp.exp(pre_scores - peak[..., None])
        suf_weights = jnp.where(visible[None], jnp.exp(suf_scores - peak[..., None]), 0.0)
        total = jnp.sum(pre_weights, axis=-1) + jnp.sum(suf_weights, axis=-1)
        summed = jnp.einsum(
            "gqk,kd->gqd",
            pre_weights.astype(jnp.bfloat16),
            prefix[:, vcols],
            preferred_element_type=jnp.float32,
        ) + jnp.einsum(
            "gqk,kd->gqd",
            suf_weights.astype(jnp.bfloat16),
            suffix[:, vcols],
            preferred_element_type=jnp.float32,
        )
        return summed / total[..., None]

    attended = jnp.stack([one_head(h) for h in range(kv_heads)])
    attn = (
        jnp.transpose(attended, (2, 0, 1, 3))
        .reshape(tok_rows, q_heads * HEAD_SIZE)
        .astype(jnp.bfloat16)
    )
    product = jnp.dot(
        attn,
        lax.all_gather(out_weight, "blk", axis=1, tiled=True),
        preferred_element_type=jnp.float32,
    )
    return lax.psum_scatter(product.astype(jnp.bfloat16), "mp", scatter_dimension=1, tiled=True)


def solution(mesh):
    placed = (
        P("blk", "mp"),
        P("blk", "mp"),
        P("blk", "mp"),
        P("blk", "mp"),
        P("blk", "mp"),
        P("mp", "blk"),
        P(),
    )
    return jax.shard_map(
        per_device, mesh=mesh, in_specs=placed, out_specs=P("blk", "mp"), check_vma=False
    )
```

time: 756 us -> 323 us (0.43)
  blocking collectives: 346 us -> 0 us
  starting transfers between devices: 211 us -> 26.6 us
  waiting for transfers between devices: 136 us -> 216 us
  local copies, waits for them, and re-layouts: 7.01 us -> 16.1 us
    all_gather x2 -> x0, blocking collectives: 346 us -> none  [the longest x1 198 us: per_device(): lax.all_gather(shared_prefix_keys, 'blk', axis=0, tiled=True)]
    ppermute x16 -> x6, starting transfers between devices: 211 us -> 26.6 us  [shifted(): return lax.ppermute(block, axis, route)]
    all_gather x1, waiting for transfers between devices: 0.02 us -> 65.7 us  [per_device(): lax.all_gather(out_weight, 'blk', axis=1, tiled=True)]
    ppermute x16 -> x6, waiting for transfers between devices: 35.9 us -> 88.6 us  [shifted(): return lax.ppermute(block, axis, route)]
    unnamed x3, waiting for transfers between devices: 100 us -> 61.7 us
    dot_general x36 -> x4, matrix products: 19.8 us -> 24.5 us  [the longest x1 11.5 us: one_head(): jnp.einsum('gqk,kd->gqd', suf_weights.astype(jnp.bfloat16), suffix[:, vco...]
  transfers between devices with their start and end apart: 18 -> 8, of which waited for: 17 -> 7; matrix products, arithmetic and copies ran while one was open for 4% -> 16% of each run, Pallas kernels for 0% -> 0%
where the time goes in v1:
time: 323 us; the launch traced here: 319 us
  waiting for transfers between devices  216 us (67%)
  matrix products  29.6 us (9%)
  starting transfers between devices  26.6 us (8%)
  other arithmetic  17.4 us (5%)
  local copies, waits for them, and re-layouts  16.1 us (5%)
  between operations  13.8 us (4%)
    ppermute x6, waiting for transfers between devices, shifted(): return lax.ppermute(block, axis, route)  88.6 us
    all_gather x1, waiting for transfers between devices, per_device(): lax.all_gather(out_weight, 'blk', axis=1, tiled=True)  65.7 us
    unnamed x3, waiting for transfers between devices  61.7 us
    ppermute x6, starting transfers between devices, shifted(): return lax.ppermute(block, axis, route)  26.6 us
    unnamed x31, local copies, waits for them, and re-layouts  12.1 us
    reduce_sum x2, other arithmetic, one_head(): total = jnp.sum(pre_weights, axis=-1) + jnp.sum(suf_weights, axis=-1)  12 us
    dot_general x1, matrix products, one_head(): jnp.einsum('gqk,kd->gqd', suf_weights.astype(jnp.bfloat16), suffix[:, vco...  11.5 us
    dot_general x1, matrix products, one_head(): jnp.einsum('qgd,kd->gqk', q, suffix[:, cols], preferred_element_type=jnp....  9.39 us
  transfers between devices with their start and end apart: 8, of which 7 were waited for; matrix products, arithmetic and copies ran while one was open for 16% of the time, Pallas kernels for 0%

profile of v1, /device:TPU:1, one launch (start us, length us, event | category | flops | bytes accessed | tf_op | source)
XLA Modules:
  0.0 319.5 jit_solution(10166735036793005471)
XLA Ops:
  9.7 16.8 %collective-permute-start = (bf16[288,256]{1,0:T(8,128)(2,1)S(1)}, bf16[288,256]{1,0:T(8,128)(2,1)S(1)}, u32[]{:S(2)}, u32[]{:S(2)}) collective-permute-start(bf16[288,256]{1,0:T(8,128)(2,1)S(1)} %pad_maximum_fusion.7), channel_id=1, source_target_pairs={{504,0},{0,8},{8,16},{16,24},{24,32},{32,40},{40,48},{48,56},{56,6... | collective-permute-start | bytes 442376 | tf_op jit(solution)/shard_map/ppermute | solution.py:17
  26.5 5.8 %collective-permute-done = bf16[288,256]{1,0:T(8,128)(2,1)S(1)} collective-permute-done((bf16[288,256]{1,0:T(8,128)(2,1)S(1)}, bf16[288,256]{1,0:T(8,128)(2,1)S(1)}, u32[]{:S(2)}, u32[]{:S(2)}) %collective-permute-start) | collective-permute-done | bytes 147488 | tf_op jit(solution)/shard_map/ppermute | solution.py:17
  33.0 1.9 collective-permute-start.1
  34.9 37.3 %collective-permute-done.1 = bf16[576,256]{1,0:T(8,128)(2,1)S(1)} collective-permute-done((bf16[576,256]{1,0:T(8,128)(2,1)S(1)}, bf16[576,256]{1,0:T(8,128)(2,1)S(1)}, u32[]{:S(2)}, u32[]{:S(2)}) %collective-permute-start.1) | collective-permute-done | bytes 294944 | tf_op jit(solution)/shard_map/ppermute | solution.py:17
  72.4 1.9 collective-permute-start.2
  74.4 15.7 %collective-permute-done.2 = bf16[1152,256]{1,0:T(8,128)(2,1)S(1)} collective-permute-done((bf16[1152,256]{1,0:T(8,128)(2,1)S(1)}, bf16[1152,256]{1,0:T(8,128)(2,1)S(1)}, u32[]{:S(2)}, u32[]{:S(2)}) %collective-permute-start.2) | collective-permute-done | bytes 589856 | tf_op jit(solution)/shard_map/ppermute | solution.py:17
  90.5 1.9 collective-permute-start.3
  92.9 27.8 %collective-permute-done.3 = bf16[2304,256]{1,0:T(8,128)(2,1)S(1)} collective-permute-done((bf16[2304,256]{1,0:T(8,128)(2,1)S(1)}, bf16[2304,256]{1,0:T(8,128)(2,1)S(1)}, u32[]{:S(2)}, u32[]{:S(2)}) %collective-permute-start.3) | collective-permute-done | bytes 1179680 | tf_op jit(solution)/shard_map/ppermute | solution.py:17
  122.4 1.9 collective-permute-start.4
  124.3 3.7 %and_and_fusion = pred[256,4352]{0,1:T(8,128)(4,1)S(1)} fusion(s32[256]{0:T(256)S(1)} %iota_add_fusion.1, s32[256]{0:T(256)S(1)} %convert_reduce_fusion.1, s32[4352]{0:T(1024)S(1)} %iota_add_fusion, s32[4352]{0:T(1024)S(1)} %convert_reduce_fusion, pred[4352]{0:T(1024)(128)(4,1)S(1)} %broadcast_compare_fusion), kind=kLoop, calls=%fused_computation.14 | loop fusion | flops 4456448 | bytes 1155328 | tf_op jit(solution)/shard_map/and | solution.py:82
  129.2 1.3 slice.66
  130.5 2.0 collective-permute-done.4
  134.2 2.1 collective-permute-start.5
  138.3 9.4 %fusion = (f32[5,256]{1,0:T(8,128)S(1)}, f32[4352,256,5]{1,0,2:T(8,128)}) fusion(pred[256,4352]{0,1:T(8,128)(4,1)S(1)} %and_and_fusion, bf16[256,5,128]{0,2,1:T(8,128)(2,1)S(1)} %bitcast.121, bf16[4352,256]{1,0:T(8,128)(2,1)S(1)} %bitcast.137), kind=kOutput, calls=%fused_computation.2 | convolution fusion | flops 1442773760 | bytes 24843264 | tf_op jit(solution)/shard_map/qgd,kd->gqk/dot_general | solution.py:98
  148.6 1.5 bitcast_reduce_fusion
  150.1 1.7 fusion.7
  151.8 10.3 %fusion.1 = f32[5,256]{1,0:T(8,128)S(1)} fusion(f32[4352,256,5]{1,0,2:T(8,128)} %get-tuple-element.8, f32[5,256]{1,0:T(8,128)S(1)} %max.7, pred[256,4352]{0,1:T(8,128)(4,1)S(1)} %and_and_fusion), kind=kLoop, calls=%fused_computation.3 | loop fusion | flops 27851520 | bytes 23406592 | tf_op jit(solution)/shard_map/reduce_sum | solution.py:105
  162.1 2.0 fusion.9
  164.2 11.5 %fusion.18 = bf16[5,256,128]{1,2,0:T(8,128)(2,1)S(1)} fusion(f32[5,256,128]{1,2,0:T(8,128)S(1)} %fusion.9, bf16[4352,256]{1,0:T(8,128)(2,1)S(1)} %bitcast.138, f32[4352,256,5]{1,0,2:T(8,128)} %get-tuple-element.8, f32[5,256]{1,0:T(8,128)S(1)} %max.7, pred[256,4352]{0,1:T(8,128)(4,1)S(1)} %and_and_fusion, f32[5,256]{1,0:T(8,128)S(1)} %add.45), kind=kOutput, calls=%fused_computation.22 | convolution fusion | flops 1454407680 | bytes 25509888 | tf_op jit(solution)/shard_map/gqk,kd->gqd/dot_general | solution.py:111
  175.7 65.7 %all-gather.2.cloned.1.call-done = bf16[640,5120]{0,1:T(8,128)(2,1)} async-done(((bf16[640,80]{0,1:T(8,128)(2,1)}), bf16[640,5120]{0,1:T(8,128)(2,1)}) %all-gather.2.cloned.1.call-update) | async-done | bytes 6553616 | tf_op jit(solution)/shard_map/all_gather | solution.py:127
  241.4 5.1 %convolution_convert_fusion = bf16[256,5120]{1,0:T(8,128)(2,1)S(1)} fusion(bf16[256,640]{0,1:T(8,128)(2,1)S(1)} %bitcast.140, bf16[640,5120]{0,1:T(8,128)(2,1)} %all-gather.2.cloned.1.call-done), kind=kOutput, calls=%fused_computation.12 | convolution fusion | flops 1679032320 | bytes 9502720 | tf_op jit(solution)/shard_map/dot_general | solution.py:125
  246.5 2.6 copy.47
  249.1 61.7 %reduce-scatter.4.cloned.1.call-done = bf16[640,256]{1,0:T(8,128)(2,1)} async-done(((bf16[5120,256]{1,0:T(8,128)(2,1)}), bf16[640,256]{1,0:T(8,128)(2,1)}) %reduce-scatter.4.cloned.1.call-update) | async-done | bytes 327696
  310.8 1.9 copy.48
  (69 shorter events, 12.1 us)
Async XLA Ops:
  6.5 234.9 %all-gather.2.cloned.1.call-start = ((), (), s32[]{:S(2)}) async-start(), calls=%async_computation.1 | async-start | bytes 6656000 | tf_op jit(solution)/shard_map/all_gather | solution.py:127
  9.7 82.8 %copy-start.2 = (s32[16]{0:T(128)S(1)}, s32[16]{0:T(128)}, u32[]{:S(2)}) copy-start(s32[16]{0:T(128)} %param.13) | copy-start | bytes 196
  9.7 22.6 %collective-permute-start = (bf16[288,256]{1,0:T(8,128)(2,1)S(1)}, bf16[288,256]{1,0:T(8,128)(2,1)S(1)}, u32[]{:S(2)}, u32[]{:S(2)}) collective-permute-start(bf16[288,256]{1,0:T(8,128)(2,1)S(1)} %pad_maximum_fusion.7), channel_id=1, source_target_pairs={{504,0},{0,8},{8,16},{16,24},{24,32},{32,40},{40,48},{48,56},{56,6... | collective-permute-start | bytes 442376 | tf_op jit(solution)/shard_map/ppermute | solution.py:17
  32.3 0.7 copy-start.1
  33.0 39.3 %collective-permute-start.1 = (bf16[576,256]{1,0:T(8,128)(2,1)S(1)}, bf16[576,256]{1,0:T(8,128)(2,1)S(1)}, u32[]{:S(2)}, u32[]{:S(2)}) collective-permute-start(bf16[576,256]{1,0:T(8,128)(2,1)S(1)} %pad_maximum_fusion.5), channel_id=1, source_target_pairs={{496,0},{504,8},{0,16},{8,24},{16,32},{24,40},{32,48},{40,56},{48,... | collective-permute-start | bytes 884744 | tf_op jit(solution)/shard_map/ppermute | solution.py:17
  72.4 17.7 %collective-permute-start.2 = (bf16[1152,256]{1,0:T(8,128)(2,1)S(1)}, bf16[1152,256]{1,0:T(8,128)(2,1)S(1)}, u32[]{:S(2)}, u32[]{:S(2)}) collective-permute-start(bf16[1152,256]{1,0:T(8,128)(2,1)S(1)} %pad_maximum_fusion.2), channel_id=1, source_target_pairs={{480,0},{488,8},{496,16},{504,24},{0,32},{8,40},{16,48},{24,56},{3... | collective-permute-start | bytes 1769480 | tf_op jit(solution)/shard_map/ppermute | solution.py:17
  74.4 236.4 %reduce-scatter.4.cloned.1.call-start = ((), (), s32[]{:S(2)}) async-start(), calls=%async_computation.2 | async-start | bytes 2949120
  90.5 30.3 %collective-permute-start.3 = (bf16[2304,256]{1,0:T(8,128)(2,1)S(1)}, bf16[2304,256]{1,0:T(8,128)(2,1)S(1)}, u32[]{:S(2)}, u32[]{:S(2)}) collective-permute-start(bf16[2304,256]{1,0:T(8,128)(2,1)S(1)} %pad_maximum_fusion), channel_id=1, source_target_pairs={{448,0},{456,8},{464,16},{472,24},{480,32},{488,40},{496,48},{504,... | collective-permute-start | bytes 3538952 | tf_op jit(solution)/shard_map/ppermute | solution.py:17
  120.8 3.5 %copy-start = (bf16[2304,256]{1,0:T(8,128)(2,1)}, bf16[2304,256]{1,0:T(8,128)(2,1)S(1)}, u32[]{:S(2)}) copy-start(bf16[2304,256]{1,0:T(8,128)(2,1)S(1)} %collective-permute-done.3) | copy-start | bytes 3538948
  122.4 10.0 %collective-permute-start.4 = (bf16[768,256]{1,0:T(8,128)(2,1)}, bf16[768,256]{1,0:T(8,128)(2,1)}, u32[]{:S(2)}, u32[]{:S(2)}) collective-permute-start(bf16[768,256]{1,0:T(8,128)(2,1)} %pad_maximum_fusion.4), channel_id=1, source_target_pairs={{384,0},{392,8},{400,16},{408,24},{416,32},{424,40},{432,48},{440,... | collective-permute-start | bytes 1179656 | tf_op jit(solution)/shard_map/ppermute | solution.py:17
  134.2 13.5 %collective-permute-start.5 = (bf16[32,32,256]{2,1,0:T(8,128)(2,1)S(1)}, bf16[32,32,256]{2,1,0:T(8,128)(2,1)S(1)}, u32[]{:S(2)}, u32[]{:S(2)}) collective-permute-start(bf16[32,32,256]{2,1,0:T(8,128)(2,1)S(1)} %constant_dynamic-update-slice_fusion.9), channel_id=1, source_target_pairs={{256,0},{264,8},{272,16},{280,24},{288,32},{296,40},{304,48},{312,... | collective-permute-start | bytes 1572872 | tf_op jit(solution)/shard_map/ppermute | solution.py:17
Sparse Core Ops, SparseCore 0:
  74.5 166.8 all-gather.1
  249.2 61.4 reduce-scatter.3

commit v2 on v1

--- a/solution.py
+++ b/solution.py
@@ -11,8 +11,13 @@
 MASKED_SCORE = -1e30
 
 
+BLK_PARTS = (("y", 4), ("x", 4), ("zh", 2), ("core", 2))
+BLK = tuple(name for name, _ in BLK_PARTS)
+BLOCKS = math.prod(size for _, size in BLK_PARTS)
+
+
 def shifted(block, axis, distance):
-    devices = lax.axis_size(axis)
+    devices = BLOCKS
     route = [((i - distance) % devices, i) for i in range(devices)]
     return lax.ppermute(block, axis, route)
 
@@ -42,30 +47,34 @@
     kv_heads = suffix_key_rows.shape[1] // HEAD_SIZE
     q_heads = queries.shape[1] // HEAD_SIZE
     heads_per_group = q_heads // kv_heads
-    blocks = lax.axis_size("blk")
-    my_block = lax.axis_index("blk")
+    blocks = BLOCKS
+    my_block = lax.axis_index(BLK)
     score_scale = 1.0 / math.sqrt(HEAD_SIZE)
     width = kv_heads * HEAD_SIZE
 
     own_kv = jnp.concatenate((suffix_key_rows, suffix_value_rows), axis=1)[None]
     prefix = jnp.concatenate((shared_prefix_keys, shared_prefix_values), axis=1)[None]
     suffix = own_kv
-    distance = 1
-    while 2 * distance <= blocks // 4:
-        got_suffix, got_prefix = shifted_pair(suffix, prefix, "blk", distance)
+    reach = blocks // 4
+    shifts = [1 << k for k in range(reach.bit_length() - 1)]
+    shifts = shifts[1:2] + shifts[:1] + shifts[2:][::-1]
+    distances = [0]
+    for distance in shifts:
+        got_suffix, got_prefix = shifted_pair(suffix, prefix, BLK, distance)
         suffix = jnp.concatenate((got_suffix, suffix), axis=0)
         prefix = jnp.concatenate((got_prefix, prefix), axis=0)
-        distance *= 2
-    got_suffix, got_prefix = shifted_pair(own_kv, prefix, "blk", distance)
+        distances = [d + distance for d in distances] + distances
+    got_suffix, got_prefix = shifted_pair(own_kv, prefix, BLK, reach)
     suffix = jnp.concatenate((got_suffix, suffix), axis=0)
     prefix = jnp.concatenate((got_prefix, prefix), axis=0)
-    distance *= 2
+    distances = [reach] + distances
+    distance = 2 * reach
     while distance < blocks:
-        prefix = jnp.concatenate((shifted(prefix, "blk", distance), prefix), axis=0)
+        prefix = jnp.concatenate((shifted(prefix, BLK, distance), prefix), axis=0)
         distance *= 2
 
-    reach = suffix.shape[0]
-    suffix = suffix.reshape(reach * tok_rows, 2 * width)
+    count = suffix.shape[0]
+    suffix = suffix.reshape(count * tok_rows, 2 * width)
     prefix = prefix.reshape(-1, 2 * width)
 
     req_ends = jnp.cumsum(lengths)
@@ -76,7 +85,8 @@
         return jnp.sum((position[:, None] >= req_ends[None, :]).astype(jnp.int32), axis=1)
 
     query_owner = owner_of(query_pos)
-    key_pos = (my_block - (reach - 1)) * tok_rows + jnp.arange(reach * tok_rows, dtype=jnp.int32)
+    block_of_key = my_block - jnp.repeat(jnp.array(distances, jnp.int32), tok_rows)
+    key_pos = block_of_key * tok_rows + jnp.tile(local_rows, count)
     key_owner = owner_of(key_pos)
     visible = (
         (key_owner[None, :] == query_owner[:, None])
@@ -122,24 +132,36 @@
         .reshape(tok_rows, q_heads * HEAD_SIZE)
         .astype(jnp.bfloat16)
     )
-    product = jnp.dot(
-        attn,
-        lax.all_gather(out_weight, "blk", axis=1, tiled=True),
-        preferred_element_type=jnp.float32,
-    )
-    return lax.psum_scatter(product.astype(jnp.bfloat16), "mp", scatter_dimension=1, tiled=True)
+    swap = [(0, 1), (1, 0)]
+    core = lax.axis_index("core")
+    both = jnp.concatenate((attn, lax.ppermute(attn, "core", swap)), axis=0)
+    weight = lax.all_gather(out_weight, BLK[:-1], axis=1, tiled=True)
+    product = jnp.dot(both, weight, preferred_element_type=jnp.float32)
+    reduced = lax.psum_scatter(product.astype(jnp.bfloat16), "mp", scatter_dimension=1, tiled=True)
+    other = lax.ppermute(reduced[tok_rows:], "core", swap)
+    mine = reduced[:tok_rows]
+    per_block = out_weight.shape[1]
+    mine = mine.reshape(tok_rows, -1, per_block)
+    other = other.reshape(tok_rows, -1, per_block)
+    even = jnp.where(core == 0, mine, other)
+    odd = jnp.where(core == 0, other, mine)
+    return jnp.stack((even, odd), axis=2).reshape(tok_rows, -1)
 
 
 def solution(mesh):
+    sizes = tuple(size for _, size in BLK_PARTS)
+    split = jax.sharding.Mesh(
+        mesh.devices.reshape(sizes + (mesh.shape["mp"],)), BLK + ("mp",)
+    )
     placed = (
-        P("blk", "mp"),
-        P("blk", "mp"),
-        P("blk", "mp"),
-        P("blk", "mp"),
-        P("blk", "mp"),
-        P("mp", "blk"),
+        P(BLK, "mp"),
+        P(BLK, "mp"),
+        P(BLK, "mp"),
+        P(BLK, "mp"),
+        P(BLK, "mp"),
+        P("mp", BLK),
         P(),
     )
     return jax.shard_map(
-        per_device, mesh=mesh, in_specs=placed, out_specs=P("blk", "mp"), check_vma=False
+        per_device, mesh=split, in_specs=placed, out_specs=P(BLK, "mp"), check_vma=False
     )

time: 323 us -> 332 us (1.028)
  starting transfers between devices: 26.6 us -> 59.2 us
  waiting for transfers between devices: 216 us -> 197 us
    reduce_scatter x0 -> x1, waiting for transfers between devices: none -> 63.8 us  [per_device(): lax.psum_scatter(product.astype(jnp.bfloat16), 'mp', scatter_dimension=1,...]
    unnamed x3 -> x2, waiting for transfers between devices: 61.7 us -> 0.03 us
    ppermute x6, waiting for transfers between devices: 88.6 us -> 47.7 us  [shifted(): return lax.ppermute(block, axis, route)]
    ppermute x0 -> x2, starting transfers between devices: none -> 19 us  [the longest x1 12.5 us: per_device(): both = jnp.concatenate((attn, lax.ppermute(attn, 'core', swap)), axis=0)]
    all_gather x1, waiting for transfers between devices: 65.7 us -> 83.1 us  [per_device(): weight = lax.all_gather(out_weight, BLK[:-1], axis=1, tiled=True)]
    ppermute x6, starting transfers between devices: 26.6 us -> 40.1 us  [shifted(): return lax.ppermute(block, axis, route)]
    unnamed x31, local copies, waits for them, and re-layouts: 12.1 us -> 7.63 us
  transfers between devices with their start and end apart: 8 -> 10, of which waited for: 7 -> 10; matrix products, arithmetic and copies ran while one was open for 16% -> 15% of each run, Pallas kernels for 0% -> 0%
where the time goes in v2:
time: 332 us; the launch traced here: 331 us
  waiting for transfers between devices  197 us (59%)
  starting transfers between devices  59.2 us (18%)
  matrix products  29.2 us (9%)
  other arithmetic  18.4 us (6%)
  between operations  13.9 us (4%)
  local copies, waits for them, and re-layouts  13.5 us (4%)
    all_gather x1, waiting for transfers between devices, per_device(): weight = lax.all_gather(out_weight, BLK[:-1], axis=1, tiled=True)  83.1 us
    reduce_scatter x1, waiting for transfers between devices, per_device(): lax.psum_scatter(product.astype(jnp.bfloat16), 'mp', scatter_dimension=1,...  63.8 us
    ppermute x6, waiting for transfers between devices, shifted(): return lax.ppermute(block, axis, route)  47.7 us
    ppermute x6, starting transfers between devices, shifted(): return lax.ppermute(block, axis, route)  40.1 us
    ppermute x1, starting transfers between devices, per_device(): both = jnp.concatenate((attn, lax.ppermute(attn, 'core', swap)), axis=0)  12.5 us
    reduce_sum x2, other arithmetic, one_head(): total = jnp.sum(pre_weights, axis=-1) + jnp.sum(suf_weights, axis=-1)  12 us
    dot_general x1, matrix products, one_head(): jnp.einsum('gqk,kd->gqd', suf_weights.astype(jnp.bfloat16), suffix[:, vco...  10.7 us
    dot_general x1, matrix products, one_head(): jnp.einsum('qgd,kd->gqk', q, suffix[:, cols], preferred_element_type=jnp....  9.33 us
  transfers between devices with their start and end apart: 10, of which 10 were waited for; matrix products, arithmetic and copies ran while one was open for 15% of the time, Pallas kernels for 0%

profile of v2, /device:TPU:1, one launch (start us, length us, event | category | flops | bytes accessed | tf_op | source)
XLA Modules:
  0.0 330.9 jit_solution(10927618670636965421)
XLA Ops:
  9.7 16.3 %collective-permute-start = (bf16[288,256]{1,0:T(8,128)(2,1)S(1)}, bf16[288,256]{1,0:T(8,128)(2,1)S(1)}, u32[]{:S(2)}, u32[]{:S(2)}) collective-permute-start(bf16[288,256]{1,0:T(8,128)(2,1)S(1)} %pad_maximum_fusion.8), channel_id=1, source_target_pairs={{496,0},{504,8},{0,16},{8,24},{16,32},{24,40},{32,48},{40,56},{48,... | collective-permute-start | bytes 442376 | tf_op jit(solution)/shard_map/ppermute | solution.py:22
  26.0 7.5 %collective-permute-done = bf16[288,256]{1,0:T(8,128)(2,1)S(1)} collective-permute-done((bf16[288,256]{1,0:T(8,128)(2,1)S(1)}, bf16[288,256]{1,0:T(8,128)(2,1)S(1)}, u32[]{:S(2)}, u32[]{:S(2)}) %collective-permute-start) | collective-permute-done | bytes 147488 | tf_op jit(solution)/shard_map/ppermute | solution.py:22
  34.1 9.5 %collective-permute-start.1 = (bf16[576,256]{1,0:T(8,128)(2,1)S(1)}, bf16[576,256]{1,0:T(8,128)(2,1)S(1)}, u32[]{:S(2)}, u32[]{:S(2)}) collective-permute-start(bf16[576,256]{1,0:T(8,128)(2,1)S(1)} %pad_maximum_fusion.6), channel_id=1, source_target_pairs={{504,0},{0,8},{8,16},{16,24},{24,32},{32,40},{40,48},{48,56},{56,6... | collective-permute-start | bytes 884744 | tf_op jit(solution)/shard_map/ppermute | solution.py:22
  43.7 3.6 %collective-permute-done.1 = bf16[576,256]{1,0:T(8,128)(2,1)S(1)} collective-permute-done((bf16[576,256]{1,0:T(8,128)(2,1)S(1)}, bf16[576,256]{1,0:T(8,128)(2,1)S(1)}, u32[]{:S(2)}, u32[]{:S(2)}) %collective-permute-start.1) | collective-permute-done | bytes 294944 | tf_op jit(solution)/shard_map/ppermute | solution.py:22
  47.5 4.7 %collective-permute-start.2 = (bf16[1152,256]{1,0:T(8,128)(2,1)S(1)}, bf16[1152,256]{1,0:T(8,128)(2,1)S(1)}, u32[]{:S(2)}, u32[]{:S(2)}) collective-permute-start(bf16[1152,256]{1,0:T(8,128)(2,1)S(1)} %pad_maximum_fusion.2), channel_id=1, source_target_pairs={{448,0},{456,8},{464,16},{472,24},{480,32},{488,40},{496,48},{504,... | collective-permute-start | bytes 1769480 | tf_op jit(solution)/shard_map/ppermute | solution.py:22
  52.2 11.9 %collective-permute-done.2 = bf16[1152,256]{1,0:T(8,128)(2,1)S(1)} collective-permute-done((bf16[1152,256]{1,0:T(8,128)(2,1)S(1)}, bf16[1152,256]{1,0:T(8,128)(2,1)S(1)}, u32[]{:S(2)}, u32[]{:S(2)}) %collective-permute-start.2) | collective-permute-done | bytes 589856 | tf_op jit(solution)/shard_map/ppermute | solution.py:22
  64.5 5.5 %collective-permute-start.3 = (bf16[2304,256]{1,0:T(8,128)(2,1)S(1)}, bf16[2304,256]{1,0:T(8,128)(2,1)S(1)}, u32[]{:S(2)}, u32[]{:S(2)}) collective-permute-start(bf16[2304,256]{1,0:T(8,128)(2,1)S(1)} %pad_maximum_fusion), channel_id=1, source_target_pairs={{480,0},{488,8},{496,16},{504,24},{0,32},{8,40},{16,48},{24,56},{3... | collective-permute-start | bytes 3538952 | tf_op jit(solution)/shard_map/ppermute | solution.py:22
  70.7 20.6 %collective-permute-done.3 = bf16[2304,256]{1,0:T(8,128)(2,1)S(1)} collective-permute-done((bf16[2304,256]{1,0:T(8,128)(2,1)S(1)}, bf16[2304,256]{1,0:T(8,128)(2,1)S(1)}, u32[]{:S(2)}, u32[]{:S(2)}) %collective-permute-start.3) | collective-permute-done | bytes 1179680 | tf_op jit(solution)/shard_map/ppermute | solution.py:22
  92.9 2.0 collective-permute-start.4
  94.9 3.7 %and_and_fusion = pred[256,4352]{0,1:T(8,128)(4,1)S(1)} fusion(s32[256]{0:T(256)S(1)} %iota_add_fusion.1, s32[256]{0:T(256)S(1)} %convert_reduce_fusion.1, s32[4352]{0:T(1024)S(1)} %add.52, s32[4352]{0:T(1024)S(1)} %convert_reduce_fusion, pred[4352]{0:T(1024)(128)(4,1)S(1)} %broadcast_compare_fusion), kind=kLoop, calls=%fused_computation.14 | loop fusion | flops 4456448 | bytes 1155328 | tf_op jit(solution)/shard_map/and | solution.py:92
  99.8 1.3 slice.74
  101.1 3.5 %collective-permute-done.4 = bf16[768,256]{1,0:T(8,128)(2,1)} collective-permute-done((bf16[768,256]{1,0:T(8,128)(2,1)}, bf16[768,256]{1,0:T(8,128)(2,1)}, u32[]{:S(2)}, u32[]{:S(2)}) %collective-permute-start.4) | collective-permute-done | bytes 393248 | tf_op jit(solution)/shard_map/ppermute | solution.py:22
  108.4 2.1 collective-permute-start.5
  110.5 9.3 %fusion = (f32[5,256]{1,0:T(8,128)S(1)}, f32[4352,256,5]{1,0,2:T(8,128)}) fusion(pred[256,4352]{0,1:T(8,128)(4,1)S(1)} %and_and_fusion, bf16[256,5,128]{0,2,1:T(8,128)(2,1)S(1)} %bitcast.124, bf16[4352,256]{1,0:T(8,128)(2,1)S(1)} %bitcast.142), kind=kOutput, calls=%fused_computation.2 | convolution fusion | flops 1442773760 | bytes 24843264 | tf_op jit(solution)/shard_map/qgd,kd->gqk/dot_general | solution.py:108
  121.2 1.5 bitcast_reduce_fusion
  122.7 1.7 fusion.7
  124.4 10.3 %fusion.1 = f32[5,256]{1,0:T(8,128)S(1)} fusion(f32[4352,256,5]{1,0,2:T(8,128)} %get-tuple-element.10, f32[5,256]{1,0:T(8,128)S(1)} %max.7, pred[256,4352]{0,1:T(8,128)(4,1)S(1)} %and_and_fusion), kind=kLoop, calls=%fused_computation.3 | loop fusion | flops 27851520 | bytes 23406592 | tf_op jit(solution)/shard_map/reduce_sum | solution.py:115
  134.7 2.0 fusion.9
  136.8 10.7 %fusion.18 = bf16[5,256,128]{1,2,0:T(8,128)(2,1)S(1)} fusion(f32[5,256,128]{1,2,0:T(8,128)S(1)} %fusion.9, bf16[4352,256]{1,0:T(8,128)(2,1)S(1)} %bitcast.143, f32[4352,256,5]{1,0,2:T(8,128)} %get-tuple-element.10, f32[5,256]{1,0:T(8,128)S(1)} %max.7, pred[256,4352]{0,1:T(8,128)(4,1)S(1)} %and_and_fusion, f32[5,256]{1,0:T(8,128)S(1)} %add.56), kind=kOutput, calls=%fused_computation.22 | convolution fusion | flops 1454407680 | bytes 25509888 | tf_op jit(solution)/shard_map/gqk,kd->gqd/dot_general | solution.py:121
  147.5 12.5 %collective-permute-start.6 = (bf16[256,640]{0,1:T(8,128)(2,1)S(1)}, bf16[256,640]{0,1:T(8,128)(2,1)S(1)}, u32[]{:S(2)}, u32[]{:S(2)}) collective-permute-start(bf16[256,640]{0,1:T(8,128)(2,1)S(1)} %bitcast.145), channel_id=1, source_target_pairs={{0,8},{8,0},{1,9},{9,1},{2,10},{10,2},{3,11},{11,3},{4,12},{12,4},... | collective-permute-start | bytes 983048 | tf_op jit(solution)/shard_map/ppermute | solution.py:137
  161.2 83.1 %all-gather.2.cloned.1.call-done = bf16[640,2560]{0,1:T(8,128)(2,1)} async-done(((bf16[640,80]{0,1:T(8,128)(2,1)}), bf16[640,2560]{0,1:T(8,128)(2,1)}) %all-gather.2.cloned.1.call-update) | async-done | bytes 3276816 | tf_op jit(solution)/shard_map/all_gather | solution.py:138
  244.3 5.6 %convolution_convert_fusion = bf16[512,2560]{0,1:T(8,128)(2,1)} fusion(bf16[640,2560]{0,1:T(8,128)(2,1)} %all-gather.2.cloned.1.call-done, bf16[256,640]{0,1:T(8,128)(2,1)S(1)} %collective-permute-done.6, bf16[256,640]{0,1:T(8,128)(2,1)S(1)} %bitcast.146), kind=kOutput, calls=%fused_computation.13 | convolution fusion | flops 1680343040 | bytes 6553600 | tf_op jit(solution)/shard_map/dot_general | solution.py:139
  249.9 63.8 %reduce-scatter.2.cloned.1.call-done = bf16[512,320]{0,1:T(8,128)(2,1)} async-done(((bf16[512,2560]{0,1:T(8,128)(2,1)}), bf16[512,320]{0,1:T(8,128)(2,1)}) %reduce-scatter.2.cloned.1.call-update) | async-done | bytes 327696 | tf_op jit(solution)/shard_map/reduce_scatter | solution.py:140
  314.7 6.5 %collective-permute-start.7 = (bf16[256,320]{0,1:T(8,128)(2,1)S(1)}, bf16[256,320]{0,1:T(8,128)(2,1)S(1)}, u32[]{:S(2)}, u32[]{:S(2)}) collective-permute-start(bf16[256,320]{0,1:T(8,128)(2,1)S(1)} %slice.79), channel_id=1, source_target_pairs={{0,8},{8,0},{1,9},{9,1},{2,10},{10,2},{3,11},{11,3},{4,12},{12,4},... | collective-permute-start | bytes 491528 | tf_op jit(solution)/shard_map/ppermute | solution.py:141
  (79 shorter events, 17.7 us)
Async XLA Ops:
  6.5 237.8 %all-gather.2.cloned.1.call-start = ((), (), s32[]{:S(2)}) async-start(), calls=%async_computation.1 | async-start | bytes 3379200 | tf_op jit(solution)/shard_map/all_gather | solution.py:138
  9.7 23.7 %collective-permute-start = (bf16[288,256]{1,0:T(8,128)(2,1)S(1)}, bf16[288,256]{1,0:T(8,128)(2,1)S(1)}, u32[]{:S(2)}, u32[]{:S(2)}) collective-permute-start(bf16[288,256]{1,0:T(8,128)(2,1)S(1)} %pad_maximum_fusion.8), channel_id=1, source_target_pairs={{496,0},{504,8},{0,16},{8,24},{16,32},{24,40},{32,48},{40,56},{48,... | collective-permute-start | bytes 442376 | tf_op jit(solution)/shard_map/ppermute | solution.py:22
  33.4 0.7 copy-start.1
  34.1 13.2 %collective-permute-start.1 = (bf16[576,256]{1,0:T(8,128)(2,1)S(1)}, bf16[576,256]{1,0:T(8,128)(2,1)S(1)}, u32[]{:S(2)}, u32[]{:S(2)}) collective-permute-start(bf16[576,256]{1,0:T(8,128)(2,1)S(1)} %pad_maximum_fusion.6), channel_id=1, source_target_pairs={{504,0},{0,8},{8,16},{16,24},{24,32},{32,40},{40,48},{48,56},{56,6... | collective-permute-start | bytes 884744 | tf_op jit(solution)/shard_map/ppermute | solution.py:22
  47.3 22.8 %copy-start.3 = (s32[17]{0:T(128)S(1)}, s32[17]{0:T(128)}, u32[]{:S(2)}) copy-start(s32[17]{0:T(128)} %constant.49) | copy-start | bytes 208
  47.4 22.9 %copy-start.2 = (s32[16]{0:T(128)S(1)}, s32[16]{0:T(128)}, u32[]{:S(2)}) copy-start(s32[16]{0:T(128)} %param.14) | copy-start | bytes 196
  47.5 16.6 %collective-permute-start.2 = (bf16[1152,256]{1,0:T(8,128)(2,1)S(1)}, bf16[1152,256]{1,0:T(8,128)(2,1)S(1)}, u32[]{:S(2)}, u32[]{:S(2)}) collective-permute-start(bf16[1152,256]{1,0:T(8,128)(2,1)S(1)} %pad_maximum_fusion.2), channel_id=1, source_target_pairs={{448,0},{456,8},{464,16},{472,24},{480,32},{488,40},{496,48},{504,... | collective-permute-start | bytes 1769480 | tf_op jit(solution)/shard_map/ppermute | solution.py:22
  64.5 26.8 %collective-permute-start.3 = (bf16[2304,256]{1,0:T(8,128)(2,1)S(1)}, bf16[2304,256]{1,0:T(8,128)(2,1)S(1)}, u32[]{:S(2)}, u32[]{:S(2)}) collective-permute-start(bf16[2304,256]{1,0:T(8,128)(2,1)S(1)} %pad_maximum_fusion), channel_id=1, source_target_pairs={{480,0},{488,8},{496,16},{504,24},{0,32},{8,40},{16,48},{24,56},{3... | collective-permute-start | bytes 3538952 | tf_op jit(solution)/shard_map/ppermute | solution.py:22
  70.1 243.7 %reduce-scatter.2.cloned.1.call-start = ((), (), s32[]{:S(2)}) async-start(), calls=%async_computation.2 | async-start | bytes 2949120 | tf_op jit(solution)/shard_map/reduce_scatter | solution.py:140
  91.3 3.6 %copy-start = (bf16[2304,256]{1,0:T(8,128)(2,1)}, bf16[2304,256]{1,0:T(8,128)(2,1)S(1)}, u32[]{:S(2)}) copy-start(bf16[2304,256]{1,0:T(8,128)(2,1)S(1)} %collective-permute-done.3) | copy-start | bytes 3538948
  92.9 11.7 %collective-permute-start.4 = (bf16[768,256]{1,0:T(8,128)(2,1)}, bf16[768,256]{1,0:T(8,128)(2,1)}, u32[]{:S(2)}, u32[]{:S(2)}) collective-permute-start(bf16[768,256]{1,0:T(8,128)(2,1)} %pad_maximum_fusion.4), channel_id=1, source_target_pairs={{384,0},{392,8},{400,16},{408,24},{416,32},{424,40},{432,48},{440,... | collective-permute-start | bytes 1179656 | tf_op jit(solution)/shard_map/ppermute | solution.py:22
  108.4 11.9 %collective-permute-start.5 = (bf16[32,32,256]{2,1,0:T(8,128)(2,1)S(1)}, bf16[32,32,256]{2,1,0:T(8,128)(2,1)S(1)}, u32[]{:S(2)}, u32[]{:S(2)}) collective-permute-start(bf16[32,32,256]{2,1,0:T(8,128)(2,1)S(1)} %constant_dynamic-update-slice_fusion.9), channel_id=1, source_target_pairs={{256,0},{264,8},{272,16},{280,24},{288,32},{296,40},{304,48},{312,... | collective-permute-start | bytes 1572872 | tf_op jit(solution)/shard_map/ppermute | solution.py:22
  147.5 13.8 %collective-permute-start.6 = (bf16[256,640]{0,1:T(8,128)(2,1)S(1)}, bf16[256,640]{0,1:T(8,128)(2,1)S(1)}, u32[]{:S(2)}, u32[]{:S(2)}) collective-permute-start(bf16[256,640]{0,1:T(8,128)(2,1)S(1)} %bitcast.145), channel_id=1, source_target_pairs={{0,8},{8,0},{1,9},{9,1},{2,10},{10,2},{3,11},{11,3},{4,12},{12,4},... | collective-permute-start | bytes 983048 | tf_op jit(solution)/shard_map/ppermute | solution.py:137
  314.7 7.5 %collective-permute-start.7 = (bf16[256,320]{0,1:T(8,128)(2,1)S(1)}, bf16[256,320]{0,1:T(8,128)(2,1)S(1)}, u32[]{:S(2)}, u32[]{:S(2)}) collective-permute-start(bf16[256,320]{0,1:T(8,128)(2,1)S(1)} %slice.79), channel_id=1, source_target_pairs={{0,8},{8,0},{1,9},{9,1},{2,10},{10,2},{3,11},{11,3},{4,12},{12,4},... | collective-permute-start | bytes 491528 | tf_op jit(solution)/shard_map/ppermute | solution.py:141
Sparse Core Ops, SparseCore 0:
  70.2 174.0 all-gather.1
  250.1 63.6 reduce-scatter.1

commit v3 on v2

--- a/solution.py
+++ b/solution.py
@@ -135,7 +135,9 @@
     swap = [(0, 1), (1, 0)]
     core = lax.axis_index("core")
     both = jnp.concatenate((attn, lax.ppermute(attn, "core", swap)), axis=0)
-    weight = lax.all_gather(out_weight, BLK[:-1], axis=1, tiled=True)
+    weight = out_weight
+    for name in BLK[-2::-1]:
+        weight = lax.all_gather(weight, name, axis=1, tiled=True)
     product = jnp.dot(both, weight, preferred_element_type=jnp.float32)
     reduced = lax.psum_scatter(product.astype(jnp.bfloat16), "mp", scatter_dimension=1, tiled=True)
     other = lax.ppermute(reduced[tok_rows:], "core", swap)

time: 332 us -> 289 us (0.87)
  waiting for transfers between devices: 197 us -> 99.3 us
  blocking collectives: 0 us -> 48.5 us
  starting transfers between devices: 59.2 us -> 64.9 us
    all_gather x1, waiting for transfers between devices: 83.1 us -> 0.01 us  [per_device(): weight = lax.all_gather(weight, name, axis=1, tiled=True)]
    all_gather x0 -> x2, blocking collectives: none -> 48.5 us  [per_device(): weight = lax.all_gather(weight, name, axis=1, tiled=True)]
    ppermute x6, waiting for transfers between devices: 47.7 us -> 12 us  [shifted(): return lax.ppermute(block, axis, route)]
    reduce_scatter x1, waiting for transfers between devices: 63.8 us -> 85.1 us  [per_device(): lax.psum_scatter(product.astype(jnp.bfloat16), 'mp', scatter_dimension=1,...]
    ppermute x1, starting transfers between devices: 12.5 us -> 16.6 us  [per_device(): both = jnp.concatenate((attn, lax.ppermute(attn, 'core', swap)), axis=0)]
    unnamed x31 -> x33, local copies, waits for them, and re-layouts: 7.63 us -> 7.68 us
  transfers between devices with their start and end apart: 10 -> 10, of which waited for: 10 -> 6; matrix products, arithmetic and copies ran while one was open for 15% -> 17% of each run, Pallas kernels for 0% -> 0%
where the time goes in v3:
time: 289 us; the launch traced here: 288 us
  waiting for transfers between devices  99.3 us (34%)
  starting transfers between devices  64.9 us (22%)
  blocking collectives  48.5 us (17%)
  matrix products  29.5 us (10%)
  other arithmetic  18.4 us (6%)
  between operations  13.9 us (5%)
  local copies, waits for them, and re-layouts  13.5 us (5%)
    reduce_scatter x1, waiting for transfers between devices, per_device(): lax.psum_scatter(product.astype(jnp.bfloat16), 'mp', scatter_dimension=1,...  85.1 us
    all_gather x2, blocking collectives, per_device(): weight = lax.all_gather(weight, name, axis=1, tiled=True)  48.5 us
    ppermute x6, starting transfers between devices, shifted(): return lax.ppermute(block, axis, route)  42.5 us
    ppermute x1, starting transfers between devices, per_device(): both = jnp.concatenate((attn, lax.ppermute(attn, 'core', swap)), axis=0)  16.6 us
    reduce_sum x2, other arithmetic, one_head(): total = jnp.sum(pre_weights, axis=-1) + jnp.sum(suf_weights, axis=-1)  12 us
    ppermute x6, waiting for transfers between devices, shifted(): return lax.ppermute(block, axis, route)  12 us
    dot_general x1, matrix products, one_head(): jnp.einsum('gqk,kd->gqd', suf_weights.astype(jnp.bfloat16), suffix[:, vco...  10.8 us
    dot_general x1, matrix products, one_head(): jnp.einsum('qgd,kd->gqk', q, suffix[:, cols], preferred_element_type=jnp....  9.48 us
  transfers between devices with their start and end apart: 10, of which 6 were waited for; matrix products, arithmetic and copies ran while one was open for 17% of the time, Pallas kernels for 0%

profile of v3, /device:TPU:1, one launch (start us, length us, event | category | flops | bytes accessed | tf_op | source)
XLA Modules:
  0.0 287.9 jit_solution(7152190589090825945)
XLA Ops:
  9.7 16.3 %collective-permute-start = (bf16[288,256]{1,0:T(8,128)(2,1)S(1)}, bf16[288,256]{1,0:T(8,128)(2,1)S(1)}, u32[]{:S(2)}, u32[]{:S(2)}) collective-permute-start(bf16[288,256]{1,0:T(8,128)(2,1)S(1)} %pad_maximum_fusion.8), channel_id=1, source_target_pairs={{496,0},{504,8},{0,16},{8,24},{16,32},{24,40},{32,48},{40,56},{48,... | collective-permute-start | bytes 442376 | tf_op jit(solution)/shard_map/ppermute | solution.py:22
  26.0 7.5 %collective-permute-done = bf16[288,256]{1,0:T(8,128)(2,1)S(1)} collective-permute-done((bf16[288,256]{1,0:T(8,128)(2,1)S(1)}, bf16[288,256]{1,0:T(8,128)(2,1)S(1)}, u32[]{:S(2)}, u32[]{:S(2)}) %collective-permute-start) | collective-permute-done | bytes 147488 | tf_op jit(solution)/shard_map/ppermute | solution.py:22
  34.2 9.5 %collective-permute-start.1 = (bf16[576,256]{1,0:T(8,128)(2,1)S(1)}, bf16[576,256]{1,0:T(8,128)(2,1)S(1)}, u32[]{:S(2)}, u32[]{:S(2)}) collective-permute-start(bf16[576,256]{1,0:T(8,128)(2,1)S(1)} %pad_maximum_fusion.6), channel_id=1, source_target_pairs={{504,0},{0,8},{8,16},{16,24},{24,32},{32,40},{40,48},{48,56},{56,6... | collective-permute-start | bytes 884744 | tf_op jit(solution)/shard_map/ppermute | solution.py:22
  43.7 3.6 %collective-permute-done.1 = bf16[576,256]{1,0:T(8,128)(2,1)S(1)} collective-permute-done((bf16[576,256]{1,0:T(8,128)(2,1)S(1)}, bf16[576,256]{1,0:T(8,128)(2,1)S(1)}, u32[]{:S(2)}, u32[]{:S(2)}) %collective-permute-start.1) | collective-permute-done | bytes 294944 | tf_op jit(solution)/shard_map/ppermute | solution.py:22
  47.6 4.7 %collective-permute-start.2 = (bf16[1152,256]{1,0:T(8,128)(2,1)S(1)}, bf16[1152,256]{1,0:T(8,128)(2,1)S(1)}, u32[]{:S(2)}, u32[]{:S(2)}) collective-permute-start(bf16[1152,256]{1,0:T(8,128)(2,1)S(1)} %pad_maximum_fusion.2), channel_id=1, source_target_pairs={{448,0},{456,8},{464,16},{472,24},{480,32},{488,40},{496,48},{504,... | collective-permute-start | bytes 1769480 | tf_op jit(solution)/shard_map/ppermute | solution.py:22
  52.3 14.1 %all_gather.9 = bf16[640,160]{0,1:T(8,128)(2,1)S(1)} all-gather(bf16[640,80]{0,1:T(8,128)(2,1)S(1)} %copy-done.2), channel_id=1, replica_groups=mesh['y'=4,'x'=4,'zh'=2,'core'=2,'mp'=8] {'zh'}, dimensions={1}, use_global_device_ids=true | all-gather | bytes 307200 | tf_op jit(solution)/shard_map/all_gather | solution.py:140
  66.7 3.4 %collective-permute-start.3 = (bf16[2304,256]{1,0:T(8,128)(2,1)S(1)}, bf16[2304,256]{1,0:T(8,128)(2,1)S(1)}, u32[]{:S(2)}, u32[]{:S(2)}) collective-permute-start(bf16[2304,256]{1,0:T(8,128)(2,1)S(1)} %pad_maximum_fusion), channel_id=1, source_target_pairs={{480,0},{488,8},{496,16},{504,24},{0,32},{8,40},{16,48},{24,56},{3... | collective-permute-start | bytes 3538952 | tf_op jit(solution)/shard_map/ppermute | solution.py:22
  70.1 34.4 %all_gather.10 = bf16[640,640]{0,1:T(8,128)(2,1)} all-gather(bf16[640,160]{0,1:T(8,128)(2,1)S(1)} %all_gather.9), channel_id=1, replica_groups=mesh['y'=4,'x'=4,'zh'=2,'core'=2,'mp'=8] {'x'}, dimensions={1}, use_global_device_ids=true | all-gather | bytes 1024000 | tf_op jit(solution)/shard_map/all_gather | solution.py:140
  106.8 3.0 %collective-permute-start.4 = (bf16[768,256]{1,0:T(8,128)(2,1)}, bf16[768,256]{1,0:T(8,128)(2,1)}, u32[]{:S(2)}, u32[]{:S(2)}) collective-permute-start(bf16[768,256]{1,0:T(8,128)(2,1)} %pad_maximum_fusion.4), channel_id=1, source_target_pairs={{384,0},{392,8},{400,16},{408,24},{416,32},{424,40},{432,48},{440,... | collective-permute-start | bytes 1179656 | tf_op jit(solution)/shard_map/ppermute | solution.py:22
  109.8 3.7 %and_and_fusion = pred[256,4352]{0,1:T(8,128)(4,1)S(1)} fusion(s32[256]{0:T(256)S(1)} %iota_add_fusion.1, s32[256]{0:T(256)S(1)} %convert_reduce_fusion.1, s32[4352]{0:T(1024)S(1)} %add.52, s32[4352]{0:T(1024)S(1)} %convert_reduce_fusion, pred[4352]{0:T(1024)(128)(4,1)S(1)} %broadcast_compare_fusion), kind=kLoop, calls=%fused_computation.14 | loop fusion | flops 4456448 | bytes 1155328 | tf_op jit(solution)/shard_map/and | solution.py:92
  113.5 1.1 copy.28
  114.7 1.3 slice.74
  120.6 5.6 %collective-permute-start.5 = (bf16[32,32,256]{2,1,0:T(8,128)(2,1)S(1)}, bf16[32,32,256]{2,1,0:T(8,128)(2,1)S(1)}, u32[]{:S(2)}, u32[]{:S(2)}) collective-permute-start(bf16[32,32,256]{2,1,0:T(8,128)(2,1)S(1)} %constant_dynamic-update-slice_fusion.9), channel_id=1, source_target_pairs={{256,0},{264,8},{272,16},{280,24},{288,32},{296,40},{304,48},{312,... | collective-permute-start | bytes 1572872 | tf_op jit(solution)/shard_map/ppermute | solution.py:22
  126.2 9.5 %fusion = (f32[5,256]{1,0:T(8,128)S(1)}, f32[4352,256,5]{1,0,2:T(8,128)}) fusion(pred[256,4352]{0,1:T(8,128)(4,1)S(1)} %and_and_fusion, bf16[256,5,128]{0,2,1:T(8,128)(2,1)S(1)} %bitcast.124, bf16[4352,256]{1,0:T(8,128)(2,1)S(1)} %bitcast.142), kind=kOutput, calls=%fused_computation.2 | convolution fusion | flops 1442773760 | bytes 24843264 | tf_op jit(solution)/shard_map/qgd,kd->gqk/dot_general | solution.py:108
  136.6 1.5 bitcast_reduce_fusion
  138.1 1.7 fusion.7
  139.8 10.3 %fusion.1 = f32[5,256]{1,0:T(8,128)S(1)} fusion(f32[4352,256,5]{1,0,2:T(8,128)} %get-tuple-element.10, f32[5,256]{1,0:T(8,128)S(1)} %max.7, pred[256,4352]{0,1:T(8,128)(4,1)S(1)} %and_and_fusion), kind=kLoop, calls=%fused_computation.3 | loop fusion | flops 27851520 | bytes 23406592 | tf_op jit(solution)/shard_map/reduce_sum | solution.py:115
  150.1 2.0 fusion.9
  152.2 10.8 %fusion.18 = bf16[5,256,128]{1,2,0:T(8,128)(2,1)S(1)} fusion(f32[5,256,128]{1,2,0:T(8,128)S(1)} %fusion.9, bf16[4352,256]{1,0:T(8,128)(2,1)S(1)} %bitcast.143, f32[4352,256,5]{1,0,2:T(8,128)} %get-tuple-element.10, f32[5,256]{1,0:T(8,128)S(1)} %max.7, pred[256,4352]{0,1:T(8,128)(4,1)S(1)} %and_and_fusion, f32[5,256]{1,0:T(8,128)S(1)} %add.56), kind=kOutput, calls=%fused_computation.22 | convolution fusion | flops 1454407680 | bytes 25509888 | tf_op jit(solution)/shard_map/gqk,kd->gqd/dot_general | solution.py:121
  163.0 16.6 %collective-permute-start.6 = (bf16[256,640]{0,1:T(8,128)(2,1)S(1)}, bf16[256,640]{0,1:T(8,128)(2,1)S(1)}, u32[]{:S(2)}, u32[]{:S(2)}) collective-permute-start(bf16[256,640]{0,1:T(8,128)(2,1)S(1)} %bitcast.145), channel_id=1, source_target_pairs={{0,8},{8,0},{1,9},{9,1},{2,10},{10,2},{3,11},{11,3},{4,12},{12,4},... | collective-permute-start | bytes 983048 | tf_op jit(solution)/shard_map/ppermute | solution.py:137
  179.6 1.2 collective-permute-done.6
  180.9 5.6 %convolution_convert_fusion = bf16[512,2560]{0,1:T(8,128)(2,1)} fusion(bf16[640,2560]{0,1:T(8,128)(2,1)} %all-gather.2.cloned.1.call-done, bf16[256,640]{0,1:T(8,128)(2,1)S(1)} %collective-permute-done.6, bf16[256,640]{0,1:T(8,128)(2,1)S(1)} %bitcast.146), kind=kOutput, calls=%fused_computation.13 | convolution fusion | flops 1680343040 | bytes 6553600 | tf_op jit(solution)/shard_map/dot_general | solution.py:141
  186.5 85.1 %reduce-scatter.2.cloned.1.call-done = bf16[512,320]{0,1:T(8,128)(2,1)} async-done(((bf16[512,2560]{0,1:T(8,128)(2,1)}), bf16[512,320]{0,1:T(8,128)(2,1)}) %reduce-scatter.2.cloned.1.call-update) | async-done | bytes 327696 | tf_op jit(solution)/shard_map/reduce_scatter | solution.py:142
  272.5 5.6 %collective-permute-start.7 = (bf16[256,320]{0,1:T(8,128)(2,1)S(1)}, bf16[256,320]{0,1:T(8,128)(2,1)S(1)}, u32[]{:S(2)}, u32[]{:S(2)}) collective-permute-start(bf16[256,320]{0,1:T(8,128)(2,1)S(1)} %slice.79), channel_id=1, source_target_pairs={{0,8},{8,0},{1,9},{9,1},{2,10},{10,2},{3,11},{11,3},{4,12},{12,4},... | collective-permute-start | bytes 491528 | tf_op jit(solution)/shard_map/ppermute | solution.py:143
  (83 shorter events, 15.7 us)
Async XLA Ops:
  6.5 45.8 %copy-start.2 = (bf16[640,80]{0,1:T(8,128)(2,1)S(1)}, bf16[640,80]{0,1:T(8,128)(2,1)}, u32[]{:S(2)}) copy-start(bf16[640,80]{0,1:T(8,128)(2,1)} %param.13) | copy-start | bytes 307204
  6.5 174.3 %all-gather.2.cloned.1.call-start = ((), (), s32[]{:S(2)}) async-start(), calls=%async_computation.1 | async-start | bytes 4096000 | tf_op jit(solution)/shard_map/all_gather | solution.py:140
  9.7 23.7 %collective-permute-start = (bf16[288,256]{1,0:T(8,128)(2,1)S(1)}, bf16[288,256]{1,0:T(8,128)(2,1)S(1)}, u32[]{:S(2)}, u32[]{:S(2)}) collective-permute-start(bf16[288,256]{1,0:T(8,128)(2,1)S(1)} %pad_maximum_fusion.8), channel_id=1, source_target_pairs={{496,0},{504,8},{0,16},{8,24},{16,32},{24,40},{32,48},{40,56},{48,... | collective-permute-start | bytes 442376 | tf_op jit(solution)/shard_map/ppermute | solution.py:22
  33.5 0.7 copy-start.1
  34.2 13.2 %collective-permute-start.1 = (bf16[576,256]{1,0:T(8,128)(2,1)S(1)}, bf16[576,256]{1,0:T(8,128)(2,1)S(1)}, u32[]{:S(2)}, u32[]{:S(2)}) collective-permute-start(bf16[576,256]{1,0:T(8,128)(2,1)S(1)} %pad_maximum_fusion.6), channel_id=1, source_target_pairs={{504,0},{0,8},{8,16},{16,24},{24,32},{32,40},{40,48},{48,56},{56,6... | collective-permute-start | bytes 884744 | tf_op jit(solution)/shard_map/ppermute | solution.py:22
  47.5 57.1 %copy-start.4 = (s32[17]{0:T(128)S(1)}, s32[17]{0:T(128)}, u32[]{:S(2)}) copy-start(s32[17]{0:T(128)} %constant.49) | copy-start | bytes 208
  47.5 57.2 %copy-start.3 = (s32[16]{0:T(128)S(1)}, s32[16]{0:T(128)}, u32[]{:S(2)}) copy-start(s32[16]{0:T(128)} %param.14) | copy-start | bytes 196
  47.6 18.8 %collective-permute-start.2 = (bf16[1152,256]{1,0:T(8,128)(2,1)S(1)}, bf16[1152,256]{1,0:T(8,128)(2,1)S(1)}, u32[]{:S(2)}, u32[]{:S(2)}) collective-permute-start(bf16[1152,256]{1,0:T(8,128)(2,1)S(1)} %pad_maximum_fusion.2), channel_id=1, source_target_pairs={{448,0},{456,8},{464,16},{472,24},{480,32},{488,40},{496,48},{504,... | collective-permute-start | bytes 1769480 | tf_op jit(solution)/shard_map/ppermute | solution.py:22
  66.7 38.4 %collective-permute-start.3 = (bf16[2304,256]{1,0:T(8,128)(2,1)S(1)}, bf16[2304,256]{1,0:T(8,128)(2,1)S(1)}, u32[]{:S(2)}, u32[]{:S(2)}) collective-permute-start(bf16[2304,256]{1,0:T(8,128)(2,1)S(1)} %pad_maximum_fusion), channel_id=1, source_target_pairs={{480,0},{488,8},{496,16},{504,24},{0,32},{8,40},{16,48},{24,56},{3... | collective-permute-start | bytes 3538952 | tf_op jit(solution)/shard_map/ppermute | solution.py:22
  104.5 167.1 %reduce-scatter.2.cloned.1.call-start = ((), (), s32[]{:S(2)}) async-start(), calls=%async_computation.2 | async-start | bytes 2949120 | tf_op jit(solution)/shard_map/reduce_scatter | solution.py:142
  105.2 4.6 %copy-start = (bf16[2304,256]{1,0:T(8,128)(2,1)}, bf16[2304,256]{1,0:T(8,128)(2,1)S(1)}, u32[]{:S(2)}) copy-start(bf16[2304,256]{1,0:T(8,128)(2,1)S(1)} %collective-permute-done.3) | copy-start | bytes 3538948
  106.8 10.0 %collective-permute-start.4 = (bf16[768,256]{1,0:T(8,128)(2,1)}, bf16[768,256]{1,0:T(8,128)(2,1)}, u32[]{:S(2)}, u32[]{:S(2)}) collective-permute-start(bf16[768,256]{1,0:T(8,128)(2,1)} %pad_maximum_fusion.4), channel_id=1, source_target_pairs={{384,0},{392,8},{400,16},{408,24},{416,32},{424,40},{432,48},{440,... | collective-permute-start | bytes 1179656 | tf_op jit(solution)/shard_map/ppermute | solution.py:22
  120.6 15.1 %collective-permute-start.5 = (bf16[32,32,256]{2,1,0:T(8,128)(2,1)S(1)}, bf16[32,32,256]{2,1,0:T(8,128)(2,1)S(1)}, u32[]{:S(2)}, u32[]{:S(2)}) collective-permute-start(bf16[32,32,256]{2,1,0:T(8,128)(2,1)S(1)} %constant_dynamic-update-slice_fusion.9), channel_id=1, source_target_pairs={{256,0},{264,8},{272,16},{280,24},{288,32},{296,40},{304,48},{312,... | collective-permute-start | bytes 1572872 | tf_op jit(solution)/shard_map/ppermute | solution.py:22
  163.0 17.9 %collective-permute-start.6 = (bf16[256,640]{0,1:T(8,128)(2,1)S(1)}, bf16[256,640]{0,1:T(8,128)(2,1)S(1)}, u32[]{:S(2)}, u32[]{:S(2)}) collective-permute-start(bf16[256,640]{0,1:T(8,128)(2,1)S(1)} %bitcast.145), channel_id=1, source_target_pairs={{0,8},{8,0},{1,9},{9,1},{2,10},{10,2},{3,11},{11,3},{4,12},{12,4},... | collective-permute-start | bytes 983048 | tf_op jit(solution)/shard_map/ppermute | solution.py:137
  272.5 6.7 %collective-permute-start.7 = (bf16[256,320]{0,1:T(8,128)(2,1)S(1)}, bf16[256,320]{0,1:T(8,128)(2,1)S(1)}, u32[]{:S(2)}, u32[]{:S(2)}) collective-permute-start(bf16[256,320]{0,1:T(8,128)(2,1)S(1)} %slice.79), channel_id=1, source_target_pairs={{0,8},{8,0},{1,9},{9,1},{2,10},{10,2},{3,11},{11,3},{4,12},{12,4},... | collective-permute-start | bytes 491528 | tf_op jit(solution)/shard_map/ppermute | solution.py:143
Sparse Core Ops, SparseCore 0:
  104.6 66.2 all-gather.1
  186.6 84.9 reduce-scatter.1

commit v4 on v3

--- a/solution.py
+++ b/solution.py
@@ -68,6 +68,7 @@
     suffix = jnp.concatenate((got_suffix, suffix), axis=0)
     prefix = jnp.concatenate((got_prefix, prefix), axis=0)
     distances = [reach] + distances
+    early_count = prefix.shape[0]
     distance = 2 * reach
     while distance < blocks:
         prefix = jnp.concatenate((shifted(prefix, BLK, distance), prefix), axis=0)
@@ -75,7 +76,8 @@
 
     count = suffix.shape[0]
     suffix = suffix.reshape(count * tok_rows, 2 * width)
-    prefix = prefix.reshape(-1, 2 * width)
+    early_prefix = prefix[prefix.shape[0] - early_count:].reshape(-1, 2 * width)
+    late_prefix = prefix[: prefix.shape[0] - early_count].reshape(-1, 2 * width)
 
     req_ends = jnp.cumsum(lengths)
     local_rows = jnp.arange(tok_rows, dtype=jnp.int32)
@@ -96,34 +98,39 @@
 
     heads_of_query = queries.reshape(tok_rows, kv_heads, heads_per_group, HEAD_SIZE)
 
+    def scores_of(q, keys):
+        return (
+            jnp.einsum("qgd,kd->gqk", q, keys, preferred_element_type=jnp.float32) * score_scale
+        )
+
+    def weighted(weights, values):
+        return jnp.einsum(
+            "gqk,kd->gqd", weights.astype(jnp.bfloat16), values, preferred_element_type=jnp.float32
+        )
+
     def one_head(kv_head):
         cols = slice(kv_head * HEAD_SIZE, (kv_head + 1) * HEAD_SIZE)
         vcols = slice(width + kv_head * HEAD_SIZE, width + (kv_head + 1) * HEAD_SIZE)
         q = heads_of_query[:, kv_head]
-        pre_scores = (
-            jnp.einsum("qgd,kd->gqk", q, prefix[:, cols], preferred_element_type=jnp.float32)
-            * score_scale
+        pre_scores = scores_of(q, early_prefix[:, cols])
+        suf_scores = jnp.where(visible[None], scores_of(q, suffix[:, cols]), MASKED_SCORE)
+        first_peak = jnp.maximum(jnp.max(pre_scores, axis=-1), jnp.max(suf_scores, axis=-1))
+        pre_weights = jnp.exp(pre_scores - first_peak[..., None])
+        suf_weights = jnp.where(visible[None], jnp.exp(suf_scores - first_peak[..., None]), 0.0)
+        first_total = jnp.sum(pre_weights, axis=-1) + jnp.sum(suf_weights, axis=-1)
+        first_sum = weighted(pre_weights, early_prefix[:, vcols]) + weighted(
+            suf_weights, suffix[:, vcols]
         )
-        suf_scores = (
-            jnp.einsum("qgd,kd->gqk", q, suffix[:, cols], preferred_element_type=jnp.float32)
-            * score_scale
-        )
-        suf_scores = jnp.where(visible[None], suf_scores, MASKED_SCORE)
-        peak = jnp.maximum(jnp.max(pre_scores, axis=-1), jnp.max(suf_scores, axis=-1))
-        pre_weights = jnp.exp(pre_scores - peak[..., None])
-        suf_weights = jnp.where(visible[None], jnp.exp(suf_scores - peak[..., None]), 0.0)
-        total = jnp.sum(pre_weights, axis=-1) + jnp.sum(suf_weights, axis=-1)
-        summed = jnp.einsum(
-            "gqk,kd->gqd",
-            pre_weights.astype(jnp.bfloat16),
-            prefix[:, vcols],
-            preferred_element_type=jnp.float32,
-        ) + jnp.einsum(
-            "gqk,kd->gqd",
-            suf_weights.astype(jnp.bfloat16),
-            suffix[:, vcols],
-            preferred_element_type=jnp.float32,
-        )
+        late_scores = scores_of(q, late_prefix[:, cols])
+        late_peak = jnp.max(late_scores, axis=-1)
+        late_weights = jnp.exp(late_scores - late_peak[..., None])
+        late_total = jnp.sum(late_weights, axis=-1)
+        late_sum = weighted(late_weights, late_prefix[:, vcols])
+        peak = jnp.maximum(first_peak, late_peak)
+        first_scale = jnp.exp(first_peak - peak)
+        late_scale = jnp.exp(late_peak - peak)
+        total = first_total * first_scale + late_total * late_scale
+        summed = first_sum * first_scale[..., None] + late_sum * late_scale[..., None]
         return summed / total[..., None]
 
     attended = jnp.stack([one_head(h) for h in range(kv_heads)])

time: 289 us -> 277 us (0.958)
  local copies, waits for them, and re-layouts: 13.5 us -> 8.49 us
  waiting for transfers between devices: 99.3 us -> 94.9 us
  starting transfers between devices: 64.9 us -> 62 us
    reduce_scatter x1, waiting for transfers between devices: 85.1 us -> 78.3 us  [per_device(): lax.psum_scatter(product.astype(jnp.bfloat16), 'mp', scatter_dimension=1,...]
    unnamed x33 -> x37, local copies, waits for them, and re-layouts: 7.68 us -> 3.87 us
    ppermute x1, starting transfers between devices: 16.6 us -> 13.6 us  [per_device(): both = jnp.concatenate((attn, lax.ppermute(attn, 'core', swap)), axis=0)]
    dot_general x4 -> x6, matrix products: 23.8 us -> 24.3 us  [the longest x3 13.3 us: weighted(): jnp.einsum('gqk,kd->gqd', weights.astype(jnp.bfloat16), values, preferred...]
  transfers between devices with their start and end apart: 10 -> 10, of which waited for: 6 -> 6; matrix products, arithmetic and copies ran while one was open for 17% -> 16% of each run, Pallas kernels for 0% -> 0%
where the time goes in v4:
time: 277 us; the launch traced here: 276 us
  waiting for transfers between devices  94.9 us (34%)
  starting transfers between devices  62 us (22%)
  blocking collectives  47.5 us (17%)
  matrix products  30 us (11%)
  other arithmetic  19.5 us (7%)
  between operations  14 us (5%)
  local copies, waits for them, and re-layouts  8.49 us (3%)
    reduce_scatter x1, waiting for transfers between devices, per_device(): lax.psum_scatter(product.astype(jnp.bfloat16), 'mp', scatter_dimension=1,...  78.3 us
    all_gather x2, blocking collectives, per_device(): weight = lax.all_gather(weight, name, axis=1, tiled=True)  47.5 us
    ppermute x6, starting transfers between devices, shifted(): return lax.ppermute(block, axis, route)  41.8 us
    ppermute x6, waiting for transfers between devices, shifted(): return lax.ppermute(block, axis, route)  14.4 us
    ppermute x1, starting transfers between devices, per_device(): both = jnp.concatenate((attn, lax.ppermute(attn, 'core', swap)), axis=0)  13.6 us
    dot_general x3, matrix products, weighted(): jnp.einsum('gqk,kd->gqd', weights.astype(jnp.bfloat16), values, preferred...  13.3 us
    reduce_sum x2, other arithmetic, one_head(): first_total = jnp.sum(pre_weights, axis=-1) + jnp.sum(suf_weights, axis=-1)  12.1 us
    dot_general x3, matrix products, scores_of(): jnp.einsum('qgd,kd->gqk', q, keys, preferred_element_type=jnp.float32)  11 us
  transfers between devices with their start and end apart: 10, of which 6 were waited for; matrix products, arithmetic and copies ran while one was open for 16% of the time, Pallas kernels for 0%

profile of v4, /device:TPU:1, one launch (start us, length us, event | category | flops | bytes accessed | tf_op | source)
XLA Modules:
  0.0 276.4 jit_solution(5544522411360556232)
XLA Ops:
  9.7 16.3 %collective-permute-start = (bf16[288,256]{1,0:T(8,128)(2,1)S(1)}, bf16[288,256]{1,0:T(8,128)(2,1)S(1)}, u32[]{:S(2)}, u32[]{:S(2)}) collective-permute-start(bf16[288,256]{1,0:T(8,128)(2,1)S(1)} %pad_maximum_fusion.8), channel_id=1, source_target_pairs={{496,0},{504,8},{0,16},{8,24},{16,32},{24,40},{32,48},{40,56},{48,... | collective-permute-start | bytes 442376 | tf_op jit(solution)/shard_map/ppermute | solution.py:22
  26.0 7.5 %collective-permute-done = bf16[288,256]{1,0:T(8,128)(2,1)S(1)} collective-permute-done((bf16[288,256]{1,0:T(8,128)(2,1)S(1)}, bf16[288,256]{1,0:T(8,128)(2,1)S(1)}, u32[]{:S(2)}, u32[]{:S(2)}) %collective-permute-start) | collective-permute-done | bytes 147488 | tf_op jit(solution)/shard_map/ppermute | solution.py:22
  33.5 9.5 %collective-permute-start.1 = (bf16[576,256]{1,0:T(8,128)(2,1)S(1)}, bf16[576,256]{1,0:T(8,128)(2,1)S(1)}, u32[]{:S(2)}, u32[]{:S(2)}) collective-permute-start(bf16[576,256]{1,0:T(8,128)(2,1)S(1)} %pad_maximum_fusion.6), channel_id=1, source_target_pairs={{504,0},{0,8},{8,16},{16,24},{24,32},{32,40},{40,48},{48,56},{56,6... | collective-permute-start | bytes 884744 | tf_op jit(solution)/shard_map/ppermute | solution.py:22
  43.1 3.6 %collective-permute-done.1 = bf16[576,256]{1,0:T(8,128)(2,1)S(1)} collective-permute-done((bf16[576,256]{1,0:T(8,128)(2,1)S(1)}, bf16[576,256]{1,0:T(8,128)(2,1)S(1)}, u32[]{:S(2)}, u32[]{:S(2)}) %collective-permute-start.1) | collective-permute-done | bytes 294944 | tf_op jit(solution)/shard_map/ppermute | solution.py:22
  46.9 4.7 %collective-permute-start.2 = (bf16[1152,256]{1,0:T(8,128)(2,1)S(1)}, bf16[1152,256]{1,0:T(8,128)(2,1)S(1)}, u32[]{:S(2)}, u32[]{:S(2)}) collective-permute-start(bf16[1152,256]{1,0:T(8,128)(2,1)S(1)} %pad_maximum_fusion.2), channel_id=1, source_target_pairs={{448,0},{456,8},{464,16},{472,24},{480,32},{488,40},{496,48},{504,... | collective-permute-start | bytes 1769480 | tf_op jit(solution)/shard_map/ppermute | solution.py:22
  51.6 14.1 %all_gather.9 = bf16[640,160]{0,1:T(8,128)(2,1)S(1)} all-gather(bf16[640,80]{0,1:T(8,128)(2,1)} %param.13), channel_id=1, replica_groups=mesh['y'=4,'x'=4,'zh'=2,'core'=2,'mp'=8] {'zh'}, dimensions={1}, use_global_device_ids=true | all-gather | bytes 307200 | tf_op jit(solution)/shard_map/all_gather | solution.py:147
  67.1 3.1 %collective-permute-start.3 = (bf16[2304,256]{1,0:T(8,128)(2,1)}, bf16[2304,256]{1,0:T(8,128)(2,1)S(1)}, u32[]{:S(2)}, u32[]{:S(2)}) collective-permute-start(bf16[2304,256]{1,0:T(8,128)(2,1)} %pad_maximum_fusion), channel_id=1, source_target_pairs={{480,0},{488,8},{496,16},{504,24},{0,32},{8,40},{16,48},{24,56},{3... | collective-permute-start | bytes 3538952 | tf_op jit(solution)/shard_map/ppermute | solution.py:22
  70.2 33.5 %all_gather.10 = bf16[640,640]{0,1:T(8,128)(2,1)} all-gather(bf16[640,160]{0,1:T(8,128)(2,1)S(1)} %all_gather.9), channel_id=1, replica_groups=mesh['y'=4,'x'=4,'zh'=2,'core'=2,'mp'=8] {'x'}, dimensions={1}, use_global_device_ids=true | all-gather | bytes 1024000 | tf_op jit(solution)/shard_map/all_gather | solution.py:147
  105.2 3.2 %collective-permute-start.4 = (bf16[768,256]{1,0:T(8,128)(2,1)}, bf16[768,256]{1,0:T(8,128)(2,1)}, u32[]{:S(2)}, u32[]{:S(2)}) collective-permute-start(bf16[768,256]{1,0:T(8,128)(2,1)} %pad_maximum_fusion.4), channel_id=1, source_target_pairs={{384,0},{392,8},{400,16},{408,24},{416,32},{424,40},{432,48},{440,... | collective-permute-start | bytes 1179656 | tf_op jit(solution)/shard_map/ppermute | solution.py:22
  108.4 3.7 %and_and_fusion = pred[256,4352]{0,1:T(8,128)(4,1)S(1)} fusion(s32[256]{0:T(256)S(1)} %iota_add_fusion.1, s32[256]{0:T(256)S(1)} %convert_reduce_fusion.1, s32[4352]{0:T(1024)S(1)} %add.62, s32[4352]{0:T(1024)S(1)} %convert_reduce_fusion, pred[4352]{0:T(1024)(128)(4,1)S(1)} %broadcast_compare_fusion), kind=kLoop, calls=%fused_computation.14 | loop fusion | flops 4456448 | bytes 1155328 | tf_op jit(solution)/shard_map/and | solution.py:94
  112.1 1.1 copy.34
  113.4 3.3 %collective-permute-done.4 = bf16[768,256]{1,0:T(8,128)(2,1)} collective-permute-done((bf16[768,256]{1,0:T(8,128)(2,1)}, bf16[768,256]{1,0:T(8,128)(2,1)}, u32[]{:S(2)}, u32[]{:S(2)}) %collective-permute-start.4) | collective-permute-done | bytes 393248 | tf_op jit(solution)/shard_map/ppermute | solution.py:22
  118.9 5.0 %collective-permute-start.5 = (bf16[32,32,256]{2,1,0:T(8,128)(2,1)S(1)}, bf16[32,32,256]{2,1,0:T(8,128)(2,1)S(1)}, u32[]{:S(2)}, u32[]{:S(2)}) collective-permute-start(bf16[32,32,256]{2,1,0:T(8,128)(2,1)S(1)} %constant_dynamic-update-slice_fusion.9), channel_id=1, source_target_pairs={{256,0},{264,8},{272,16},{280,24},{288,32},{296,40},{304,48},{312,... | collective-permute-start | bytes 1572872 | tf_op jit(solution)/shard_map/ppermute | solution.py:22
  124.8 9.4 %fusion = (f32[5,256]{1,0:T(8,128)S(1)}, f32[4352,256,5]{1,0,2:T(8,128)}) fusion(pred[256,4352]{0,1:T(8,128)(4,1)S(1)} %and_and_fusion, bf16[256,5,128]{0,2,1:T(8,128)(2,1)S(1)} %bitcast.132, bf16[4352,256]{1,0:T(8,128)(2,1)S(1)} %bitcast.160), kind=kOutput, calls=%fused_computation.2 | convolution fusion | flops 1442773760 | bytes 24843264 | tf_op jit(solution)/shard_map/qgd,kd->gqk/dot_general | solution.py:103
  134.1 11.1 %fusion.3 = f32[5,256,128]{1,2,0:T(8,128)S(1)} fusion(f32[4352,256,5]{1,0,2:T(8,128)} %get-tuple-element.13, f32[5,256]{1,0:T(8,128)S(1)} %max.29, pred[256,4352]{0,1:T(8,128)(4,1)S(1)} %and_and_fusion, bf16[4352,256]{1,0:T(8,128)(2,1)S(1)} %bitcast.161), kind=kOutput, calls=%fused_computation.5 | convolution fusion | flops 1453916160 | bytes 25174016 | tf_op jit(solution)/shard_map/gqk,kd->gqd/dot_general | solution.py:107
  145.2 10.4 %fusion.1 = f32[5,256]{1,0:T(8,128)S(1)} fusion(f32[4352,256,5]{1,0,2:T(8,128)} %get-tuple-element.13, f32[5,256]{1,0:T(8,128)S(1)} %max.29, pred[256,4352]{0,1:T(8,128)(4,1)S(1)} %and_and_fusion), kind=kLoop, calls=%fused_computation.3 | loop fusion | flops 27851520 | bytes 23406592 | tf_op jit(solution)/shard_map/reduce_sum | solution.py:120
  156.5 1.7 fusion.8
  158.3 1.1 fusion.29
  159.4 1.1 fusion.36
  160.5 13.6 %collective-permute-start.6 = (bf16[256,640]{0,1:T(8,128)(2,1)S(1)}, bf16[256,640]{0,1:T(8,128)(2,1)S(1)}, u32[]{:S(2)}, u32[]{:S(2)}) collective-permute-start(bf16[256,640]{0,1:T(8,128)(2,1)S(1)} %bitcast.163), channel_id=1, source_target_pairs={{0,8},{8,0},{1,9},{9,1},{2,10},{10,2},{3,11},{11,3},{4,12},{12,4},... | collective-permute-start | bytes 983048 | tf_op jit(solution)/shard_map/ppermute | solution.py:144
  174.1 1.2 collective-permute-done.6
  175.3 5.6 %convolution_convert_fusion = bf16[512,2560]{0,1:T(8,128)(2,1)} fusion(bf16[640,2560]{0,1:T(8,128)(2,1)} %all-gather.2.cloned.1.call-done, bf16[256,640]{0,1:T(8,128)(2,1)S(1)} %collective-permute-done.6, bf16[256,640]{0,1:T(8,128)(2,1)S(1)} %bitcast.164), kind=kOutput, calls=%fused_computation.13 | convolution fusion | flops 1680343040 | bytes 6553600 | tf_op jit(solution)/shard_map/dot_general | solution.py:148
  181.0 78.3 %reduce-scatter.2.cloned.1.call-done = bf16[512,320]{0,1:T(8,128)(2,1)} async-done(((bf16[512,2560]{0,1:T(8,128)(2,1)}), bf16[512,320]{0,1:T(8,128)(2,1)}) %reduce-scatter.2.cloned.1.call-update) | async-done | bytes 327696 | tf_op jit(solution)/shard_map/reduce_scatter | solution.py:149
  260.2 6.5 %collective-permute-start.7 = (bf16[256,320]{0,1:T(8,128)(2,1)S(1)}, bf16[256,320]{0,1:T(8,128)(2,1)S(1)}, u32[]{:S(2)}, u32[]{:S(2)}) collective-permute-start(bf16[256,320]{0,1:T(8,128)(2,1)S(1)} %slice.89), channel_id=1, source_target_pairs={{0,8},{8,0},{1,9},{9,1},{2,10},{10,2},{3,11},{11,3},{4,12},{12,4},... | collective-permute-start | bytes 491528 | tf_op jit(solution)/shard_map/ppermute | solution.py:150
  (88 shorter events, 13.8 us)
Async XLA Ops:
  6.5 168.8 %all-gather.2.cloned.1.call-start = ((), (), s32[]{:S(2)}) async-start(), calls=%async_computation.1 | async-start | bytes 4096000 | tf_op jit(solution)/shard_map/all_gather | solution.py:147
  9.7 23.7 %collective-permute-start = (bf16[288,256]{1,0:T(8,128)(2,1)S(1)}, bf16[288,256]{1,0:T(8,128)(2,1)S(1)}, u32[]{:S(2)}, u32[]{:S(2)}) collective-permute-start(bf16[288,256]{1,0:T(8,128)(2,1)S(1)} %pad_maximum_fusion.8), channel_id=1, source_target_pairs={{496,0},{504,8},{0,16},{8,24},{16,32},{24,40},{32,48},{40,56},{48,... | collective-permute-start | bytes 442376 | tf_op jit(solution)/shard_map/ppermute | solution.py:22
  33.4 71.0 %copy-start.6 = (bf16[288,256]{1,0:T(8,128)(2,1)}, bf16[288,256]{1,0:T(8,128)(2,1)S(1)}, u32[]{:S(2)}) copy-start(bf16[288,256]{1,0:T(8,128)(2,1)S(1)} %collective-permute-done) | copy-start | bytes 442372
  33.5 13.2 %collective-permute-start.1 = (bf16[576,256]{1,0:T(8,128)(2,1)S(1)}, bf16[576,256]{1,0:T(8,128)(2,1)S(1)}, u32[]{:S(2)}, u32[]{:S(2)}) collective-permute-start(bf16[576,256]{1,0:T(8,128)(2,1)S(1)} %pad_maximum_fusion.6), channel_id=1, source_target_pairs={{504,0},{0,8},{8,16},{16,24},{24,32},{32,40},{40,48},{48,56},{56,6... | collective-permute-start | bytes 884744 | tf_op jit(solution)/shard_map/ppermute | solution.py:22
  46.7 57.7 %copy-start.4 = (bf16[64,256]{1,0:T(8,128)(2,1)}, bf16[64,256]{1,0:T(8,128)(2,1)S(1)}, u32[]{:S(2)}) copy-start(bf16[64,256]{1,0:T(8,128)(2,1)S(1)} %slice.75) | copy-start | bytes 98308
  46.8 57.0 %copy-start.9 = (s32[17]{0:T(128)S(1)}, s32[17]{0:T(128)}, u32[]{:S(2)}) copy-start(s32[17]{0:T(128)} %constant.49) | copy-start | bytes 208
  46.8 57.1 %copy-start.8 = (s32[16]{0:T(128)S(1)}, s32[16]{0:T(128)}, u32[]{:S(2)}) copy-start(s32[16]{0:T(128)} %param.14) | copy-start | bytes 196
  46.9 18.8 %collective-permute-start.2 = (bf16[1152,256]{1,0:T(8,128)(2,1)S(1)}, bf16[1152,256]{1,0:T(8,128)(2,1)S(1)}, u32[]{:S(2)}, u32[]{:S(2)}) collective-permute-start(bf16[1152,256]{1,0:T(8,128)(2,1)S(1)} %pad_maximum_fusion.2), channel_id=1, source_target_pairs={{448,0},{456,8},{464,16},{472,24},{480,32},{488,40},{496,48},{504,... | collective-permute-start | bytes 1769480 | tf_op jit(solution)/shard_map/ppermute | solution.py:22
  65.7 42.7 %copy-start.2 = (bf16[128,256]{1,0:T(8,128)(2,1)}, bf16[128,256]{1,0:T(8,128)(2,1)S(1)}, u32[]{:S(2)}) copy-start(bf16[128,256]{1,0:T(8,128)(2,1)S(1)} %slice.77) | copy-start | bytes 196612
  67.1 37.3 %collective-permute-start.3 = (bf16[2304,256]{1,0:T(8,128)(2,1)}, bf16[2304,256]{1,0:T(8,128)(2,1)S(1)}, u32[]{:S(2)}, u32[]{:S(2)}) collective-permute-start(bf16[2304,256]{1,0:T(8,128)(2,1)} %pad_maximum_fusion), channel_id=1, source_target_pairs={{480,0},{488,8},{496,16},{504,24},{0,32},{8,40},{16,48},{24,56},{3... | collective-permute-start | bytes 3538952 | tf_op jit(solution)/shard_map/ppermute | solution.py:22
  103.7 155.6 %reduce-scatter.2.cloned.1.call-start = ((), (), s32[]{:S(2)}) async-start(), calls=%async_computation.2 | async-start | bytes 2949120 | tf_op jit(solution)/shard_map/reduce_scatter | solution.py:149
  104.3 4.1 %copy-start = (bf16[256,256]{1,0:T(8,128)(2,1)}, bf16[256,256]{1,0:T(8,128)(2,1)S(1)}, u32[]{:S(2)}) copy-start(bf16[256,256]{1,0:T(8,128)(2,1)S(1)} %slice.78) | copy-start | bytes 393220
  105.2 11.5 %collective-permute-start.4 = (bf16[768,256]{1,0:T(8,128)(2,1)}, bf16[768,256]{1,0:T(8,128)(2,1)}, u32[]{:S(2)}, u32[]{:S(2)}) collective-permute-start(bf16[768,256]{1,0:T(8,128)(2,1)} %pad_maximum_fusion.4), channel_id=1, source_target_pairs={{384,0},{392,8},{400,16},{408,24},{416,32},{424,40},{432,48},{440,... | collective-permute-start | bytes 1179656 | tf_op jit(solution)/shard_map/ppermute | solution.py:22
  113.3 4.5 %copy-start.7 = (bf16[288,256]{1,0:T(8,128)(2,1)S(1)}, bf16[288,256]{1,0:T(8,128)(2,1)}, u32[]{:S(2)}) copy-start(bf16[288,256]{1,0:T(8,128)(2,1)} %copy-done.6) | copy-start | bytes 442372
  113.3 5.5 %copy-start.1 = (bf16[256,256]{1,0:T(8,128)(2,1)S(1)}, bf16[256,256]{1,0:T(8,128)(2,1)}, u32[]{:S(2)}) copy-start(bf16[256,256]{1,0:T(8,128)(2,1)} %copy-done) | copy-start | bytes 393220
  113.3 5.5 %copy-start.3 = (bf16[128,256]{1,0:T(8,128)(2,1)S(1)}, bf16[128,256]{1,0:T(8,128)(2,1)}, u32[]{:S(2)}) copy-start(bf16[128,256]{1,0:T(8,128)(2,1)} %copy-done.2) | copy-start | bytes 196612
  113.3 5.5 %copy-start.5 = (bf16[64,256]{1,0:T(8,128)(2,1)S(1)}, bf16[64,256]{1,0:T(8,128)(2,1)}, u32[]{:S(2)}) copy-start(bf16[64,256]{1,0:T(8,128)(2,1)} %copy-done.4) | copy-start | bytes 98308
  118.9 36.8 %collective-permute-start.5 = (bf16[32,32,256]{2,1,0:T(8,128)(2,1)S(1)}, bf16[32,32,256]{2,1,0:T(8,128)(2,1)S(1)}, u32[]{:S(2)}, u32[]{:S(2)}) collective-permute-start(bf16[32,32,256]{2,1,0:T(8,128)(2,1)S(1)} %constant_dynamic-update-slice_fusion.9), channel_id=1, source_target_pairs={{256,0},{264,8},{272,16},{280,24},{288,32},{296,40},{304,48},{312,... | collective-permute-start | bytes 1572872 | tf_op jit(solution)/shard_map/ppermute | solution.py:22
  160.5 14.9 %collective-permute-start.6 = (bf16[256,640]{0,1:T(8,128)(2,1)S(1)}, bf16[256,640]{0,1:T(8,128)(2,1)S(1)}, u32[]{:S(2)}, u32[]{:S(2)}) collective-permute-start(bf16[256,640]{0,1:T(8,128)(2,1)S(1)} %bitcast.163), channel_id=1, source_target_pairs={{0,8},{8,0},{1,9},{9,1},{2,10},{10,2},{3,11},{11,3},{4,12},{12,4},... | collective-permute-start | bytes 983048 | tf_op jit(solution)/shard_map/ppermute | solution.py:144
  260.2 7.5 %collective-permute-start.7 = (bf16[256,320]{0,1:T(8,128)(2,1)S(1)}, bf16[256,320]{0,1:T(8,128)(2,1)S(1)}, u32[]{:S(2)}, u32[]{:S(2)}) collective-permute-start(bf16[256,320]{0,1:T(8,128)(2,1)S(1)} %slice.89), channel_id=1, source_target_pairs={{0,8},{8,0},{1,9},{9,1},{2,10},{10,2},{3,11},{11,3},{4,12},{12,4},... | collective-permute-start | bytes 491528 | tf_op jit(solution)/shard_map/ppermute | solution.py:150
Sparse Core Ops, SparseCore 0:
  103.8 67.5 all-gather.1
  181.1 78.1 reduce-scatter.1

commit v5 on v4

--- a/solution.py
+++ b/solution.py
@@ -56,28 +56,25 @@
     prefix = jnp.concatenate((shared_prefix_keys, shared_prefix_values), axis=1)[None]
     suffix = own_kv
     reach = blocks // 4
-    shifts = [1 << k for k in range(reach.bit_length() - 1)]
-    shifts = shifts[1:2] + shifts[:1] + shifts[2:][::-1]
     distances = [0]
-    for distance in shifts:
-        got_suffix, got_prefix = shifted_pair(suffix, prefix, BLK, distance)
-        suffix = jnp.concatenate((got_suffix, suffix), axis=0)
-        prefix = jnp.concatenate((got_prefix, prefix), axis=0)
-        distances = [d + distance for d in distances] + distances
-    got_suffix, got_prefix = shifted_pair(own_kv, prefix, BLK, reach)
-    suffix = jnp.concatenate((got_suffix, suffix), axis=0)
-    prefix = jnp.concatenate((got_prefix, prefix), axis=0)
-    distances = [reach] + distances
-    early_count = prefix.shape[0]
-    distance = 2 * reach
-    while distance < blocks:
-        prefix = jnp.concatenate((shifted(prefix, BLK, distance), prefix), axis=0)
-        distance *= 2
-
+    step = 1
+    while step < reach:
+        got = [shifted_pair(suffix, prefix, BLK, step * k) for k in (1, 2, 3)]
+        suffix = jnp.concatenate([pair[0] for pair in got] + [suffix], axis=0)
+        prefix = jnp.concatenate([pair[1] for pair in got] + [prefix], axis=0)
+        distances = [d + step * k for k in (1, 2, 3) for d in distances] + distances
+        step *= 4
+    late_suffix, got_prefix = shifted_pair(own_kv, prefix, BLK, reach)
+    late_prefix = jnp.concatenate(
+        [got_prefix]
+        + [shifted(prefix, BLK, distance) for distance in range(2 * reach, blocks, reach)],
+        axis=0,
+    )
     count = suffix.shape[0]
-    suffix = suffix.reshape(count * tok_rows, 2 * width)
-    early_prefix = prefix[prefix.shape[0] - early_count:].reshape(-1, 2 * width)
-    late_prefix = prefix[: prefix.shape[0] - early_count].reshape(-1, 2 * width)
+    early_suffix = suffix.reshape(count * tok_rows, 2 * width)
+    late_suffix = late_suffix.reshape(tok_rows, 2 * width)
+    early_prefix = prefix.reshape(-1, 2 * width)
+    late_prefix = late_prefix.reshape(-1, 2 * width)
 
     req_ends = jnp.cumsum(lengths)
     local_rows = jnp.arange(tok_rows, dtype=jnp.int32)
@@ -87,14 +84,19 @@
         return jnp.sum((position[:, None] >= req_ends[None, :]).astype(jnp.int32), axis=1)
 
     query_owner = owner_of(query_pos)
-    block_of_key = my_block - jnp.repeat(jnp.array(distances, jnp.int32), tok_rows)
-    key_pos = block_of_key * tok_rows + jnp.tile(local_rows, count)
-    key_owner = owner_of(key_pos)
-    visible = (
-        (key_owner[None, :] == query_owner[:, None])
-        & (key_pos[None, :] <= query_pos[:, None])
-        & (key_pos[None, :] >= 0)
-    )
+
+    def visible_at(block_distances):
+        block_of_key = my_block - jnp.repeat(jnp.array(block_distances, jnp.int32), tok_rows)
+        key_pos = block_of_key * tok_rows + jnp.tile(local_rows, len(block_distances))
+        key_owner = owner_of(key_pos)
+        return (
+            (key_owner[None, :] == query_owner[:, None])
+            & (key_pos[None, :] <= query_pos[:, None])
+            & (key_pos[None, :] >= 0)
+        )
+
+    early_visible = visible_at(distances)
+    late_visible = visible_at([reach])
 
     heads_of_query = queries.reshape(tok_rows, kv_heads, heads_per_group, HEAD_SIZE)
 
@@ -108,24 +110,28 @@
             "gqk,kd->gqd", weights.astype(jnp.bfloat16), values, preferred_element_type=jnp.float32
         )
 
+    def piece(q, cols, vcols, prefix_rows, suffix_rows, visible):
+        pre_scores = scores_of(q, prefix_rows[:, cols])
+        suf_scores = jnp.where(visible[None], scores_of(q, suffix_rows[:, cols]), MASKED_SCORE)
+        peak = jnp.maximum(jnp.max(pre_scores, axis=-1), jnp.max(suf_scores, axis=-1))
+        pre_weights = jnp.exp(pre_scores - peak[..., None])
+        suf_weights = jnp.where(visible[None], jnp.exp(suf_scores - peak[..., None]), 0.0)
+        total = jnp.sum(pre_weights, axis=-1) + jnp.sum(suf_weights, axis=-1)
+        summed = weighted(pre_weights, prefix_rows[:, vcols]) + weighted(
+            suf_weights, suffix_rows[:, vcols]
+        )
+        return peak, total, summed
+
     def one_head(kv_head):
         cols = slice(kv_head * HEAD_SIZE, (kv_head + 1) * HEAD_SIZE)
         vcols = slice(width + kv_head * HEAD_SIZE, width + (kv_head + 1) * HEAD_SIZE)
         q = heads_of_query[:, kv_head]
-        pre_scores = scores_of(q, early_prefix[:, cols])
-        suf_scores = jnp.where(visible[None], scores_of(q, suffix[:, cols]), MASKED_SCORE)
-        first_peak = jnp.maximum(jnp.max(pre_scores, axis=-1), jnp.max(suf_scores, axis=-1))
-        pre_weights = jnp.exp(pre_scores - first_peak[..., None])
-        suf_weights = jnp.where(visible[None], jnp.exp(suf_scores - first_peak[..., None]), 0.0)
-        first_total = jnp.sum(pre_weights, axis=-1) + jnp.sum(suf_weights, axis=-1)
-        first_sum = weighted(pre_weights, early_prefix[:, vcols]) + weighted(
-            suf_weights, suffix[:, vcols]
+        first_peak, first_total, first_sum = piece(
+            q, cols, vcols, early_prefix, early_suffix, early_visible
         )
-        late_scores = scores_of(q, late_prefix[:, cols])
-        late_peak = jnp.max(late_scores, axis=-1)
-        late_weights = jnp.exp(late_scores - late_peak[..., None])
-        late_total = jnp.sum(late_weights, axis=-1)
-        late_sum = weighted(late_weights, late_prefix[:, vcols])
+        late_peak, late_total, late_sum = piece(
+            q, cols, vcols, late_prefix, late_suffix, late_visible
+        )
         peak = jnp.maximum(first_peak, late_peak)
         first_scale = jnp.exp(first_peak - peak)
         late_scale = jnp.exp(late_peak - peak)

time: 277 us -> 265 us (0.957)
  blocking collectives: 47.5 us -> 35.7 us
  waiting for transfers between devices: 94.9 us -> 104 us
  matrix products: 30 us -> 23.9 us
    ppermute x6 -> x9, waiting for transfers between devices: 14.4 us -> 32.9 us  [shifted(): return lax.ppermute(block, axis, route)]
    all_gather x2, blocking collectives: 47.5 us -> 35.7 us  [per_device(): weight = lax.all_gather(weight, name, axis=1, tiled=True)]
    ppermute x1, starting transfers between devices: 13.6 us -> 3.29 us  [per_device(): both = jnp.concatenate((attn, lax.ppermute(attn, 'core', swap)), axis=0)]
    reduce_scatter x1, waiting for transfers between devices: 78.3 us -> 68.5 us  [per_device(): lax.psum_scatter(product.astype(jnp.bfloat16), 'mp', scatter_dimension=1,...]
    ppermute x6 -> x9, starting transfers between devices: 41.8 us -> 51.4 us  [shifted(): return lax.ppermute(block, axis, route)]
    dot_general x3 -> x4, matrix products: 11 us -> 6.47 us  [scores_of(): jnp.einsum('qgd,kd->gqk', q, keys, preferred_element_type=jnp.float32)]
    reduce_sum x2 -> x4, other arithmetic: 12.1 us -> 8.14 us  [piece(): total = jnp.sum(pre_weights, axis=-1) + jnp.sum(suf_weights, axis=-1)]
    and x1 -> x2, other arithmetic: 3.7 us -> 5.6 us  [visible_at(): (key_owner[None, :] == query_owner[:, None]) & (key_pos[None, :] <= query...]
  transfers between devices with their start and end apart: 10 -> 13, of which waited for: 6 -> 6; matrix products, arithmetic and copies ran while one was open for 16% -> 14% of each run, Pallas kernels for 0% -> 0%
where the time goes in v5:
time: 265 us
  waiting for transfers between devices  104 us (39%)
  starting transfers between devices  61 us (23%)
  blocking collectives  35.7 us (13%)
  matrix products  23.9 us (9%)
  other arithmetic  18.7 us (7%)
  between operations  14 us (5%)
  local copies, waits for them, and re-layouts  7.6 us (3%)
    reduce_scatter x1, waiting for transfers between devices, per_device(): lax.psum_scatter(product.astype(jnp.bfloat16), 'mp', scatter_dimension=1,...  68.5 us
    ppermute x9, starting transfers between devices, shifted(): return lax.ppermute(block, axis, route)  51.4 us
    all_gather x2, blocking collectives, per_device(): weight = lax.all_gather(weight, name, axis=1, tiled=True)  35.7 us
    ppermute x9, waiting for transfers between devices, shifted(): return lax.ppermute(block, axis, route)  32.9 us
    dot_general x4, matrix products, weighted(): jnp.einsum('gqk,kd->gqd', weights.astype(jnp.bfloat16), values, preferred...  11.7 us
    reduce_sum x4, other arithmetic, piece(): total = jnp.sum(pre_weights, axis=-1) + jnp.sum(suf_weights, axis=-1)  8.14 us
    dot_general x4, matrix products, scores_of(): jnp.einsum('qgd,kd->gqk', q, keys, preferred_element_type=jnp.float32)  6.47 us
    ppermute x1, starting transfers between devices, per_device(): other = lax.ppermute(reduced[tok_rows:], 'core', swap)  6.28 us
  transfers between devices with their start and end apart: 13, of which 6 were waited for; matrix products, arithmetic and copies ran while one was open for 14% of the time, Pallas kernels for 0%

profile of v5, /device:TPU:1, one launch (start us, length us, event | category | flops | bytes accessed | tf_op | source)
XLA Modules:
  0.0 264.6 jit_solution(4169738815519415476)
XLA Ops:
  9.7 4.5 %collective-permute-start.2 = (bf16[288,256]{1,0:T(8,128)(2,1)S(1)}, bf16[288,256]{1,0:T(8,128)(2,1)S(1)}, u32[]{:S(2)}, u32[]{:S(2)}) collective-permute-start(bf16[288,256]{1,0:T(8,128)(2,1)S(1)} %pad_maximum_fusion.5), channel_id=1, source_target_pairs={{488,0},{496,8},{504,16},{0,24},{8,32},{16,40},{24,48},{32,56},{40... | collective-permute-start | bytes 442376 | tf_op jit(solution)/shard_map/ppermute | solution.py:22
  14.2 15.4 %collective-permute-start.1 = (bf16[288,256]{1,0:T(8,128)(2,1)S(1)}, bf16[288,256]{1,0:T(8,128)(2,1)S(1)}, u32[]{:S(2)}, u32[]{:S(2)}) collective-permute-start(bf16[288,256]{1,0:T(8,128)(2,1)S(1)} %pad_maximum_fusion.5), channel_id=1, source_target_pairs={{496,0},{504,8},{0,16},{8,24},{16,32},{24,40},{32,48},{40,56},{48,... | collective-permute-start | bytes 442376 | tf_op jit(solution)/shard_map/ppermute | solution.py:22
  29.7 11.8 %collective-permute-start = (bf16[288,256]{1,0:T(8,128)(2,1)S(1)}, bf16[288,256]{1,0:T(8,128)(2,1)S(1)}, u32[]{:S(2)}, u32[]{:S(2)}) collective-permute-start(bf16[288,256]{1,0:T(8,128)(2,1)S(1)} %pad_maximum_fusion.5), channel_id=1, source_target_pairs={{504,0},{0,8},{8,16},{16,24},{24,32},{32,40},{40,48},{48,56},{56,6... | collective-permute-start | bytes 442376 | tf_op jit(solution)/shard_map/ppermute | solution.py:22
  41.5 23.1 %all_gather.9 = bf16[640,160]{0,1:T(8,128)(2,1)S(1)} all-gather(bf16[640,80]{0,1:T(8,128)(2,1)} %param.14), channel_id=1, replica_groups=mesh['y'=4,'x'=4,'zh'=2,'core'=2,'mp'=8] {'zh'}, dimensions={1}, use_global_device_ids=true | all-gather | bytes 307200 | tf_op jit(solution)/shard_map/all_gather | solution.py:153
  64.6 12.6 %all_gather.10 = bf16[640,640]{0,1:T(8,128)(2,1)} all-gather(bf16[640,160]{0,1:T(8,128)(2,1)S(1)} %all_gather.9), channel_id=1, replica_groups=mesh['y'=4,'x'=4,'zh'=2,'core'=2,'mp'=8] {'x'}, dimensions={1}, use_global_device_ids=true | all-gather | bytes 1024000 | tf_op jit(solution)/shard_map/all_gather | solution.py:153
  78.9 4.6 %collective-permute-start.5 = (bf16[1152,256]{1,0:T(8,128)(2,1)}, bf16[1152,256]{1,0:T(8,128)(2,1)S(1)}, u32[]{:S(2)}, u32[]{:S(2)}) collective-permute-start(bf16[1152,256]{1,0:T(8,128)(2,1)} %pad_maximum_fusion.1), channel_id=1, source_target_pairs={{416,0},{424,8},{432,16},{440,24},{448,32},{456,40},{464,48},{472,... | collective-permute-start | bytes 1769480 | tf_op jit(solution)/shard_map/ppermute | solution.py:22
  83.5 3.5 %collective-permute-start.4 = (bf16[1152,256]{1,0:T(8,128)(2,1)}, bf16[1152,256]{1,0:T(8,128)(2,1)S(1)}, u32[]{:S(2)}, u32[]{:S(2)}) collective-permute-start(bf16[1152,256]{1,0:T(8,128)(2,1)} %pad_maximum_fusion.1), channel_id=1, source_target_pairs={{448,0},{456,8},{464,16},{472,24},{480,32},{488,40},{496,48},{504,... | collective-permute-start | bytes 1769480 | tf_op jit(solution)/shard_map/ppermute | solution.py:22
  87.0 1.9 collective-permute-start.3
  89.0 4.8 %and_and_fusion = pred[256,4096]{0,1:T(8,128)(4,1)} fusion(s32[256]{0:T(256)S(1)} %iota_add_fusion.1, s32[256]{0:T(256)S(1)} %get-tuple-element.6, s32[4096]{0:T(1024)S(1)} %bitcast.153, s32[4096]{0:T(1024)S(1)} %convert_reduce_fusion, pred[4096]{0:T(1024)(128)(4,1)S(1)} %broadcast_compare_fusion), kind=kLoop, calls=%fused_computation.13 | loop fusion | flops 4194304 | bytes 1087488 | tf_op jit(solution)/shard_map/and | solution.py:93
  94.8 15.3 %collective-permute-done.4 = bf16[1152,256]{1,0:T(8,128)(2,1)S(1)} collective-permute-done((bf16[1152,256]{1,0:T(8,128)(2,1)}, bf16[1152,256]{1,0:T(8,128)(2,1)S(1)}, u32[]{:S(2)}, u32[]{:S(2)}) %collective-permute-start.4) | collective-permute-done | bytes 589856 | tf_op jit(solution)/shard_map/ppermute | solution.py:22
  110.1 13.8 %collective-permute-done.3 = bf16[1152,256]{1,0:T(8,128)(2,1)S(1)} collective-permute-done((bf16[1152,256]{1,0:T(8,128)(2,1)}, bf16[1152,256]{1,0:T(8,128)(2,1)S(1)}, u32[]{:S(2)}, u32[]{:S(2)}) %collective-permute-start.3) | collective-permute-done | bytes 589856 | tf_op jit(solution)/shard_map/ppermute | solution.py:22
  124.0 5.1 %collective-permute-start.8 = (bf16[16,32,256]{2,1,0:T(8,128)(2,1)S(1)}, bf16[16,32,256]{2,1,0:T(8,128)(2,1)}, u32[]{:S(2)}, u32[]{:S(2)}) collective-permute-start(bf16[16,32,256]{2,1,0:T(8,128)(2,1)S(1)} %constant_dynamic-update-slice_fusion.4), channel_id=1, source_target_pairs={{128,0},{136,8},{144,16},{152,24},{160,32},{168,40},{176,48},{184,... | collective-permute-start | bytes 786440 | tf_op jit(solution)/shard_map/ppermute | solution.py:22
  129.1 1.9 collective-permute-start.7
  131.9 2.7 %collective-permute-start.6 = (bf16[768,256]{1,0:T(8,128)(2,1)}, bf16[768,256]{1,0:T(8,128)(2,1)}, u32[]{:S(2)}, u32[]{:S(2)}) collective-permute-start(bf16[768,256]{1,0:T(8,128)(2,1)} %pad_maximum_fusion.3), channel_id=1, source_target_pairs={{384,0},{392,8},{400,16},{408,24},{416,32},{424,40},{432,48},{440,... | collective-permute-start | bytes 1179656 | tf_op jit(solution)/shard_map/ppermute | solution.py:22
  136.4 3.6 %fusion = (f32[5,256]{1,0:T(8,128)S(1)}, f32[4096,256,5]{1,0,2:T(8,128)S(1)}) fusion(pred[256,4096]{0,1:T(8,128)(4,1)S(1)} %copy-done, bf16[256,5,128]{0,2,1:T(8,128)(2,1)S(1)} %bitcast.134, bf16[4096,256]{1,0:T(8,128)(2,1)S(1)} %bitcast.159), kind=kOutput, calls=%fused_computation.2 | convolution fusion | flops 1357904640 | bytes 23401472 | tf_op jit(solution)/shard_map/qgd,kd->gqk/dot_general | solution.py:105
  140.6 8.3 %fusion.3 = f32[5,256,128]{1,2,0:T(8,128)} fusion(f32[4096,256,5]{1,0,2:T(8,128)S(1)} %get-tuple-element.15, f32[5,256]{1,0:T(8,128)} %max.45, pred[256,4096]{0,1:T(8,128)(4,1)} %and_and_fusion, bf16[4096,256]{1,0:T(8,128)(2,1)} %bitcast.160), kind=kOutput, calls=%fused_computation.5 | convolution fusion | flops 1368391680 | bytes 23732224 | tf_op jit(solution)/shard_map/gqk,kd->gqd/dot_general | solution.py:109
  148.9 6.2 %fusion.1 = f32[5,256]{1,0:T(8,128)S(1)} fusion(f32[4096,256,5]{1,0,2:T(8,128)S(1)} %get-tuple-element.15, f32[5,256]{1,0:T(8,128)} %max.45, pred[256,4096]{0,1:T(8,128)(4,1)} %and_and_fusion), kind=kLoop, calls=%fused_computation.3 | loop fusion | flops 26213120 | bytes 22030336 | tf_op jit(solution)/shard_map/reduce_sum | solution.py:119
  155.6 3.8 %collective-permute-done.6 = bf16[768,256]{1,0:T(8,128)(2,1)} collective-permute-done((bf16[768,256]{1,0:T(8,128)(2,1)}, bf16[768,256]{1,0:T(8,128)(2,1)}, u32[]{:S(2)}, u32[]{:S(2)}) %collective-permute-start.6) | collective-permute-done | bytes 393248 | tf_op jit(solution)/shard_map/ppermute | solution.py:22
  164.1 1.3 fusion.7
  166.1 1.6 fusion.9
  168.9 3.3 %collective-permute-start.9 = (bf16[256,640]{0,1:T(8,128)(2,1)S(1)}, bf16[256,640]{0,1:T(8,128)(2,1)S(1)}, u32[]{:S(2)}, u32[]{:S(2)}) collective-permute-start(bf16[256,640]{0,1:T(8,128)(2,1)S(1)} %bitcast.162), channel_id=1, source_target_pairs={{0,8},{8,0},{1,9},{9,1},{2,10},{10,2},{3,11},{11,3},{4,12},{12,4},... | collective-permute-start | bytes 983048 | tf_op jit(solution)/shard_map/ppermute | solution.py:150
  173.4 5.7 %convolution_convert_fusion = bf16[512,2560]{0,1:T(8,128)(2,1)} fusion(bf16[640,2560]{0,1:T(8,128)(2,1)} %all-gather.2.cloned.1.call-done, bf16[256,640]{0,1:T(8,128)(2,1)S(1)} %collective-permute-done.9, bf16[256,640]{0,1:T(8,128)(2,1)S(1)} %bitcast.163), kind=kOutput, calls=%fused_computation.12 | convolution fusion | flops 1680343040 | bytes 6553600 | tf_op jit(solution)/shard_map/dot_general | solution.py:154
  179.1 68.5 %reduce-scatter.2.cloned.1.call-done = bf16[512,320]{0,1:T(8,128)(2,1)} async-done(((bf16[512,2560]{0,1:T(8,128)(2,1)}), bf16[512,320]{0,1:T(8,128)(2,1)}) %reduce-scatter.2.cloned.1.call-update) | async-done | bytes 327696 | tf_op jit(solution)/shard_map/reduce_scatter | solution.py:155
  248.5 6.3 %collective-permute-start.10 = (bf16[256,320]{0,1:T(8,128)(2,1)S(1)}, bf16[256,320]{0,1:T(8,128)(2,1)S(1)}, u32[]{:S(2)}, u32[]{:S(2)}) collective-permute-start(bf16[256,320]{0,1:T(8,128)(2,1)S(1)} %slice.117), channel_id=1, source_target_pairs={{0,8},{8,0},{1,9},{9,1},{2,10},{10,2},{3,11},{11,3},{4,12},{12,4},... | collective-permute-start | bytes 491528 | tf_op jit(solution)/shard_map/ppermute | solution.py:156
  (94 shorter events, 21.1 us)
Async XLA Ops:
  6.5 70.7 %copy-start.7 = (s32[16]{0:T(128)S(1)}, s32[16]{0:T(128)}, u32[]{:S(2)}) copy-start(s32[16]{0:T(128)} %constant.56) | copy-start | bytes 196
  6.5 70.7 %copy-start.6 = (s32[16]{0:T(128)S(1)}, s32[16]{0:T(128)}, u32[]{:S(2)}) copy-start(s32[16]{0:T(128)} %param.15) | copy-start | bytes 196
  6.5 166.9 %all-gather.2.cloned.1.call-start = ((), (), s32[]{:S(2)}) async-start(), calls=%async_computation.1 | async-start | bytes 4096000 | tf_op jit(solution)/shard_map/all_gather | solution.py:153
  9.7 68.1 %collective-permute-start.2 = (bf16[288,256]{1,0:T(8,128)(2,1)S(1)}, bf16[288,256]{1,0:T(8,128)(2,1)S(1)}, u32[]{:S(2)}, u32[]{:S(2)}) collective-permute-start(bf16[288,256]{1,0:T(8,128)(2,1)S(1)} %pad_maximum_fusion.5), channel_id=1, source_target_pairs={{488,0},{496,8},{504,16},{0,24},{8,32},{16,40},{24,48},{32,56},{40... | collective-permute-start | bytes 442376 | tf_op jit(solution)/shard_map/ppermute | solution.py:22
  14.2 63.7 %collective-permute-start.1 = (bf16[288,256]{1,0:T(8,128)(2,1)S(1)}, bf16[288,256]{1,0:T(8,128)(2,1)S(1)}, u32[]{:S(2)}, u32[]{:S(2)}) collective-permute-start(bf16[288,256]{1,0:T(8,128)(2,1)S(1)} %pad_maximum_fusion.5), channel_id=1, source_target_pairs={{496,0},{504,8},{0,16},{8,24},{16,32},{24,40},{32,48},{40,56},{48,... | collective-permute-start | bytes 442376 | tf_op jit(solution)/shard_map/ppermute | solution.py:22
  29.7 48.2 %collective-permute-start = (bf16[288,256]{1,0:T(8,128)(2,1)S(1)}, bf16[288,256]{1,0:T(8,128)(2,1)S(1)}, u32[]{:S(2)}, u32[]{:S(2)}) collective-permute-start(bf16[288,256]{1,0:T(8,128)(2,1)S(1)} %pad_maximum_fusion.5), channel_id=1, source_target_pairs={{504,0},{0,8},{8,16},{16,24},{24,32},{32,40},{40,48},{48,56},{56,6... | collective-permute-start | bytes 442376 | tf_op jit(solution)/shard_map/ppermute | solution.py:22
  77.1 16.6 %copy-start.3 = (bf16[256,640]{1,0:T(8,128)(2,1)S(1)}, bf16[256,640]{1,0:T(8,128)(2,1)}, u32[]{:S(2)}) copy-start(bf16[256,640]{1,0:T(8,128)(2,1)} %param.9) | copy-start | bytes 983044
  77.2 170.4 %reduce-scatter.2.cloned.1.call-start = ((), (), s32[]{:S(2)}) async-start(), calls=%async_computation.2 | async-start | bytes 2949120 | tf_op jit(solution)/shard_map/reduce_scatter | solution.py:155
  78.9 45.0 %collective-permute-start.5 = (bf16[1152,256]{1,0:T(8,128)(2,1)}, bf16[1152,256]{1,0:T(8,128)(2,1)S(1)}, u32[]{:S(2)}, u32[]{:S(2)}) collective-permute-start(bf16[1152,256]{1,0:T(8,128)(2,1)} %pad_maximum_fusion.1), channel_id=1, source_target_pairs={{416,0},{424,8},{432,16},{440,24},{448,32},{456,40},{464,48},{472,... | collective-permute-start | bytes 1769480 | tf_op jit(solution)/shard_map/ppermute | solution.py:22
  83.5 26.5 %collective-permute-start.4 = (bf16[1152,256]{1,0:T(8,128)(2,1)}, bf16[1152,256]{1,0:T(8,128)(2,1)S(1)}, u32[]{:S(2)}, u32[]{:S(2)}) collective-permute-start(bf16[1152,256]{1,0:T(8,128)(2,1)} %pad_maximum_fusion.1), channel_id=1, source_target_pairs={{448,0},{456,8},{464,16},{472,24},{480,32},{488,40},{496,48},{504,... | collective-permute-start | bytes 1769480 | tf_op jit(solution)/shard_map/ppermute | solution.py:22
  87.0 36.9 %collective-permute-start.3 = (bf16[1152,256]{1,0:T(8,128)(2,1)}, bf16[1152,256]{1,0:T(8,128)(2,1)S(1)}, u32[]{:S(2)}, u32[]{:S(2)}) collective-permute-start(bf16[1152,256]{1,0:T(8,128)(2,1)} %pad_maximum_fusion.1), channel_id=1, source_target_pairs={{480,0},{488,8},{496,16},{504,24},{0,32},{8,40},{16,48},{24,56},{3... | collective-permute-start | bytes 1769480 | tf_op jit(solution)/shard_map/ppermute | solution.py:22
  124.0 36.3 %collective-permute-start.8 = (bf16[16,32,256]{2,1,0:T(8,128)(2,1)S(1)}, bf16[16,32,256]{2,1,0:T(8,128)(2,1)}, u32[]{:S(2)}, u32[]{:S(2)}) collective-permute-start(bf16[16,32,256]{2,1,0:T(8,128)(2,1)S(1)} %constant_dynamic-update-slice_fusion.4), channel_id=1, source_target_pairs={{128,0},{136,8},{144,16},{152,24},{160,32},{168,40},{176,48},{184,... | collective-permute-start | bytes 786440 | tf_op jit(solution)/shard_map/ppermute | solution.py:22
  129.1 31.2 %collective-permute-start.7 = (bf16[16,32,256]{2,1,0:T(8,128)(2,1)S(1)}, bf16[16,32,256]{2,1,0:T(8,128)(2,1)}, u32[]{:S(2)}, u32[]{:S(2)}) collective-permute-start(bf16[16,32,256]{2,1,0:T(8,128)(2,1)S(1)} %constant_dynamic-update-slice_fusion.4), channel_id=1, source_target_pairs={{256,0},{264,8},{272,16},{280,24},{288,32},{296,40},{304,48},{312,... | collective-permute-start | bytes 786440 | tf_op jit(solution)/shard_map/ppermute | solution.py:22
  131.9 27.5 %collective-permute-start.6 = (bf16[768,256]{1,0:T(8,128)(2,1)}, bf16[768,256]{1,0:T(8,128)(2,1)}, u32[]{:S(2)}, u32[]{:S(2)}) collective-permute-start(bf16[768,256]{1,0:T(8,128)(2,1)} %pad_maximum_fusion.3), channel_id=1, source_target_pairs={{384,0},{392,8},{400,16},{408,24},{416,32},{424,40},{432,48},{440,... | collective-permute-start | bytes 1179656 | tf_op jit(solution)/shard_map/ppermute | solution.py:22
  134.7 1.7 copy-start
  134.9 5.1 %copy-start.5 = (bf16[16,256,256]{2,1,0:T(8,128)(2,1)}, bf16[16,256,256]{2,1,0:T(8,128)(2,1)S(1)}, u32[]{:S(2)}) copy-start(bf16[16,256,256]{2,1,0:T(8,128)(2,1)S(1)} %constant_dynamic-update-slice_fusion.11) | copy-start | bytes 6291460
  148.9 6.2 %copy-start.4 = (f32[5,256]{1,0:T(8,128)S(1)}, f32[5,256]{1,0:T(8,128)}, u32[]{:S(2)}) copy-start(f32[5,256]{1,0:T(8,128)} %max.45) | copy-start | bytes 15364
  155.1 6.3 %copy-start.2 = (pred[256,256]{0,1:T(8,128)(4,1)S(1)}, pred[256,256]{0,1:T(8,128)(4,1)}, u32[]{:S(2)}) copy-start(pred[256,256]{0,1:T(8,128)(4,1)} %and_and_fusion.1) | copy-start | bytes 196612
  164.1 1.3 copy-start.1
  168.9 4.5 %collective-permute-start.9 = (bf16[256,640]{0,1:T(8,128)(2,1)S(1)}, bf16[256,640]{0,1:T(8,128)(2,1)S(1)}, u32[]{:S(2)}, u32[]{:S(2)}) collective-permute-start(bf16[256,640]{0,1:T(8,128)(2,1)S(1)} %bitcast.162), channel_id=1, source_target_pairs={{0,8},{8,0},{1,9},{9,1},{2,10},{10,2},{3,11},{11,3},{4,12},{12,4},... | collective-permute-start | bytes 983048 | tf_op jit(solution)/shard_map/ppermute | solution.py:150
  248.5 7.3 %collective-permute-start.10 = (bf16[256,320]{0,1:T(8,128)(2,1)S(1)}, bf16[256,320]{0,1:T(8,128)(2,1)S(1)}, u32[]{:S(2)}, u32[]{:S(2)}) collective-permute-start(bf16[256,320]{0,1:T(8,128)(2,1)S(1)} %slice.117), channel_id=1, source_target_pairs={{0,8},{8,0},{1,9},{9,1},{2,10},{10,2},{3,11},{11,3},{4,12},{12,4},... | collective-permute-start | bytes 491528 | tf_op jit(solution)/shard_map/ppermute | solution.py:156
Sparse Core Ops, SparseCore 0:
  77.3 87.2 all-gather.1
  179.2 68.3 reduce-scatter.1

commit v6 on v5

--- a/solution.py
+++ b/solution.py
@@ -148,9 +148,21 @@
     swap = [(0, 1), (1, 0)]
     core = lax.axis_index("core")
     both = jnp.concatenate((attn, lax.ppermute(attn, "core", swap)), axis=0)
-    weight = out_weight
-    for name in BLK[-2::-1]:
-        weight = lax.all_gather(weight, name, axis=1, tiled=True)
+    z_hi = lax.axis_index(BLK[2])
+    partner = lax.ppermute(out_weight, BLK[2], swap)
+    pair = jnp.where(
+        z_hi == 0,
+        jnp.concatenate((out_weight, partner), axis=1),
+        jnp.concatenate((partner, out_weight), axis=1),
+    )
+    across = dict(BLK_PARTS)[BLK[1]]
+    from_behind = [pair] + [
+        lax.ppermute(pair, BLK[1], [((i - k) % across, i) for i in range(across)])
+        for k in range(1, across)
+    ]
+    in_order = jnp.roll(jnp.stack(from_behind[::-1]), lax.axis_index(BLK[1]) + 1, axis=0)
+    row = jnp.moveaxis(in_order, 0, 1).reshape(out_weight.shape[0], -1)
+    weight = lax.all_gather(row, BLK[0], axis=1, tiled=True)
     product = jnp.dot(both, weight, preferred_element_type=jnp.float32)
     reduced = lax.psum_scatter(product.astype(jnp.bfloat16), "mp", scatter_dimension=1, tiled=True)
     other = lax.ppermute(reduced[tok_rows:], "core", swap)

time: 265 us -> 263 us (level)
  blocking collectives: 35.7 us -> 0 us
  waiting for transfers between devices: 104 us -> 120 us
  starting transfers between devices: 61 us -> 70.9 us
  local copies, waits for them, and re-layouts: 7.6 us -> 13.2 us
    all_gather x2 -> x0, blocking collectives: 35.7 us -> none  [per_device(): weight = lax.all_gather(weight, name, axis=1, tiled=True)]
    ppermute x0 -> x4, starting transfers between devices: none -> 13.4 us  [the longest x3 11.2 us: per_device(): lax.ppermute(pair, BLK[1], [((i - k) % across, i) for i in range(across)])]
    ppermute x0 -> x4, waiting for transfers between devices: none -> 12.2 us  [the longest x1 12.2 us: per_device(): partner = lax.ppermute(out_weight, BLK[2], swap)]
    ppermute x9, waiting for transfers between devices: 32.9 us -> 37.3 us  [shifted(): return lax.ppermute(block, axis, route)]
  transfers between devices with their start and end apart: 13 -> 17, of which waited for: 6 -> 7; matrix products, arithmetic and copies ran while one was open for 14% -> 17% of each run, Pallas kernels for 0% -> 0%
where the time goes in v6:
time: 263 us; the launch traced here: 262 us
  waiting for transfers between devices  120 us (46%)
  starting transfers between devices  70.9 us (27%)
  matrix products  23.9 us (9%)
  other arithmetic  19.5 us (7%)
  between operations  14.1 us (5%)
  local copies, waits for them, and re-layouts  13.2 us (5%)
    reduce_scatter x1, waiting for transfers between devices, per_device(): lax.psum_scatter(product.astype(jnp.bfloat16), 'mp', scatter_dimension=1,...  68.3 us
    ppermute x9, starting transfers between devices, shifted(): return lax.ppermute(block, axis, route)  48.8 us
    ppermute x9, waiting for transfers between devices, shifted(): return lax.ppermute(block, axis, route)  37.3 us
    ppermute x1, waiting for transfers between devices, per_device(): partner = lax.ppermute(out_weight, BLK[2], swap)  12.2 us
    dot_general x4, matrix products, weighted(): jnp.einsum('gqk,kd->gqd', weights.astype(jnp.bfloat16), values, preferred...  11.7 us
    ppermute x3, starting transfers between devices, per_device(): lax.ppermute(pair, BLK[1], [((i - k) % across, i) for i in range(across)])  11.2 us
    reduce_sum x4, other arithmetic, piece(): total = jnp.sum(pre_weights, axis=-1) + jnp.sum(suf_weights, axis=-1)  8.14 us
    dot_general x4, matrix products, scores_of(): jnp.einsum('qgd,kd->gqk', q, keys, preferred_element_type=jnp.float32)  6.48 us
  transfers between devices with their start and end apart: 17, of which 7 were waited for; matrix products, arithmetic and copies ran while one was open for 17% of the time, Pallas kernels for 0%

profile of v6, /device:TPU:1, one launch (start us, length us, event | category | flops | bytes accessed | tf_op | source)
XLA Modules:
  0.0 261.7 jit_solution(4736073166537562170)
XLA Ops:
  9.7 4.5 %collective-permute-start.2 = (bf16[288,256]{1,0:T(8,128)(2,1)S(1)}, bf16[288,256]{1,0:T(8,128)(2,1)S(1)}, u32[]{:S(2)}, u32[]{:S(2)}) collective-permute-start(bf16[288,256]{1,0:T(8,128)(2,1)S(1)} %pad_maximum_fusion.5), channel_id=1, source_target_pairs={{488,0},{496,8},{504,16},{0,24},{8,32},{16,40},{24,48},{32,56},{40... | collective-permute-start | bytes 442376 | tf_op jit(solution)/shard_map/ppermute | solution.py:22
  14.2 15.4 %collective-permute-start.1 = (bf16[288,256]{1,0:T(8,128)(2,1)S(1)}, bf16[288,256]{1,0:T(8,128)(2,1)S(1)}, u32[]{:S(2)}, u32[]{:S(2)}) collective-permute-start(bf16[288,256]{1,0:T(8,128)(2,1)S(1)} %pad_maximum_fusion.5), channel_id=1, source_target_pairs={{496,0},{504,8},{0,16},{8,24},{16,32},{24,40},{32,48},{40,56},{48,... | collective-permute-start | bytes 442376 | tf_op jit(solution)/shard_map/ppermute | solution.py:22
  29.7 11.8 %collective-permute-start = (bf16[288,256]{1,0:T(8,128)(2,1)S(1)}, bf16[288,256]{1,0:T(8,128)(2,1)S(1)}, u32[]{:S(2)}, u32[]{:S(2)}) collective-permute-start(bf16[288,256]{1,0:T(8,128)(2,1)S(1)} %pad_maximum_fusion.5), channel_id=1, source_target_pairs={{504,0},{0,8},{8,16},{16,24},{24,32},{32,40},{40,48},{48,56},{56,6... | collective-permute-start | bytes 442376 | tf_op jit(solution)/shard_map/ppermute | solution.py:22
  41.5 2.2 collective-permute-start.10
  45.6 4.8 %and_and_fusion = pred[256,4096]{0,1:T(8,128)(4,1)} fusion(s32[256]{0:T(256)S(1)} %iota_add_fusion.1, s32[256]{0:T(256)S(1)} %get-tuple-element.6, s32[4096]{0:T(1024)S(1)} %bitcast.172, s32[4096]{0:T(1024)S(1)} %convert_reduce_fusion, pred[4096]{0:T(1024)(128)(4,1)S(1)} %broadcast_compare_fusion), kind=kLoop, calls=%fused_computation.13 | loop fusion | flops 4194304 | bytes 1087488 | tf_op jit(solution)/shard_map/and | solution.py:93
  52.4 12.2 %collective-permute-done.10 = bf16[640,80]{0,1:T(8,128)(2,1)S(1)} collective-permute-done((bf16[640,80]{0,1:T(8,128)(2,1)}, bf16[640,80]{0,1:T(8,128)(2,1)S(1)}, u32[]{:S(2)}, u32[]{:S(2)}) %collective-permute-start.10) | collective-permute-done | bytes 102432 | tf_op jit(solution)/shard_map/ppermute | solution.py:152
  64.6 2.9 %collective-permute-start.13 = (bf16[640,160]{0,1:T(8,128)(2,1)S(1)}, bf16[640,160]{0,1:T(8,128)(2,1)S(1)}, u32[]{:S(2)}, u32[]{:S(2)}) collective-permute-start(bf16[640,160]{0,1:T(8,128)(2,1)S(1)} %maximum_select_fusion), channel_id=1, source_target_pairs={{96,0},{0,32},{32,64},{64,96},{97,1},{1,33},{33,65},{65,97},{98,2}... | collective-permute-start | bytes 614408 | tf_op jit(solution)/shard_map/ppermute | solution.py:160
  67.5 4.4 %collective-permute-start.12 = (bf16[640,160]{0,1:T(8,128)(2,1)S(1)}, bf16[640,160]{0,1:T(8,128)(2,1)S(1)}, u32[]{:S(2)}, u32[]{:S(2)}) collective-permute-start(bf16[640,160]{0,1:T(8,128)(2,1)S(1)} %maximum_select_fusion), channel_id=1, source_target_pairs={{64,0},{96,32},{0,64},{32,96},{65,1},{97,33},{1,65},{33,97},{66,2}... | collective-permute-start | bytes 614408 | tf_op jit(solution)/shard_map/ppermute | solution.py:160
  71.9 4.0 %collective-permute-start.11 = (bf16[640,160]{0,1:T(8,128)(2,1)S(1)}, bf16[640,160]{0,1:T(8,128)(2,1)S(1)}, u32[]{:S(2)}, u32[]{:S(2)}) collective-permute-start(bf16[640,160]{0,1:T(8,128)(2,1)S(1)} %maximum_select_fusion), channel_id=1, source_target_pairs={{32,0},{64,32},{96,64},{0,96},{33,1},{65,33},{97,65},{1,97},{34,2}... | collective-permute-start | bytes 614408 | tf_op jit(solution)/shard_map/ppermute | solution.py:160
  79.4 4.1 %collective-permute-start.4 = (bf16[1152,256]{1,0:T(8,128)(2,1)}, bf16[1152,256]{1,0:T(8,128)(2,1)S(1)}, u32[]{:S(2)}, u32[]{:S(2)}) collective-permute-start(bf16[1152,256]{1,0:T(8,128)(2,1)} %pad_maximum_fusion.1), channel_id=1, source_target_pairs={{448,0},{456,8},{464,16},{472,24},{480,32},{488,40},{496,48},{504,... | collective-permute-start | bytes 1769480 | tf_op jit(solution)/shard_map/ppermute | solution.py:22
  83.6 2.2 collective-permute-start.3
  87.2 19.9 %collective-permute-done.4 = bf16[1152,256]{1,0:T(8,128)(2,1)S(1)} collective-permute-done((bf16[1152,256]{1,0:T(8,128)(2,1)}, bf16[1152,256]{1,0:T(8,128)(2,1)S(1)}, u32[]{:S(2)}, u32[]{:S(2)}) %collective-permute-start.4) | collective-permute-done | bytes 589856 | tf_op jit(solution)/shard_map/ppermute | solution.py:22
  107.1 14.4 %collective-permute-done.3 = bf16[1152,256]{1,0:T(8,128)(2,1)} collective-permute-done((bf16[1152,256]{1,0:T(8,128)(2,1)}, bf16[1152,256]{1,0:T(8,128)(2,1)}, u32[]{:S(2)}, u32[]{:S(2)}) %collective-permute-start.3) | collective-permute-done | bytes 589856 | tf_op jit(solution)/shard_map/ppermute | solution.py:22
  123.1 4.3 %collective-permute-start.8 = (bf16[16,32,256]{2,1,0:T(8,128)(2,1)S(1)}, bf16[16,32,256]{2,1,0:T(8,128)(2,1)}, u32[]{:S(2)}, u32[]{:S(2)}) collective-permute-start(bf16[16,32,256]{2,1,0:T(8,128)(2,1)S(1)} %constant_dynamic-update-slice_fusion.6), channel_id=1, source_target_pairs={{128,0},{136,8},{144,16},{152,24},{160,32},{168,40},{176,48},{184,... | collective-permute-start | bytes 786440 | tf_op jit(solution)/shard_map/ppermute | solution.py:22
  127.3 1.9 collective-permute-start.7
  130.1 2.7 %collective-permute-start.6 = (bf16[768,256]{1,0:T(8,128)(2,1)}, bf16[768,256]{1,0:T(8,128)(2,1)}, u32[]{:S(2)}, u32[]{:S(2)}) collective-permute-start(bf16[768,256]{1,0:T(8,128)(2,1)} %pad_maximum_fusion.3), channel_id=1, source_target_pairs={{384,0},{392,8},{400,16},{408,24},{416,32},{424,40},{432,48},{440,... | collective-permute-start | bytes 1179656 | tf_op jit(solution)/shard_map/ppermute | solution.py:22
  135.3 3.6 %fusion = (f32[5,256]{1,0:T(8,128)S(1)}, f32[4096,256,5]{1,0,2:T(8,128)S(1)}) fusion(pred[256,4096]{0,1:T(8,128)(4,1)S(1)} %copy-done, bf16[256,5,128]{0,2,1:T(8,128)(2,1)S(1)} %bitcast.148, bf16[4096,256]{1,0:T(8,128)(2,1)S(1)} %bitcast.178), kind=kOutput, calls=%fused_computation.2 | convolution fusion | flops 1357904640 | bytes 23401472 | tf_op jit(solution)/shard_map/qgd,kd->gqk/dot_general | solution.py:105
  139.6 8.3 %fusion.3 = f32[5,256,128]{1,2,0:T(8,128)} fusion(f32[4096,256,5]{1,0,2:T(8,128)S(1)} %get-tuple-element.15, f32[5,256]{1,0:T(8,128)} %max.45, pred[256,4096]{0,1:T(8,128)(4,1)} %and_and_fusion, bf16[4096,256]{1,0:T(8,128)(2,1)} %bitcast.179), kind=kOutput, calls=%fused_computation.5 | convolution fusion | flops 1368391680 | bytes 23732224 | tf_op jit(solution)/shard_map/gqk,kd->gqd/dot_general | solution.py:109
  147.9 6.2 %fusion.1 = f32[5,256]{1,0:T(8,128)S(1)} fusion(f32[4096,256,5]{1,0,2:T(8,128)S(1)} %get-tuple-element.15, f32[5,256]{1,0:T(8,128)} %max.45, pred[256,4096]{0,1:T(8,128)(4,1)} %and_and_fusion), kind=kLoop, calls=%fused_computation.3 | loop fusion | flops 26213120 | bytes 22030336 | tf_op jit(solution)/shard_map/reduce_sum | solution.py:119
  154.6 3.1 %collective-permute-done.6 = bf16[768,256]{1,0:T(8,128)(2,1)} collective-permute-done((bf16[768,256]{1,0:T(8,128)(2,1)}, bf16[768,256]{1,0:T(8,128)(2,1)}, u32[]{:S(2)}, u32[]{:S(2)}) %collective-permute-start.6) | collective-permute-done | bytes 393248 | tf_op jit(solution)/shard_map/ppermute | solution.py:22
  167.1 3.2 %collective-permute-start.9 = (bf16[256,640]{0,1:T(8,128)(2,1)S(1)}, bf16[256,640]{0,1:T(8,128)(2,1)S(1)}, u32[]{:S(2)}, u32[]{:S(2)}) collective-permute-start(bf16[256,640]{0,1:T(8,128)(2,1)S(1)} %bitcast.181), channel_id=1, source_target_pairs={{0,8},{8,0},{1,9},{9,1},{2,10},{10,2},{3,11},{11,3},{4,12},{12,4},... | collective-permute-start | bytes 983048 | tf_op jit(solution)/shard_map/ppermute | solution.py:150
  171.6 5.7 %convolution_convert_fusion = bf16[512,2560]{0,1:T(8,128)(2,1)} fusion(bf16[640,2560]{0,1:T(8,128)(2,1)} %all-gather.2.cloned.1.call-done, bf16[256,640]{0,1:T(8,128)(2,1)S(1)} %collective-permute-done.9, bf16[256,640]{0,1:T(8,128)(2,1)S(1)} %bitcast.182), kind=kOutput, calls=%fused_computation.12 | convolution fusion | flops 1680343040 | bytes 6553600 | tf_op jit(solution)/shard_map/dot_general | solution.py:166
  177.3 68.3 %reduce-scatter.2.cloned.1.call-done = bf16[512,320]{0,1:T(8,128)(2,1)} async-done(((bf16[512,2560]{0,1:T(8,128)(2,1)}), bf16[512,320]{0,1:T(8,128)(2,1)}) %reduce-scatter.2.cloned.1.call-update) | async-done | bytes 327696 | tf_op jit(solution)/shard_map/reduce_scatter | solution.py:167
  246.5 5.4 %collective-permute-start.14 = (bf16[256,320]{0,1:T(8,128)(2,1)S(1)}, bf16[256,320]{0,1:T(8,128)(2,1)S(1)}, u32[]{:S(2)}, u32[]{:S(2)}) collective-permute-start(bf16[256,320]{0,1:T(8,128)(2,1)S(1)} %slice.117), channel_id=1, source_target_pairs={{0,8},{8,0},{1,9},{9,1},{2,10},{10,2},{3,11},{11,3},{4,12},{12,4},... | collective-permute-start | bytes 491528 | tf_op jit(solution)/shard_map/ppermute | solution.py:168
  (114 shorter events, 32.2 us)
Async XLA Ops:
  6.5 58.0 %copy-start.1 = (bf16[640,80]{0,1:T(8,128)(2,1)S(1)}, bf16[640,80]{0,1:T(8,128)(2,1)}, u32[]{:S(2)}) copy-start(bf16[640,80]{0,1:T(8,128)(2,1)} %param.14) | copy-start | bytes 307204
  6.5 165.1 %all-gather.2.cloned.1.call-start = ((), (), s32[]{:S(2)}) async-start(), calls=%async_computation.1 | async-start | bytes 4096000 | tf_op jit(solution)/shard_map/all_gather | solution.py:165
  8.8 67.2 %copy-start.7 = (bf16[32,256]{1,0:T(8,128)(2,1)}, bf16[32,256]{1,0:T(8,128)(2,1)S(1)}, u32[]{:S(2)}) copy-start(bf16[32,256]{1,0:T(8,128)(2,1)S(1)} %constant_dynamic-update-slice_fusion.4) | copy-start | bytes 49156
  9.7 62.2 %collective-permute-start.2 = (bf16[288,256]{1,0:T(8,128)(2,1)S(1)}, bf16[288,256]{1,0:T(8,128)(2,1)S(1)}, u32[]{:S(2)}, u32[]{:S(2)}) collective-permute-start(bf16[288,256]{1,0:T(8,128)(2,1)S(1)} %pad_maximum_fusion.5), channel_id=1, source_target_pairs={{488,0},{496,8},{504,16},{0,24},{8,32},{16,40},{24,48},{32,56},{40... | collective-permute-start | bytes 442376 | tf_op jit(solution)/shard_map/ppermute | solution.py:22
  14.2 61.7 %collective-permute-start.1 = (bf16[288,256]{1,0:T(8,128)(2,1)S(1)}, bf16[288,256]{1,0:T(8,128)(2,1)S(1)}, u32[]{:S(2)}, u32[]{:S(2)}) collective-permute-start(bf16[288,256]{1,0:T(8,128)(2,1)S(1)} %pad_maximum_fusion.5), channel_id=1, source_target_pairs={{496,0},{504,8},{0,16},{8,24},{16,32},{24,40},{32,48},{40,56},{48,... | collective-permute-start | bytes 442376 | tf_op jit(solution)/shard_map/ppermute | solution.py:22
  29.7 46.2 %collective-permute-start = (bf16[288,256]{1,0:T(8,128)(2,1)S(1)}, bf16[288,256]{1,0:T(8,128)(2,1)S(1)}, u32[]{:S(2)}, u32[]{:S(2)}) collective-permute-start(bf16[288,256]{1,0:T(8,128)(2,1)S(1)} %pad_maximum_fusion.5), channel_id=1, source_target_pairs={{504,0},{0,8},{8,16},{16,24},{24,32},{32,40},{40,48},{48,56},{56,6... | collective-permute-start | bytes 442376 | tf_op jit(solution)/shard_map/ppermute | solution.py:22
  41.5 23.1 %collective-permute-start.10 = (bf16[640,80]{0,1:T(8,128)(2,1)}, bf16[640,80]{0,1:T(8,128)(2,1)S(1)}, u32[]{:S(2)}, u32[]{:S(2)}) collective-permute-start(bf16[640,80]{0,1:T(8,128)(2,1)} %param.14), channel_id=1, source_target_pairs={{0,16},{16,0},{1,17},{17,1},{2,18},{18,2},{3,19},{19,3},{4,20},{20... | collective-permute-start | bytes 307208 | tf_op jit(solution)/shard_map/ppermute | solution.py:152
  64.6 21.2 %collective-permute-start.13 = (bf16[640,160]{0,1:T(8,128)(2,1)S(1)}, bf16[640,160]{0,1:T(8,128)(2,1)S(1)}, u32[]{:S(2)}, u32[]{:S(2)}) collective-permute-start(bf16[640,160]{0,1:T(8,128)(2,1)S(1)} %maximum_select_fusion), channel_id=1, source_target_pairs={{96,0},{0,32},{32,64},{64,96},{97,1},{1,33},{33,65},{65,97},{98,2}... | collective-permute-start | bytes 614408 | tf_op jit(solution)/shard_map/ppermute | solution.py:160
  67.5 18.2 %collective-permute-start.12 = (bf16[640,160]{0,1:T(8,128)(2,1)S(1)}, bf16[640,160]{0,1:T(8,128)(2,1)S(1)}, u32[]{:S(2)}, u32[]{:S(2)}) collective-permute-start(bf16[640,160]{0,1:T(8,128)(2,1)S(1)} %maximum_select_fusion), channel_id=1, source_target_pairs={{64,0},{96,32},{0,64},{32,96},{65,1},{97,33},{1,65},{33,97},{66,2}... | collective-permute-start | bytes 614408 | tf_op jit(solution)/shard_map/ppermute | solution.py:160
  71.9 11.6 %collective-permute-start.11 = (bf16[640,160]{0,1:T(8,128)(2,1)S(1)}, bf16[640,160]{0,1:T(8,128)(2,1)S(1)}, u32[]{:S(2)}, u32[]{:S(2)}) collective-permute-start(bf16[640,160]{0,1:T(8,128)(2,1)S(1)} %maximum_select_fusion), channel_id=1, source_target_pairs={{32,0},{64,32},{96,64},{0,96},{33,1},{65,33},{97,65},{1,97},{34,2}... | collective-permute-start | bytes 614408 | tf_op jit(solution)/shard_map/ppermute | solution.py:160
  77.5 44.8 %collective-permute-start.5 = (bf16[1152,256]{1,0:T(8,128)(2,1)}, bf16[1152,256]{1,0:T(8,128)(2,1)S(1)}, u32[]{:S(2)}, u32[]{:S(2)}) collective-permute-start(bf16[1152,256]{1,0:T(8,128)(2,1)} %pad_maximum_fusion.1), channel_id=1, source_target_pairs={{416,0},{424,8},{432,16},{440,24},{448,32},{456,40},{464,48},{472,... | collective-permute-start | bytes 1769480 | tf_op jit(solution)/shard_map/ppermute | solution.py:22
  79.4 27.6 %collective-permute-start.4 = (bf16[1152,256]{1,0:T(8,128)(2,1)}, bf16[1152,256]{1,0:T(8,128)(2,1)S(1)}, u32[]{:S(2)}, u32[]{:S(2)}) collective-permute-start(bf16[1152,256]{1,0:T(8,128)(2,1)} %pad_maximum_fusion.1), channel_id=1, source_target_pairs={{448,0},{456,8},{464,16},{472,24},{480,32},{488,40},{496,48},{504,... | collective-permute-start | bytes 1769480 | tf_op jit(solution)/shard_map/ppermute | solution.py:22
  83.6 37.8 %collective-permute-start.3 = (bf16[1152,256]{1,0:T(8,128)(2,1)}, bf16[1152,256]{1,0:T(8,128)(2,1)}, u32[]{:S(2)}, u32[]{:S(2)}) collective-permute-start(bf16[1152,256]{1,0:T(8,128)(2,1)} %pad_maximum_fusion.1), channel_id=1, source_target_pairs={{480,0},{488,8},{496,16},{504,24},{0,32},{8,40},{16,48},{24,56},{3... | collective-permute-start | bytes 1769480 | tf_op jit(solution)/shard_map/ppermute | solution.py:22
  85.9 37.2 %copy-start.8 = (bf16[32,256]{1,0:T(8,128)(2,1)S(1)}, bf16[32,256]{1,0:T(8,128)(2,1)}, u32[]{:S(2)}) copy-start(bf16[32,256]{1,0:T(8,128)(2,1)} %copy-done.7) | copy-start | bytes 49156
  87.1 158.5 %reduce-scatter.2.cloned.1.call-start = ((), (), s32[]{:S(2)}) async-start(), calls=%async_computation.2 | async-start | bytes 2949120 | tf_op jit(solution)/shard_map/reduce_scatter | solution.py:167
  123.1 35.5 %collective-permute-start.8 = (bf16[16,32,256]{2,1,0:T(8,128)(2,1)S(1)}, bf16[16,32,256]{2,1,0:T(8,128)(2,1)}, u32[]{:S(2)}, u32[]{:S(2)}) collective-permute-start(bf16[16,32,256]{2,1,0:T(8,128)(2,1)S(1)} %constant_dynamic-update-slice_fusion.6), channel_id=1, source_target_pairs={{128,0},{136,8},{144,16},{152,24},{160,32},{168,40},{176,48},{184,... | collective-permute-start | bytes 786440 | tf_op jit(solution)/shard_map/ppermute | solution.py:22
  127.3 31.3 %collective-permute-start.7 = (bf16[16,32,256]{2,1,0:T(8,128)(2,1)S(1)}, bf16[16,32,256]{2,1,0:T(8,128)(2,1)}, u32[]{:S(2)}, u32[]{:S(2)}) collective-permute-start(bf16[16,32,256]{2,1,0:T(8,128)(2,1)S(1)} %constant_dynamic-update-slice_fusion.6), channel_id=1, source_target_pairs={{256,0},{264,8},{272,16},{280,24},{288,32},{296,40},{304,48},{312,... | collective-permute-start | bytes 786440 | tf_op jit(solution)/shard_map/ppermute | solution.py:22
  130.1 27.5 %collective-permute-start.6 = (bf16[768,256]{1,0:T(8,128)(2,1)}, bf16[768,256]{1,0:T(8,128)(2,1)}, u32[]{:S(2)}, u32[]{:S(2)}) collective-permute-start(bf16[768,256]{1,0:T(8,128)(2,1)} %pad_maximum_fusion.3), channel_id=1, source_target_pairs={{384,0},{392,8},{400,16},{408,24},{416,32},{424,40},{432,48},{440,... | collective-permute-start | bytes 1179656 | tf_op jit(solution)/shard_map/ppermute | solution.py:22
  134.8 4.2 %copy-start.9 = (bf16[16,256,256]{2,1,0:T(8,128)(2,1)}, bf16[16,256,256]{2,1,0:T(8,128)(2,1)S(1)}, u32[]{:S(2)}) copy-start(bf16[16,256,256]{2,1,0:T(8,128)(2,1)S(1)} %constant_dynamic-update-slice_fusion.13) | copy-start | bytes 6291460
  147.9 6.2 %copy-start.6 = (f32[5,256]{1,0:T(8,128)S(1)}, f32[5,256]{1,0:T(8,128)}, u32[]{:S(2)}) copy-start(f32[5,256]{1,0:T(8,128)} %max.45) | copy-start | bytes 15364
  154.1 5.6 %copy-start.3 = (pred[256,256]{0,1:T(8,128)(4,1)S(1)}, pred[256,256]{0,1:T(8,128)(4,1)}, u32[]{:S(2)}) copy-start(pred[256,256]{0,1:T(8,128)(4,1)} %and_and_fusion.1) | copy-start | bytes 196612
  162.4 1.3 copy-start.2
  167.1 4.4 %collective-permute-start.9 = (bf16[256,640]{0,1:T(8,128)(2,1)S(1)}, bf16[256,640]{0,1:T(8,128)(2,1)S(1)}, u32[]{:S(2)}, u32[]{:S(2)}) collective-permute-start(bf16[256,640]{0,1:T(8,128)(2,1)S(1)} %bitcast.181), channel_id=1, source_target_pairs={{0,8},{8,0},{1,9},{9,1},{2,10},{10,2},{3,11},{11,3},{4,12},{12,4},... | collective-permute-start | bytes 983048 | tf_op jit(solution)/shard_map/ppermute | solution.py:150
  246.5 6.5 %collective-permute-start.14 = (bf16[256,320]{0,1:T(8,128)(2,1)S(1)}, bf16[256,320]{0,1:T(8,128)(2,1)S(1)}, u32[]{:S(2)}, u32[]{:S(2)}) collective-permute-start(bf16[256,320]{0,1:T(8,128)(2,1)S(1)} %slice.117), channel_id=1, source_target_pairs={{0,8},{8,0},{1,9},{9,1},{2,10},{10,2},{3,11},{11,3},{4,12},{12,4},... | collective-permute-start | bytes 491528 | tf_op jit(solution)/shard_map/ppermute | solution.py:168
  (3 other events, 2.9 us)
Sparse Core Ops, SparseCore 0:
  87.2 74.6 all-gather.1
  177.4 68.1 reduce-scatter.1

commit v7 on v6

--- a/solution.py
+++ b/solution.py
@@ -57,6 +57,7 @@
     suffix = own_kv
     reach = blocks // 4
     distances = [0]
+    last_block = shifted(own_kv, BLK, reach)
     step = 1
     while step < reach:
         got = [shifted_pair(suffix, prefix, BLK, step * k) for k in (1, 2, 3)]
@@ -64,15 +65,13 @@
         prefix = jnp.concatenate([pair[1] for pair in got] + [prefix], axis=0)
         distances = [d + step * k for k in (1, 2, 3) for d in distances] + distances
         step *= 4
-    late_suffix, got_prefix = shifted_pair(own_kv, prefix, BLK, reach)
+    suffix = jnp.concatenate((last_block, suffix), axis=0)
+    distances = [reach] + distances
     late_prefix = jnp.concatenate(
-        [got_prefix]
-        + [shifted(prefix, BLK, distance) for distance in range(2 * reach, blocks, reach)],
-        axis=0,
+        [shifted(prefix, BLK, distance) for distance in range(reach, blocks, reach)], axis=0
     )
     count = suffix.shape[0]
     early_suffix = suffix.reshape(count * tok_rows, 2 * width)
-    late_suffix = late_suffix.reshape(tok_rows, 2 * width)
     early_prefix = prefix.reshape(-1, 2 * width)
     late_prefix = late_prefix.reshape(-1, 2 * width)
 
@@ -96,7 +95,6 @@
         )
 
     early_visible = visible_at(distances)
-    late_visible = visible_at([reach])
 
     heads_of_query = queries.reshape(tok_rows, kv_heads, heads_per_group, HEAD_SIZE)
 
@@ -112,14 +110,19 @@
 
     def piece(q, cols, vcols, prefix_rows, suffix_rows, visible):
         pre_scores = scores_of(q, prefix_rows[:, cols])
-        suf_scores = jnp.where(visible[None], scores_of(q, suffix_rows[:, cols]), MASKED_SCORE)
-        peak = jnp.maximum(jnp.max(pre_scores, axis=-1), jnp.max(suf_scores, axis=-1))
+        peak = jnp.max(pre_scores, axis=-1)
+        if suffix_rows is not None:
+            suf_scores = jnp.where(
+                visible[None], scores_of(q, suffix_rows[:, cols]), MASKED_SCORE
+            )
+            peak = jnp.maximum(peak, jnp.max(suf_scores, axis=-1))
         pre_weights = jnp.exp(pre_scores - peak[..., None])
-        suf_weights = jnp.where(visible[None], jnp.exp(suf_scores - peak[..., None]), 0.0)
-        total = jnp.sum(pre_weights, axis=-1) + jnp.sum(suf_weights, axis=-1)
-        summed = weighted(pre_weights, prefix_rows[:, vcols]) + weighted(
-            suf_weights, suffix_rows[:, vcols]
-        )
+        total = jnp.sum(pre_weights, axis=-1)
+        summed = weighted(pre_weights, prefix_rows[:, vcols])
+        if suffix_rows is not None:
+            suf_weights = jnp.where(visible[None], jnp.exp(suf_scores - peak[..., None]), 0.0)
+            total = total + jnp.sum(suf_weights, axis=-1)
+            summed = summed + weighted(suf_weights, suffix_rows[:, vcols])
         return peak, total, summed
 
     def one_head(kv_head):
@@ -129,9 +132,7 @@
         first_peak, first_total, first_sum = piece(
             q, cols, vcols, early_prefix, early_suffix, early_visible
         )
-        late_peak, late_total, late_sum = piece(
-            q, cols, vcols, late_prefix, late_suffix, late_visible
-        )
+        late_peak, late_total, late_sum = piece(q, cols, vcols, late_prefix, None, None)
         peak = jnp.maximum(first_peak, late_peak)
         first_scale = jnp.exp(first_peak - peak)
         late_scale = jnp.exp(late_peak - peak)

time: 263 us -> 272 us (1.034)
  matrix products: 23.9 us -> 29.3 us
  local copies, waits for them, and re-layouts: 13.2 us -> 18.1 us
  waiting for transfers between devices: 120 us -> 116 us
  starting transfers between devices: 70.9 us -> 74.1 us
    unnamed x42 -> x40, local copies, waits for them, and re-layouts: 5.04 us -> 11.3 us
    ppermute x9 -> x10, starting transfers between devices: 48.8 us -> 54.4 us  [shifted(): return lax.ppermute(block, axis, route)]
    dot_general x4 -> x3, matrix products: 6.48 us -> 11.1 us  [scores_of(): jnp.einsum('qgd,kd->gqk', q, keys, preferred_element_type=jnp.float32)]
    reduce_sum x4 -> x3, other arithmetic: 8.14 us -> 12 us  [the longest x1 10.3 us: piece(): total = total + jnp.sum(suf_weights, axis=-1)]
    ppermute x9 -> x10, waiting for transfers between devices: 37.3 us -> 34.6 us  [shifted(): return lax.ppermute(block, axis, route)]
    and x2 -> x1, other arithmetic: 5.58 us -> 3.67 us  [visible_at(): (key_owner[None, :] == query_owner[:, None]) & (key_pos[None, :] <= query...]
    dot_general x4 -> x3, matrix products: 11.7 us -> 12.6 us  [weighted(): jnp.einsum('gqk,kd->gqd', weights.astype(jnp.bfloat16), values, preferred...]
  transfers between devices with their start and end apart: 17 -> 18, of which waited for: 7 -> 7; matrix products, arithmetic and copies ran while one was open for 17% -> 20% of each run, Pallas kernels for 0% -> 0%
where the time goes in v7:
time: 272 us; the launch traced here: 271 us
  waiting for transfers between devices  116 us (43%)
  starting transfers between devices  74.1 us (27%)
  matrix products  29.3 us (11%)
  other arithmetic  19 us (7%)
  local copies, waits for them, and re-layouts  18.1 us (7%)
  between operations  14 us (5%)
    reduce_scatter x1, waiting for transfers between devices, per_device(): lax.psum_scatter(product.astype(jnp.bfloat16), 'mp', scatter_dimension=1,...  68.5 us
    ppermute x10, starting transfers between devices, shifted(): return lax.ppermute(block, axis, route)  54.4 us
    ppermute x10, waiting for transfers between devices, shifted(): return lax.ppermute(block, axis, route)  34.6 us
    dot_general x3, matrix products, weighted(): jnp.einsum('gqk,kd->gqd', weights.astype(jnp.bfloat16), values, preferred...  12.6 us
    unnamed x40, local copies, waits for them, and re-layouts  11.3 us
    dot_general x3, matrix products, scores_of(): jnp.einsum('qgd,kd->gqk', q, keys, preferred_element_type=jnp.float32)  11.1 us
    ppermute x1, waiting for transfers between devices, per_device(): partner = lax.ppermute(out_weight, BLK[2], swap)  10.8 us
    reduce_sum x1, other arithmetic, piece(): total = total + jnp.sum(suf_weights, axis=-1)  10.3 us
  transfers between devices with their start and end apart: 18, of which 7 were waited for; matrix products, arithmetic and copies ran while one was open for 20% of the time, Pallas kernels for 0%

profile of v7, /device:TPU:1, one launch (start us, length us, event | category | flops | bytes accessed | tf_op | source)
XLA Modules:
  0.0 270.7 jit_solution(1042541209134129231)
XLA Ops:
  9.7 4.5 %collective-permute-start.2 = (bf16[288,256]{1,0:T(8,128)(2,1)S(1)}, bf16[288,256]{1,0:T(8,128)(2,1)S(1)}, u32[]{:S(2)}, u32[]{:S(2)}) collective-permute-start(bf16[288,256]{1,0:T(8,128)(2,1)S(1)} %pad_maximum_fusion.4), channel_id=1, source_target_pairs={{488,0},{496,8},{504,16},{0,24},{8,32},{16,40},{24,48},{32,56},{40... | collective-permute-start | bytes 442376 | tf_op jit(solution)/shard_map/ppermute | solution.py:22
  14.2 15.4 %collective-permute-start.1 = (bf16[288,256]{1,0:T(8,128)(2,1)S(1)}, bf16[288,256]{1,0:T(8,128)(2,1)S(1)}, u32[]{:S(2)}, u32[]{:S(2)}) collective-permute-start(bf16[288,256]{1,0:T(8,128)(2,1)S(1)} %pad_maximum_fusion.4), channel_id=1, source_target_pairs={{496,0},{504,8},{0,16},{8,24},{16,32},{24,40},{32,48},{40,56},{48,... | collective-permute-start | bytes 442376 | tf_op jit(solution)/shard_map/ppermute | solution.py:22
  29.7 11.8 %collective-permute-start = (bf16[288,256]{1,0:T(8,128)(2,1)S(1)}, bf16[288,256]{1,0:T(8,128)(2,1)S(1)}, u32[]{:S(2)}, u32[]{:S(2)}) collective-permute-start(bf16[288,256]{1,0:T(8,128)(2,1)S(1)} %pad_maximum_fusion.4), channel_id=1, source_target_pairs={{504,0},{0,8},{8,16},{16,24},{24,32},{32,40},{40,48},{48,56},{56,6... | collective-permute-start | bytes 442376 | tf_op jit(solution)/shard_map/ppermute | solution.py:22
  41.5 3.2 %collective-permute-start.6 = (bf16[1,256,256]{2,1,0:T(8,128)(2,1)S(1)}, bf16[1,256,256]{2,1,0:T(8,128)(2,1)S(1)}, u32[]{:S(2)}, u32[]{:S(2)}) collective-permute-start(bf16[1,256,256]{2,1,0:T(8,128)(2,1)S(1)} %bitcast.148), channel_id=1, source_target_pairs={{384,0},{392,8},{400,16},{408,24},{416,32},{424,40},{432,48},{440,... | collective-permute-start | bytes 393224 | tf_op jit(solution)/shard_map/ppermute | solution.py:22
  48.8 3.7 %and_and_fusion = pred[256,4352]{0,1:T(8,128)(4,1)S(1)} fusion(s32[256]{0:T(256)S(1)} %iota_add_fusion.1, s32[256]{0:T(256)S(1)} %convert_reduce_fusion.1, s32[4352]{0:T(1024)S(1)} %add.75, s32[4352]{0:T(1024)S(1)} %convert_reduce_fusion, pred[4352]{0:T(1024)(128)(4,1)S(1)} %broadcast_compare_fusion), kind=kLoop, calls=%fused_computation.13 | loop fusion | flops 4456448 | bytes 1155328 | tf_op jit(solution)/shard_map/and | solution.py:92
  53.7 10.8 %collective-permute-done.11 = bf16[640,80]{0,1:T(8,128)(2,1)S(1)} collective-permute-done((bf16[640,80]{0,1:T(8,128)(2,1)}, bf16[640,80]{0,1:T(8,128)(2,1)S(1)}, u32[]{:S(2)}, u32[]{:S(2)}) %collective-permute-start.11) | collective-permute-done | bytes 102432 | tf_op jit(solution)/shard_map/ppermute | solution.py:153
  64.6 4.2 %collective-permute-start.12 = (bf16[640,160]{0,1:T(8,128)(2,1)S(1)}, bf16[640,160]{0,1:T(8,128)(2,1)S(1)}, u32[]{:S(2)}, u32[]{:S(2)}) collective-permute-start(bf16[640,160]{0,1:T(8,128)(2,1)S(1)} %maximum_select_fusion), channel_id=1, source_target_pairs={{32,0},{64,32},{96,64},{0,96},{33,1},{65,33},{97,65},{1,97},{34,2}... | collective-permute-start | bytes 614408 | tf_op jit(solution)/shard_map/ppermute | solution.py:161
  68.8 2.5 collective-permute-start.13
  71.9 2.6 collective-permute-start.14
  75.6 3.3 %collective-permute-start.3 = (bf16[1152,256]{1,0:T(8,128)(2,1)}, bf16[1152,256]{1,0:T(8,128)(2,1)S(1)}, u32[]{:S(2)}, u32[]{:S(2)}) collective-permute-start(bf16[1152,256]{1,0:T(8,128)(2,1)} %pad_maximum_fusion.1), channel_id=1, source_target_pairs={{480,0},{488,8},{496,16},{504,24},{0,32},{8,40},{16,48},{24,56},{3... | collective-permute-start | bytes 1769480 | tf_op jit(solution)/shard_map/ppermute | solution.py:22
  78.9 3.7 %collective-permute-start.4 = (bf16[1152,256]{1,0:T(8,128)(2,1)}, bf16[1152,256]{1,0:T(8,128)(2,1)S(1)}, u32[]{:S(2)}, u32[]{:S(2)}) collective-permute-start(bf16[1152,256]{1,0:T(8,128)(2,1)} %pad_maximum_fusion.1), channel_id=1, source_target_pairs={{448,0},{456,8},{464,16},{472,24},{480,32},{488,40},{496,48},{504,... | collective-permute-start | bytes 1769480 | tf_op jit(solution)/shard_map/ppermute | solution.py:22
  82.6 3.6 %collective-permute-start.5 = (bf16[1152,256]{1,0:T(8,128)(2,1)}, bf16[1152,256]{1,0:T(8,128)(2,1)S(1)}, u32[]{:S(2)}, u32[]{:S(2)}) collective-permute-start(bf16[1152,256]{1,0:T(8,128)(2,1)} %pad_maximum_fusion.1), channel_id=1, source_target_pairs={{416,0},{424,8},{432,16},{440,24},{448,32},{456,40},{464,48},{472,... | collective-permute-start | bytes 1769480 | tf_op jit(solution)/shard_map/ppermute | solution.py:22
  87.7 9.0 %collective-permute-done.3 = bf16[1152,256]{1,0:T(8,128)(2,1)S(1)} collective-permute-done((bf16[1152,256]{1,0:T(8,128)(2,1)}, bf16[1152,256]{1,0:T(8,128)(2,1)S(1)}, u32[]{:S(2)}, u32[]{:S(2)}) %collective-permute-start.3) | collective-permute-done | bytes 589856 | tf_op jit(solution)/shard_map/ppermute | solution.py:22
  96.7 20.1 %collective-permute-done.4 = bf16[1152,256]{1,0:T(8,128)(2,1)S(1)} collective-permute-done((bf16[1152,256]{1,0:T(8,128)(2,1)}, bf16[1152,256]{1,0:T(8,128)(2,1)S(1)}, u32[]{:S(2)}, u32[]{:S(2)}) %collective-permute-start.4) | collective-permute-done | bytes 589856 | tf_op jit(solution)/shard_map/ppermute | solution.py:22
  116.8 5.6 %collective-permute-done.5 = bf16[1152,256]{1,0:T(8,128)(2,1)S(1)} collective-permute-done((bf16[1152,256]{1,0:T(8,128)(2,1)}, bf16[1152,256]{1,0:T(8,128)(2,1)S(1)}, u32[]{:S(2)}, u32[]{:S(2)}) %collective-permute-start.5) | collective-permute-done | bytes 589856 | tf_op jit(solution)/shard_map/ppermute | solution.py:22
  127.2 2.9 %collective-permute-start.8 = (bf16[16,32,256]{2,1,0:T(8,128)(2,1)S(1)}, bf16[16,32,256]{2,1,0:T(8,128)(2,1)S(1)}, u32[]{:S(2)}, u32[]{:S(2)}) collective-permute-start(bf16[16,32,256]{2,1,0:T(8,128)(2,1)S(1)} %constant_dynamic-update-slice_fusion.6), channel_id=1, source_target_pairs={{256,0},{264,8},{272,16},{280,24},{288,32},{296,40},{304,48},{312,... | collective-permute-start | bytes 786440 | tf_op jit(solution)/shard_map/ppermute | solution.py:22
  130.1 4.1 %collective-permute-start.9 = (bf16[16,32,256]{2,1,0:T(8,128)(2,1)S(1)}, bf16[16,32,256]{2,1,0:T(8,128)(2,1)S(1)}, u32[]{:S(2)}, u32[]{:S(2)}) collective-permute-start(bf16[16,32,256]{2,1,0:T(8,128)(2,1)S(1)} %constant_dynamic-update-slice_fusion.6), channel_id=1, source_target_pairs={{128,0},{136,8},{144,16},{152,24},{160,32},{168,40},{176,48},{184,... | collective-permute-start | bytes 786440 | tf_op jit(solution)/shard_map/ppermute | solution.py:22
  141.1 9.4 %fusion = (f32[5,256]{1,0:T(8,128)S(1)}, f32[4352,256,5]{1,0,2:T(8,128)}) fusion(pred[256,4352]{0,1:T(8,128)(4,1)S(1)} %and_and_fusion, bf16[256,5,128]{0,2,1:T(8,128)(2,1)S(1)} %bitcast.139, bf16[4352,256]{1,0:T(8,128)(2,1)S(1)} %bitcast.164), kind=kOutput, calls=%fused_computation.2 | convolution fusion | flops 1442773760 | bytes 24843264 | tf_op jit(solution)/shard_map/qgd,kd->gqk/dot_general | solution.py:103
  150.5 10.3 %fusion.3 = f32[5,256,128]{1,2,0:T(8,128)S(1)} fusion(f32[4352,256,5]{1,0,2:T(8,128)} %get-tuple-element.15, f32[5,256]{1,0:T(8,128)S(1)} %max.29, pred[256,4352]{0,1:T(8,128)(4,1)S(1)} %and_and_fusion, bf16[4352,256]{1,0:T(8,128)(2,1)S(1)} %bitcast.165), kind=kOutput, calls=%fused_computation.5 | convolution fusion | flops 1453916160 | bytes 25174016 | tf_op jit(solution)/shard_map/gqk,kd->gqd/dot_general | solution.py:107
  160.8 10.3 %fusion.1 = f32[5,256]{1,0:T(8,128)S(1)} fusion(f32[4352,256,5]{1,0,2:T(8,128)} %get-tuple-element.15, f32[5,256]{1,0:T(8,128)S(1)} %max.29, pred[256,4352]{0,1:T(8,128)(4,1)S(1)} %and_and_fusion), kind=kLoop, calls=%fused_computation.3 | loop fusion | flops 27851520 | bytes 23406592 | tf_op jit(solution)/shard_map/reduce_sum | solution.py:124
  176.4 2.6 collective-permute-start.10
  180.3 5.6 %convolution_convert_fusion = bf16[512,2560]{0,1:T(8,128)(2,1)} fusion(bf16[640,2560]{0,1:T(8,128)(2,1)} %all-gather.2.cloned.1.call-done, bf16[256,640]{0,1:T(8,128)(2,1)S(1)} %collective-permute-done.10, bf16[256,640]{0,1:T(8,128)(2,1)S(1)} %bitcast.168), kind=kOutput, calls=%fused_computation.12 | convolution fusion | flops 1680343040 | bytes 6553600 | tf_op jit(solution)/shard_map/dot_general | solution.py:167
  186.0 68.5 %reduce-scatter.2.cloned.1.call-done = bf16[512,320]{0,1:T(8,128)(2,1)} async-done(((bf16[512,2560]{0,1:T(8,128)(2,1)}), bf16[512,320]{0,1:T(8,128)(2,1)}) %reduce-scatter.2.cloned.1.call-update) | async-done | bytes 327696 | tf_op jit(solution)/shard_map/reduce_scatter | solution.py:168
  255.4 5.6 %collective-permute-start.15 = (bf16[256,320]{0,1:T(8,128)(2,1)S(1)}, bf16[256,320]{0,1:T(8,128)(2,1)S(1)}, u32[]{:S(2)}, u32[]{:S(2)}) collective-permute-start(bf16[256,320]{0,1:T(8,128)(2,1)S(1)} %slice.99), channel_id=1, source_target_pairs={{0,8},{8,0},{1,9},{9,1},{2,10},{10,2},{3,11},{11,3},{4,12},{12,4},... | collective-permute-start | bytes 491528 | tf_op jit(solution)/shard_map/ppermute | solution.py:169
  (106 shorter events, 33.5 us)
Async XLA Ops:
  6.5 58.0 %copy-start = (bf16[640,80]{0,1:T(8,128)(2,1)S(1)}, bf16[640,80]{0,1:T(8,128)(2,1)}, u32[]{:S(2)}) copy-start(bf16[640,80]{0,1:T(8,128)(2,1)} %param.13) | copy-start | bytes 307204
  6.5 173.8 %all-gather.2.cloned.1.call-start = ((), (), s32[]{:S(2)}) async-start(), calls=%async_computation.1 | async-start | bytes 4096000 | tf_op jit(solution)/shard_map/all_gather | solution.py:166
  9.7 65.9 %copy-start.7 = (bf16[32,256]{1,0:T(8,128)(2,1)}, bf16[32,256]{1,0:T(8,128)(2,1)S(1)}, u32[]{:S(2)}) copy-start(bf16[32,256]{1,0:T(8,128)(2,1)S(1)} %constant_dynamic-update-slice_fusion.4) | copy-start | bytes 49156
  9.7 62.2 %collective-permute-start.2 = (bf16[288,256]{1,0:T(8,128)(2,1)S(1)}, bf16[288,256]{1,0:T(8,128)(2,1)S(1)}, u32[]{:S(2)}, u32[]{:S(2)}) collective-permute-start(bf16[288,256]{1,0:T(8,128)(2,1)S(1)} %pad_maximum_fusion.4), channel_id=1, source_target_pairs={{488,0},{496,8},{504,16},{0,24},{8,32},{16,40},{24,48},{32,56},{40... | collective-permute-start | bytes 442376 | tf_op jit(solution)/shard_map/ppermute | solution.py:22
  14.2 60.3 %collective-permute-start.1 = (bf16[288,256]{1,0:T(8,128)(2,1)S(1)}, bf16[288,256]{1,0:T(8,128)(2,1)S(1)}, u32[]{:S(2)}, u32[]{:S(2)}) collective-permute-start(bf16[288,256]{1,0:T(8,128)(2,1)S(1)} %pad_maximum_fusion.4), channel_id=1, source_target_pairs={{496,0},{504,8},{0,16},{8,24},{16,32},{24,40},{32,48},{40,56},{48,... | collective-permute-start | bytes 442376 | tf_op jit(solution)/shard_map/ppermute | solution.py:22
  29.7 44.9 %collective-permute-start = (bf16[288,256]{1,0:T(8,128)(2,1)S(1)}, bf16[288,256]{1,0:T(8,128)(2,1)S(1)}, u32[]{:S(2)}, u32[]{:S(2)}) collective-permute-start(bf16[288,256]{1,0:T(8,128)(2,1)S(1)} %pad_maximum_fusion.4), channel_id=1, source_target_pairs={{504,0},{0,8},{8,16},{16,24},{24,32},{32,40},{40,48},{48,56},{56,6... | collective-permute-start | bytes 442376 | tf_op jit(solution)/shard_map/ppermute | solution.py:22
  41.5 27.3 %collective-permute-start.6 = (bf16[1,256,256]{2,1,0:T(8,128)(2,1)S(1)}, bf16[1,256,256]{2,1,0:T(8,128)(2,1)S(1)}, u32[]{:S(2)}, u32[]{:S(2)}) collective-permute-start(bf16[1,256,256]{2,1,0:T(8,128)(2,1)S(1)} %bitcast.148), channel_id=1, source_target_pairs={{384,0},{392,8},{400,16},{408,24},{416,32},{424,40},{432,48},{440,... | collective-permute-start | bytes 393224 | tf_op jit(solution)/shard_map/ppermute | solution.py:22
  44.7 19.8 %collective-permute-start.11 = (bf16[640,80]{0,1:T(8,128)(2,1)}, bf16[640,80]{0,1:T(8,128)(2,1)S(1)}, u32[]{:S(2)}, u32[]{:S(2)}) collective-permute-start(bf16[640,80]{0,1:T(8,128)(2,1)} %param.13), channel_id=1, source_target_pairs={{0,16},{16,0},{1,17},{17,1},{2,18},{18,2},{3,19},{19,3},{4,20},{20... | collective-permute-start | bytes 307208 | tf_op jit(solution)/shard_map/ppermute | solution.py:153
  64.6 18.1 %collective-permute-start.12 = (bf16[640,160]{0,1:T(8,128)(2,1)S(1)}, bf16[640,160]{0,1:T(8,128)(2,1)S(1)}, u32[]{:S(2)}, u32[]{:S(2)}) collective-permute-start(bf16[640,160]{0,1:T(8,128)(2,1)S(1)} %maximum_select_fusion), channel_id=1, source_target_pairs={{32,0},{64,32},{96,64},{0,96},{33,1},{65,33},{97,65},{1,97},{34,2}... | collective-permute-start | bytes 614408 | tf_op jit(solution)/shard_map/ppermute | solution.py:161
  68.8 17.5 %collective-permute-start.13 = (bf16[640,160]{0,1:T(8,128)(2,1)S(1)}, bf16[640,160]{0,1:T(8,128)(2,1)S(1)}, u32[]{:S(2)}, u32[]{:S(2)}) collective-permute-start(bf16[640,160]{0,1:T(8,128)(2,1)S(1)} %maximum_select_fusion), channel_id=1, source_target_pairs={{64,0},{96,32},{0,64},{32,96},{65,1},{97,33},{1,65},{33,97},{66,2}... | collective-permute-start | bytes 614408 | tf_op jit(solution)/shard_map/ppermute | solution.py:161
  71.9 10.7 %copy-start.1 = (bf16[288,256]{1,0:T(8,128)(2,1)}, bf16[288,256]{1,0:T(8,128)(2,1)S(1)}, u32[]{:S(2)}) copy-start(bf16[288,256]{1,0:T(8,128)(2,1)S(1)} %collective-permute-done.2) | copy-start | bytes 442372
  71.9 14.4 %collective-permute-start.14 = (bf16[640,160]{0,1:T(8,128)(2,1)S(1)}, bf16[640,160]{0,1:T(8,128)(2,1)S(1)}, u32[]{:S(2)}, u32[]{:S(2)}) collective-permute-start(bf16[640,160]{0,1:T(8,128)(2,1)S(1)} %maximum_select_fusion), channel_id=1, source_target_pairs={{96,0},{0,32},{32,64},{64,96},{97,1},{1,33},{33,65},{65,97},{98,2}... | collective-permute-start | bytes 614408 | tf_op jit(solution)/shard_map/ppermute | solution.py:161
  74.6 8.1 %copy-start.3 = (bf16[288,256]{1,0:T(8,128)(2,1)}, bf16[288,256]{1,0:T(8,128)(2,1)S(1)}, u32[]{:S(2)}) copy-start(bf16[288,256]{1,0:T(8,128)(2,1)S(1)} %collective-permute-done.1) | copy-start | bytes 442372
  74.6 8.0 %copy-start.5 = (bf16[288,256]{1,0:T(8,128)(2,1)}, bf16[288,256]{1,0:T(8,128)(2,1)S(1)}, u32[]{:S(2)}) copy-start(bf16[288,256]{1,0:T(8,128)(2,1)S(1)} %collective-permute-done) | copy-start | bytes 442372
  75.6 21.0 %collective-permute-start.3 = (bf16[1152,256]{1,0:T(8,128)(2,1)}, bf16[1152,256]{1,0:T(8,128)(2,1)S(1)}, u32[]{:S(2)}, u32[]{:S(2)}) collective-permute-start(bf16[1152,256]{1,0:T(8,128)(2,1)} %pad_maximum_fusion.1), channel_id=1, source_target_pairs={{480,0},{488,8},{496,16},{504,24},{0,32},{8,40},{16,48},{24,56},{3... | collective-permute-start | bytes 1769480 | tf_op jit(solution)/shard_map/ppermute | solution.py:22
  78.9 37.8 %collective-permute-start.4 = (bf16[1152,256]{1,0:T(8,128)(2,1)}, bf16[1152,256]{1,0:T(8,128)(2,1)S(1)}, u32[]{:S(2)}, u32[]{:S(2)}) collective-permute-start(bf16[1152,256]{1,0:T(8,128)(2,1)} %pad_maximum_fusion.1), channel_id=1, source_target_pairs={{448,0},{456,8},{464,16},{472,24},{480,32},{488,40},{496,48},{504,... | collective-permute-start | bytes 1769480 | tf_op jit(solution)/shard_map/ppermute | solution.py:22
  82.6 39.7 %collective-permute-start.5 = (bf16[1152,256]{1,0:T(8,128)(2,1)}, bf16[1152,256]{1,0:T(8,128)(2,1)S(1)}, u32[]{:S(2)}, u32[]{:S(2)}) collective-permute-start(bf16[1152,256]{1,0:T(8,128)(2,1)} %pad_maximum_fusion.1), channel_id=1, source_target_pairs={{416,0},{424,8},{432,16},{440,24},{448,32},{456,40},{464,48},{472,... | collective-permute-start | bytes 1769480 | tf_op jit(solution)/shard_map/ppermute | solution.py:22
  87.7 166.8 %reduce-scatter.2.cloned.1.call-start = ((), (), s32[]{:S(2)}) async-start(), calls=%async_computation.2 | async-start | bytes 2949120 | tf_op jit(solution)/shard_map/reduce_scatter | solution.py:168
  125.2 46.3 %collective-permute-start.7 = (bf16[16,32,256]{2,1,0:T(8,128)(2,1)S(1)}, bf16[16,32,256]{2,1,0:T(8,128)(2,1)S(1)}, u32[]{:S(2)}, u32[]{:S(2)}) collective-permute-start(bf16[16,32,256]{2,1,0:T(8,128)(2,1)S(1)} %constant_dynamic-update-slice_fusion.6), channel_id=1, source_target_pairs={{384,0},{392,8},{400,16},{408,24},{416,32},{424,40},{432,48},{440,... | collective-permute-start | bytes 786440 | tf_op jit(solution)/shard_map/ppermute | solution.py:22
  127.2 44.4 %collective-permute-start.8 = (bf16[16,32,256]{2,1,0:T(8,128)(2,1)S(1)}, bf16[16,32,256]{2,1,0:T(8,128)(2,1)S(1)}, u32[]{:S(2)}, u32[]{:S(2)}) collective-permute-start(bf16[16,32,256]{2,1,0:T(8,128)(2,1)S(1)} %constant_dynamic-update-slice_fusion.6), channel_id=1, source_target_pairs={{256,0},{264,8},{272,16},{280,24},{288,32},{296,40},{304,48},{312,... | collective-permute-start | bytes 786440 | tf_op jit(solution)/shard_map/ppermute | solution.py:22
  130.1 41.5 %collective-permute-start.9 = (bf16[16,32,256]{2,1,0:T(8,128)(2,1)S(1)}, bf16[16,32,256]{2,1,0:T(8,128)(2,1)S(1)}, u32[]{:S(2)}, u32[]{:S(2)}) collective-permute-start(bf16[16,32,256]{2,1,0:T(8,128)(2,1)S(1)} %constant_dynamic-update-slice_fusion.6), channel_id=1, source_target_pairs={{128,0},{136,8},{144,16},{152,24},{160,32},{168,40},{176,48},{184,... | collective-permute-start | bytes 786440 | tf_op jit(solution)/shard_map/ppermute | solution.py:22
  134.2 3.3 %copy-start.4 = (bf16[288,256]{1,0:T(8,128)(2,1)S(1)}, bf16[288,256]{1,0:T(8,128)(2,1)}, u32[]{:S(2)}) copy-start(bf16[288,256]{1,0:T(8,128)(2,1)} %copy-done.3) | copy-start | bytes 442372
  176.4 3.9 %collective-permute-start.10 = (bf16[256,640]{0,1:T(8,128)(2,1)S(1)}, bf16[256,640]{0,1:T(8,128)(2,1)S(1)}, u32[]{:S(2)}, u32[]{:S(2)}) collective-permute-start(bf16[256,640]{0,1:T(8,128)(2,1)S(1)} %bitcast.167), channel_id=1, source_target_pairs={{0,8},{8,0},{1,9},{9,1},{2,10},{10,2},{3,11},{11,3},{4,12},{12,4},... | collective-permute-start | bytes 983048 | tf_op jit(solution)/shard_map/ppermute | solution.py:151
  255.4 6.6 %collective-permute-start.15 = (bf16[256,320]{0,1:T(8,128)(2,1)S(1)}, bf16[256,320]{0,1:T(8,128)(2,1)S(1)}, u32[]{:S(2)}, u32[]{:S(2)}) collective-permute-start(bf16[256,320]{0,1:T(8,128)(2,1)S(1)} %slice.99), channel_id=1, source_target_pairs={{0,8},{8,0},{1,9},{9,1},{2,10},{10,2},{3,11},{11,3},{4,12},{12,4},... | collective-permute-start | bytes 491528 | tf_op jit(solution)/shard_map/ppermute | solution.py:169
  (3 other events, 7.3 us)
Sparse Core Ops, SparseCore 0:
  87.8 72.5 all-gather.1
  186.1 68.2 reduce-scatter.1

commit v8 on v5

--- a/solution.py
+++ b/solution.py
@@ -148,9 +148,18 @@
     swap = [(0, 1), (1, 0)]
     core = lax.axis_index("core")
     both = jnp.concatenate((attn, lax.ppermute(attn, "core", swap)), axis=0)
-    weight = out_weight
-    for name in BLK[-2::-1]:
-        weight = lax.all_gather(weight, name, axis=1, tiled=True)
+    across = dict(BLK_PARTS)[BLK[1]]
+    from_behind = [out_weight] + [
+        lax.ppermute(out_weight, BLK[1], [((i - k) % across, i) for i in range(across)])
+        for k in range(1, across)
+    ]
+    in_order = jnp.roll(jnp.stack(from_behind[::-1]), lax.axis_index(BLK[1]) + 1, axis=0)
+    row = jnp.moveaxis(in_order, 0, 1).reshape(out_weight.shape[0], -1)
+    weight = lax.all_gather(row, (BLK[0], BLK[2]), axis=1, tiled=True)
+    weight = weight.reshape(
+        out_weight.shape[0], dict(BLK_PARTS)[BLK[0]], dict(BLK_PARTS)[BLK[2]], across, -1
+    )
+    weight = jnp.swapaxes(weight, 2, 3).reshape(out_weight.shape[0], -1)
     product = jnp.dot(both, weight, preferred_element_type=jnp.float32)
     reduced = lax.psum_scatter(product.astype(jnp.bfloat16), "mp", scatter_dimension=1, tiled=True)
     other = lax.ppermute(reduced[tok_rows:], "core", swap)

time: 265 us -> 318 us (1.20)
  waiting for transfers between devices: 104 us -> 176 us
  blocking collectives: 35.7 us -> 0 us
  starting transfers between devices: 61 us -> 73.4 us
  local copies, waits for them, and re-layouts: 7.6 us -> 12.4 us
    all_gather x1, waiting for transfers between devices: 0.01 us -> 67.8 us  [per_device(): weight = lax.all_gather(row, (BLK[0], BLK[2]), axis=1, tiled=True)]
    all_gather x2 -> x0, blocking collectives: 35.7 us -> none  [per_device(): weight = lax.all_gather(weight, name, axis=1, tiled=True)]
    ppermute x0 -> x3, starting transfers between devices: none -> 10.9 us  [per_device(): lax.ppermute(out_weight, BLK[1], [((i - k) % across, i) for i in range(ac...]
    reduce_scatter x1, waiting for transfers between devices: 68.5 us -> 73.3 us  [per_device(): lax.psum_scatter(product.astype(jnp.bfloat16), 'mp', scatter_dimension=1,...]
  transfers between devices with their start and end apart: 13 -> 16, of which waited for: 6 -> 7; matrix products, arithmetic and copies ran while one was open for 14% -> 14% of each run, Pallas kernels for 0% -> 0%
where the time goes in v8:
time: 318 us; the launch traced here: 317 us
  waiting for transfers between devices  176 us (55%)
  starting transfers between devices  73.4 us (23%)
  matrix products  22 us (7%)
  other arithmetic  19.3 us (6%)
  between operations  14.1 us (4%)
  local copies, waits for them, and re-layouts  12.4 us (4%)
    reduce_scatter x1, waiting for transfers between devices, per_device(): lax.psum_scatter(product.astype(jnp.bfloat16), 'mp', scatter_dimension=1,...  73.3 us
    all_gather x1, waiting for transfers between devices, per_device(): weight = lax.all_gather(row, (BLK[0], BLK[2]), axis=1, tiled=True)  67.8 us
    ppermute x9, starting transfers between devices, shifted(): return lax.ppermute(block, axis, route)  51.8 us
    ppermute x9, waiting for transfers between devices, shifted(): return lax.ppermute(block, axis, route)  34 us
    dot_general x4, matrix products, weighted(): jnp.einsum('gqk,kd->gqd', weights.astype(jnp.bfloat16), values, preferred...  11.8 us
    ppermute x3, starting transfers between devices, per_device(): lax.ppermute(out_weight, BLK[1], [((i - k) % across, i) for i in range(ac...  10.9 us
    reduce_sum x4, other arithmetic, piece(): total = jnp.sum(pre_weights, axis=-1) + jnp.sum(suf_weights, axis=-1)  8.14 us
    dot_general x4, matrix products, scores_of(): jnp.einsum('qgd,kd->gqk', q, keys, preferred_element_type=jnp.float32)  6.48 us
  transfers between devices with their start and end apart: 16, of which 7 were waited for; matrix products, arithmetic and copies ran while one was open for 14% of the time, Pallas kernels for 0%

profile of v8, /device:TPU:1, one launch (start us, length us, event | category | flops | bytes accessed | tf_op | source)
XLA Modules:
  0.0 317.3 jit_solution(7697294712046041353)
XLA Ops:
  6.5 5.6 %collective-permute-start.11 = (bf16[640,80]{0,1:T(8,128)(2,1)}, bf16[640,80]{0,1:T(8,128)(2,1)S(1)}, u32[]{:S(2)}, u32[]{:S(2)}) collective-permute-start(bf16[640,80]{0,1:T(8,128)(2,1)} %param.14), channel_id=1, source_target_pairs={{64,0},{96,32},{0,64},{32,96},{65,1},{97,33},{1,65},{33,97},{66,2}... | collective-permute-start | bytes 307208 | tf_op jit(solution)/shard_map/ppermute | solution.py:153
  12.1 2.8 collective-permute-start.10
  14.9 2.5 collective-permute-start.12
  20.6 6.9 %collective-permute-start.2 = (bf16[288,256]{1,0:T(8,128)(2,1)S(1)}, bf16[288,256]{1,0:T(8,128)(2,1)S(1)}, u32[]{:S(2)}, u32[]{:S(2)}) collective-permute-start(bf16[288,256]{1,0:T(8,128)(2,1)S(1)} %pad_maximum_fusion.5), channel_id=1, source_target_pairs={{488,0},{496,8},{504,16},{0,24},{8,32},{16,40},{24,48},{32,56},{40... | collective-permute-start | bytes 442376 | tf_op jit(solution)/shard_map/ppermute | solution.py:22
  27.4 12.2 %collective-permute-start.1 = (bf16[288,256]{1,0:T(8,128)(2,1)S(1)}, bf16[288,256]{1,0:T(8,128)(2,1)S(1)}, u32[]{:S(2)}, u32[]{:S(2)}) collective-permute-start(bf16[288,256]{1,0:T(8,128)(2,1)S(1)} %pad_maximum_fusion.5), channel_id=1, source_target_pairs={{496,0},{504,8},{0,16},{8,24},{16,32},{24,40},{32,48},{40,56},{48,... | collective-permute-start | bytes 442376 | tf_op jit(solution)/shard_map/ppermute | solution.py:22
  41.6 4.8 %and_and_fusion = pred[256,4096]{0,1:T(8,128)(4,1)} fusion(s32[256]{0:T(256)S(1)} %iota_add_fusion.1, s32[256]{0:T(256)S(1)} %get-tuple-element.6, s32[4096]{0:T(1024)S(1)} %bitcast.175, s32[4096]{0:T(1024)S(1)} %convert_reduce_fusion, pred[4096]{0:T(1024)(128)(4,1)S(1)} %broadcast_compare_fusion), kind=kLoop, calls=%fused_computation.13 | loop fusion | flops 4194304 | bytes 1087488 | tf_op jit(solution)/shard_map/and | solution.py:93
  48.3 11.0 %collective-permute-start = (bf16[288,256]{1,0:T(8,128)(2,1)S(1)}, bf16[288,256]{1,0:T(8,128)(2,1)S(1)}, u32[]{:S(2)}, u32[]{:S(2)}) collective-permute-start(bf16[288,256]{1,0:T(8,128)(2,1)S(1)} %pad_maximum_fusion.5), channel_id=1, source_target_pairs={{504,0},{0,8},{8,16},{16,24},{24,32},{32,40},{40,48},{48,56},{56,6... | collective-permute-start | bytes 442376 | tf_op jit(solution)/shard_map/ppermute | solution.py:22
  59.5 2.9 collective-permute-done
  63.4 5.0 %collective-permute-start.4 = (bf16[1152,256]{1,0:T(8,128)(2,1)}, bf16[1152,256]{1,0:T(8,128)(2,1)S(1)}, u32[]{:S(2)}, u32[]{:S(2)}) collective-permute-start(bf16[1152,256]{1,0:T(8,128)(2,1)} %pad_maximum_fusion.1), channel_id=1, source_target_pairs={{448,0},{456,8},{464,16},{472,24},{480,32},{488,40},{496,48},{504,... | collective-permute-start | bytes 1769480 | tf_op jit(solution)/shard_map/ppermute | solution.py:22
  68.4 2.8 collective-permute-start.3
  71.2 4.7 %collective-permute-start.5 = (bf16[1152,256]{1,0:T(8,128)(2,1)}, bf16[1152,256]{1,0:T(8,128)(2,1)S(1)}, u32[]{:S(2)}, u32[]{:S(2)}) collective-permute-start(bf16[1152,256]{1,0:T(8,128)(2,1)} %pad_maximum_fusion.1), channel_id=1, source_target_pairs={{416,0},{424,8},{432,16},{440,24},{448,32},{456,40},{464,48},{472,... | collective-permute-start | bytes 1769480 | tf_op jit(solution)/shard_map/ppermute | solution.py:22
  78.5 26.2 %collective-permute-done.3 = bf16[1152,256]{1,0:T(8,128)(2,1)S(1)} collective-permute-done((bf16[1152,256]{1,0:T(8,128)(2,1)}, bf16[1152,256]{1,0:T(8,128)(2,1)S(1)}, u32[]{:S(2)}, u32[]{:S(2)}) %collective-permute-start.3) | collective-permute-done | bytes 589856 | tf_op jit(solution)/shard_map/ppermute | solution.py:22
  104.7 3.2 %collective-permute-done.5 = bf16[1152,256]{1,0:T(8,128)(2,1)S(1)} collective-permute-done((bf16[1152,256]{1,0:T(8,128)(2,1)}, bf16[1152,256]{1,0:T(8,128)(2,1)S(1)}, u32[]{:S(2)}, u32[]{:S(2)}) %collective-permute-start.5) | collective-permute-done | bytes 589856 | tf_op jit(solution)/shard_map/ppermute | solution.py:22
  108.0 4.2 %collective-permute-start.8 = (bf16[16,32,256]{2,1,0:T(8,128)(2,1)S(1)}, bf16[16,32,256]{2,1,0:T(8,128)(2,1)}, u32[]{:S(2)}, u32[]{:S(2)}) collective-permute-start(bf16[16,32,256]{2,1,0:T(8,128)(2,1)S(1)} %constant_dynamic-update-slice_fusion.4), channel_id=1, source_target_pairs={{128,0},{136,8},{144,16},{152,24},{160,32},{168,40},{176,48},{184,... | collective-permute-start | bytes 786440 | tf_op jit(solution)/shard_map/ppermute | solution.py:22
  112.2 2.3 collective-permute-start.7
  115.4 2.8 collective-permute-start.6
  120.0 3.6 %fusion = (f32[5,256]{1,0:T(8,128)S(1)}, f32[4096,256,5]{1,0,2:T(8,128)S(1)}) fusion(pred[256,4096]{0,1:T(8,128)(4,1)S(1)} %copy-done, bf16[256,5,128]{0,2,1:T(8,128)(2,1)S(1)} %bitcast.153, bf16[4096,256]{1,0:T(8,128)(2,1)S(1)} %bitcast.181), kind=kOutput, calls=%fused_computation.2 | convolution fusion | flops 1357904640 | bytes 23401472 | tf_op jit(solution)/shard_map/qgd,kd->gqk/dot_general | solution.py:105
  124.2 8.3 %fusion.3 = f32[5,256,128]{1,2,0:T(8,128)} fusion(f32[4096,256,5]{1,0,2:T(8,128)S(1)} %get-tuple-element.15, f32[5,256]{1,0:T(8,128)} %max.45, pred[256,4096]{0,1:T(8,128)(4,1)} %and_and_fusion, bf16[4096,256]{1,0:T(8,128)(2,1)} %bitcast.182), kind=kOutput, calls=%fused_computation.5 | convolution fusion | flops 1368391680 | bytes 23732224 | tf_op jit(solution)/shard_map/gqk,kd->gqd/dot_general | solution.py:109
  132.6 6.2 %fusion.1 = f32[5,256]{1,0:T(8,128)S(1)} fusion(f32[4096,256,5]{1,0,2:T(8,128)S(1)} %get-tuple-element.15, f32[5,256]{1,0:T(8,128)} %max.45, pred[256,4096]{0,1:T(8,128)(4,1)} %and_and_fusion), kind=kLoop, calls=%fused_computation.3 | loop fusion | flops 26213120 | bytes 22030336 | tf_op jit(solution)/shard_map/reduce_sum | solution.py:119
  148.9 4.7 %collective-permute-start.9 = (bf16[256,640]{0,1:T(8,128)(2,1)S(1)}, bf16[256,640]{0,1:T(8,128)(2,1)S(1)}, u32[]{:S(2)}, u32[]{:S(2)}) collective-permute-start(bf16[256,640]{0,1:T(8,128)(2,1)S(1)} %bitcast.184), channel_id=1, source_target_pairs={{0,8},{8,0},{1,9},{9,1},{2,10},{10,2},{3,11},{11,3},{4,12},{12,4},... | collective-permute-start | bytes 983048 | tf_op jit(solution)/shard_map/ppermute | solution.py:150
  153.5 67.8 %all-gather.2.cloned.1.call-done = bf16[640,2560]{0,1:T(8,128)(2,1)} async-done(((bf16[640,320]{0,1:T(8,128)(2,1)}), bf16[640,2560]{0,1:T(8,128)(2,1)}) %all-gather.2.cloned.1.call-update) | async-done | bytes 3276816 | tf_op jit(solution)/shard_map/all_gather | solution.py:158
  223.6 3.8 %convolution_convert_fusion = bf16[512,2560]{0,1:T(8,128)(2,1)} fusion(bf16[640,2560]{0,1:T(8,128)(2,1)S(1)} %bitcast.157, bf16[256,640]{0,1:T(8,128)(2,1)S(1)} %collective-permute-done.9, bf16[256,640]{0,1:T(8,128)(2,1)S(1)} %bitcast.185), kind=kOutput, calls=%fused_computation.12 | convolution fusion | flops 1680343040 | bytes 6553600 | tf_op jit(solution)/shard_map/dot_general | solution.py:163
  227.4 73.3 %reduce-scatter.2.cloned.1.call-done = bf16[512,320]{0,1:T(8,128)(2,1)} async-done(((bf16[512,2560]{0,1:T(8,128)(2,1)}), bf16[512,320]{0,1:T(8,128)(2,1)}) %reduce-scatter.2.cloned.1.call-update) | async-done | bytes 327696 | tf_op jit(solution)/shard_map/reduce_scatter | solution.py:164
  301.6 6.0 %collective-permute-start.13 = (bf16[256,320]{0,1:T(8,128)(2,1)S(1)}, bf16[256,320]{0,1:T(8,128)(2,1)S(1)}, u32[]{:S(2)}, u32[]{:S(2)}) collective-permute-start(bf16[256,320]{0,1:T(8,128)(2,1)S(1)} %slice.117), channel_id=1, source_target_pairs={{0,8},{8,0},{1,9},{9,1},{2,10},{10,2},{3,11},{11,3},{4,12},{12,4},... | collective-permute-start | bytes 491528 | tf_op jit(solution)/shard_map/ppermute | solution.py:165
  (104 shorter events, 29.8 us)
Async XLA Ops:
  6.5 52.9 %copy-start.3 = (bf16[640,80]{0,1:T(8,128)(2,1)S(1)}, bf16[640,80]{0,1:T(8,128)(2,1)}, u32[]{:S(2)}) copy-start(bf16[640,80]{0,1:T(8,128)(2,1)} %param.14) | copy-start | bytes 307204
  6.5 214.8 %all-gather.2.cloned.1.call-start = ((), (), s32[]{:S(2)}) async-start(), calls=%async_computation.1 | async-start | bytes 3686400 | tf_op jit(solution)/shard_map/all_gather | solution.py:158
  6.5 52.8 %collective-permute-start.11 = (bf16[640,80]{0,1:T(8,128)(2,1)}, bf16[640,80]{0,1:T(8,128)(2,1)S(1)}, u32[]{:S(2)}, u32[]{:S(2)}) collective-permute-start(bf16[640,80]{0,1:T(8,128)(2,1)} %param.14), channel_id=1, source_target_pairs={{64,0},{96,32},{0,64},{32,96},{65,1},{97,33},{1,65},{33,97},{66,2}... | collective-permute-start | bytes 307208 | tf_op jit(solution)/shard_map/ppermute | solution.py:153
  12.1 36.2 %collective-permute-start.10 = (bf16[640,80]{0,1:T(8,128)(2,1)}, bf16[640,80]{0,1:T(8,128)(2,1)S(1)}, u32[]{:S(2)}, u32[]{:S(2)}) collective-permute-start(bf16[640,80]{0,1:T(8,128)(2,1)} %param.14), channel_id=1, source_target_pairs={{32,0},{64,32},{96,64},{0,96},{33,1},{65,33},{97,65},{1,97},{34,2}... | collective-permute-start | bytes 307208 | tf_op jit(solution)/shard_map/ppermute | solution.py:153
  14.9 44.4 %collective-permute-start.12 = (bf16[640,80]{0,1:T(8,128)(2,1)}, bf16[640,80]{0,1:T(8,128)(2,1)S(1)}, u32[]{:S(2)}, u32[]{:S(2)}) collective-permute-start(bf16[640,80]{0,1:T(8,128)(2,1)} %param.14), channel_id=1, source_target_pairs={{96,0},{0,32},{32,64},{64,96},{97,1},{1,33},{33,65},{65,97},{98,2}... | collective-permute-start | bytes 307208 | tf_op jit(solution)/shard_map/ppermute | solution.py:153
  20.6 38.9 %collective-permute-start.2 = (bf16[288,256]{1,0:T(8,128)(2,1)S(1)}, bf16[288,256]{1,0:T(8,128)(2,1)S(1)}, u32[]{:S(2)}, u32[]{:S(2)}) collective-permute-start(bf16[288,256]{1,0:T(8,128)(2,1)S(1)} %pad_maximum_fusion.5), channel_id=1, source_target_pairs={{488,0},{496,8},{504,16},{0,24},{8,32},{16,40},{24,48},{32,56},{40... | collective-permute-start | bytes 442376 | tf_op jit(solution)/shard_map/ppermute | solution.py:22
  27.4 32.0 %collective-permute-start.1 = (bf16[288,256]{1,0:T(8,128)(2,1)S(1)}, bf16[288,256]{1,0:T(8,128)(2,1)S(1)}, u32[]{:S(2)}, u32[]{:S(2)}) collective-permute-start(bf16[288,256]{1,0:T(8,128)(2,1)S(1)} %pad_maximum_fusion.5), channel_id=1, source_target_pairs={{496,0},{504,8},{0,16},{8,24},{16,32},{24,40},{32,48},{40,56},{48,... | collective-permute-start | bytes 442376 | tf_op jit(solution)/shard_map/ppermute | solution.py:22
  48.3 14.0 %collective-permute-start = (bf16[288,256]{1,0:T(8,128)(2,1)S(1)}, bf16[288,256]{1,0:T(8,128)(2,1)S(1)}, u32[]{:S(2)}, u32[]{:S(2)}) collective-permute-start(bf16[288,256]{1,0:T(8,128)(2,1)S(1)} %pad_maximum_fusion.5), channel_id=1, source_target_pairs={{504,0},{0,8},{8,16},{16,24},{24,32},{32,40},{40,48},{48,56},{56,6... | collective-permute-start | bytes 442376 | tf_op jit(solution)/shard_map/ppermute | solution.py:22
  63.4 15.1 %collective-permute-start.4 = (bf16[1152,256]{1,0:T(8,128)(2,1)}, bf16[1152,256]{1,0:T(8,128)(2,1)S(1)}, u32[]{:S(2)}, u32[]{:S(2)}) collective-permute-start(bf16[1152,256]{1,0:T(8,128)(2,1)} %pad_maximum_fusion.1), channel_id=1, source_target_pairs={{448,0},{456,8},{464,16},{472,24},{480,32},{488,40},{496,48},{504,... | collective-permute-start | bytes 1769480 | tf_op jit(solution)/shard_map/ppermute | solution.py:22
  68.4 36.3 %collective-permute-start.3 = (bf16[1152,256]{1,0:T(8,128)(2,1)}, bf16[1152,256]{1,0:T(8,128)(2,1)S(1)}, u32[]{:S(2)}, u32[]{:S(2)}) collective-permute-start(bf16[1152,256]{1,0:T(8,128)(2,1)} %pad_maximum_fusion.1), channel_id=1, source_target_pairs={{480,0},{488,8},{496,16},{504,24},{0,32},{8,40},{16,48},{24,56},{3... | collective-permute-start | bytes 1769480 | tf_op jit(solution)/shard_map/ppermute | solution.py:22
  71.2 36.8 %collective-permute-start.5 = (bf16[1152,256]{1,0:T(8,128)(2,1)}, bf16[1152,256]{1,0:T(8,128)(2,1)S(1)}, u32[]{:S(2)}, u32[]{:S(2)}) collective-permute-start(bf16[1152,256]{1,0:T(8,128)(2,1)} %pad_maximum_fusion.1), channel_id=1, source_target_pairs={{416,0},{424,8},{432,16},{440,24},{448,32},{456,40},{464,48},{472,... | collective-permute-start | bytes 1769480 | tf_op jit(solution)/shard_map/ppermute | solution.py:22
  76.8 223.8 %reduce-scatter.2.cloned.1.call-start = ((), (), s32[]{:S(2)}) async-start(), calls=%async_computation.2 | async-start | bytes 2949120 | tf_op jit(solution)/shard_map/reduce_scatter | solution.py:164
  108.0 32.2 %collective-permute-start.8 = (bf16[16,32,256]{2,1,0:T(8,128)(2,1)S(1)}, bf16[16,32,256]{2,1,0:T(8,128)(2,1)}, u32[]{:S(2)}, u32[]{:S(2)}) collective-permute-start(bf16[16,32,256]{2,1,0:T(8,128)(2,1)S(1)} %constant_dynamic-update-slice_fusion.4), channel_id=1, source_target_pairs={{128,0},{136,8},{144,16},{152,24},{160,32},{168,40},{176,48},{184,... | collective-permute-start | bytes 786440 | tf_op jit(solution)/shard_map/ppermute | solution.py:22
  112.2 28.1 %collective-permute-start.7 = (bf16[16,32,256]{2,1,0:T(8,128)(2,1)S(1)}, bf16[16,32,256]{2,1,0:T(8,128)(2,1)}, u32[]{:S(2)}, u32[]{:S(2)}) collective-permute-start(bf16[16,32,256]{2,1,0:T(8,128)(2,1)S(1)} %constant_dynamic-update-slice_fusion.4), channel_id=1, source_target_pairs={{256,0},{264,8},{272,16},{280,24},{288,32},{296,40},{304,48},{312,... | collective-permute-start | bytes 786440 | tf_op jit(solution)/shard_map/ppermute | solution.py:22
  115.4 23.9 %collective-permute-start.6 = (bf16[768,256]{1,0:T(8,128)(2,1)}, bf16[768,256]{1,0:T(8,128)(2,1)}, u32[]{:S(2)}, u32[]{:S(2)}) collective-permute-start(bf16[768,256]{1,0:T(8,128)(2,1)} %pad_maximum_fusion.3), channel_id=1, source_target_pairs={{384,0},{392,8},{400,16},{408,24},{416,32},{424,40},{432,48},{440,... | collective-permute-start | bytes 1179656 | tf_op jit(solution)/shard_map/ppermute | solution.py:22
  118.4 1.7 copy-start
  118.5 5.1 %copy-start.5 = (bf16[16,256,256]{2,1,0:T(8,128)(2,1)}, bf16[16,256,256]{2,1,0:T(8,128)(2,1)S(1)}, u32[]{:S(2)}) copy-start(bf16[16,256,256]{2,1,0:T(8,128)(2,1)S(1)} %constant_dynamic-update-slice_fusion.11) | copy-start | bytes 6291460
  132.6 6.2 %copy-start.4 = (f32[5,256]{1,0:T(8,128)S(1)}, f32[5,256]{1,0:T(8,128)}, u32[]{:S(2)}) copy-start(f32[5,256]{1,0:T(8,128)} %max.45) | copy-start | bytes 15364
  138.8 2.7 copy-start.2
  144.1 1.3 copy-start.1
  148.9 74.7 %collective-permute-start.9 = (bf16[256,640]{0,1:T(8,128)(2,1)S(1)}, bf16[256,640]{0,1:T(8,128)(2,1)S(1)}, u32[]{:S(2)}, u32[]{:S(2)}) collective-permute-start(bf16[256,640]{0,1:T(8,128)(2,1)S(1)} %bitcast.184), channel_id=1, source_target_pairs={{0,8},{8,0},{1,9},{9,1},{2,10},{10,2},{3,11},{11,3},{4,12},{12,4},... | collective-permute-start | bytes 983048 | tf_op jit(solution)/shard_map/ppermute | solution.py:150
  301.6 7.0 %collective-permute-start.13 = (bf16[256,320]{0,1:T(8,128)(2,1)S(1)}, bf16[256,320]{0,1:T(8,128)(2,1)S(1)}, u32[]{:S(2)}, u32[]{:S(2)}) collective-permute-start(bf16[256,320]{0,1:T(8,128)(2,1)S(1)} %slice.117), channel_id=1, source_target_pairs={{0,8},{8,0},{1,9},{9,1},{2,10},{10,2},{3,11},{11,3},{4,12},{12,4},... | collective-permute-start | bytes 491528 | tf_op jit(solution)/shard_map/ppermute | solution.py:165
Sparse Core Ops, SparseCore 0:
  76.9 144.3 all-gather.1
  227.5 73.1 reduce-scatter.1

commit v9 on v8

--- a/solution.py
+++ b/solution.py
@@ -154,12 +154,14 @@
         for k in range(1, across)
     ]
     in_order = jnp.roll(jnp.stack(from_behind[::-1]), lax.axis_index(BLK[1]) + 1, axis=0)
-    row = jnp.moveaxis(in_order, 0, 1).reshape(out_weight.shape[0], -1)
-    weight = lax.all_gather(row, (BLK[0], BLK[2]), axis=1, tiled=True)
-    weight = weight.reshape(
-        out_weight.shape[0], dict(BLK_PARTS)[BLK[0]], dict(BLK_PARTS)[BLK[2]], across, -1
+    row = jnp.moveaxis(in_order, 0, 1)
+    partner = lax.ppermute(row, BLK[2], swap)
+    pair = jnp.where(
+        lax.axis_index(BLK[2]) == 0,
+        jnp.stack((row, partner), axis=2),
+        jnp.stack((partner, row), axis=2),
     )
-    weight = jnp.swapaxes(weight, 2, 3).reshape(out_weight.shape[0], -1)
+    weight = lax.all_gather(pair.reshape(out_weight.shape[0], -1), BLK[0], axis=1, tiled=True)
     product = jnp.dot(both, weight, preferred_element_type=jnp.float32)
     reduced = lax.psum_scatter(product.astype(jnp.bfloat16), "mp", scatter_dimension=1, tiled=True)
     other = lax.ppermute(reduced[tok_rows:], "core", swap)

time: 318 us -> 260 us (0.82)
  waiting for transfers between devices: 176 us -> 117 us
  starting transfers between devices: 73.4 us -> 70.1 us
    all_gather x1, waiting for transfers between devices: 67.8 us -> 0.84 us  [per_device(): lax.all_gather(pair.reshape(out_weight.shape[0], -1), BLK[0], axis=1, til...]
    ppermute x0 -> x1, waiting for transfers between devices: none -> 10.2 us  [per_device(): partner = lax.ppermute(row, BLK[2], swap)]
    ppermute x9, starting transfers between devices: 51.8 us -> 46 us  [shifted(): return lax.ppermute(block, axis, route)]
    reduce_scatter x1, waiting for transfers between devices: 73.3 us -> 69.9 us  [per_device(): lax.psum_scatter(product.astype(jnp.bfloat16), 'mp', scatter_dimension=1,...]
  transfers between devices with their start and end apart: 16 -> 17, of which waited for: 7 -> 9; matrix products, arithmetic and copies ran while one was open for 14% -> 19% of each run, Pallas kernels for 0% -> 0%
where the time goes in v9:
time: 260 us; the launch traced here: 259 us
  waiting for transfers between devices  117 us (45%)
  starting transfers between devices  70.1 us (27%)
  matrix products  23.9 us (9%)
  other arithmetic  21.5 us (8%)
  between operations  14.1 us (5%)
  local copies, waits for them, and re-layouts  11.9 us (5%)
    reduce_scatter x1, waiting for transfers between devices, per_device(): lax.psum_scatter(product.astype(jnp.bfloat16), 'mp', scatter_dimension=1,...  69.9 us
    ppermute x9, starting transfers between devices, shifted(): return lax.ppermute(block, axis, route)  46 us
    ppermute x9, waiting for transfers between devices, shifted(): return lax.ppermute(block, axis, route)  34 us
    dot_general x4, matrix products, weighted(): jnp.einsum('gqk,kd->gqd', weights.astype(jnp.bfloat16), values, preferred...  11.8 us
    ppermute x3, starting transfers between devices, per_device(): lax.ppermute(out_weight, BLK[1], [((i - k) % across, i) for i in range(ac...  10.8 us
    ppermute x1, waiting for transfers between devices, per_device(): partner = lax.ppermute(row, BLK[2], swap)  10.2 us
    reduce_sum x4, other arithmetic, piece(): total = jnp.sum(pre_weights, axis=-1) + jnp.sum(suf_weights, axis=-1)  8.14 us
    dot_general x4, matrix products, scores_of(): jnp.einsum('qgd,kd->gqk', q, keys, preferred_element_type=jnp.float32)  6.48 us
  transfers between devices with their start and end apart: 17, of which 9 were waited for; matrix products, arithmetic and copies ran while one was open for 19% of the time, Pallas kernels for 0%

profile of v9, /device:TPU:1, one launch (start us, length us, event | category | flops | bytes accessed | tf_op | source)
XLA Modules:
  0.0 258.7 jit_solution(1363255045382816386)
XLA Ops:
  6.5 5.5 %collective-permute-start.11 = (bf16[640,80]{0,1:T(8,128)(2,1)}, bf16[640,80]{0,1:T(8,128)(2,1)S(1)}, u32[]{:S(2)}, u32[]{:S(2)}) collective-permute-start(bf16[640,80]{0,1:T(8,128)(2,1)} %param.14), channel_id=1, source_target_pairs={{64,0},{96,32},{0,64},{32,96},{65,1},{97,33},{1,65},{33,97},{66,2}... | collective-permute-start | bytes 307208 | tf_op jit(solution)/shard_map/ppermute | solution.py:153
  12.0 2.8 %collective-permute-start.10 = (bf16[640,80]{0,1:T(8,128)(2,1)}, bf16[640,80]{0,1:T(8,128)(2,1)S(1)}, u32[]{:S(2)}, u32[]{:S(2)}) collective-permute-start(bf16[640,80]{0,1:T(8,128)(2,1)} %param.14), channel_id=1, source_target_pairs={{32,0},{64,32},{96,64},{0,96},{33,1},{65,33},{97,65},{1,97},{34,2}... | collective-permute-start | bytes 307208 | tf_op jit(solution)/shard_map/ppermute | solution.py:153
  14.8 2.5 collective-permute-start.12
  20.5 6.9 %collective-permute-start.2 = (bf16[288,256]{1,0:T(8,128)(2,1)S(1)}, bf16[288,256]{1,0:T(8,128)(2,1)S(1)}, u32[]{:S(2)}, u32[]{:S(2)}) collective-permute-start(bf16[288,256]{1,0:T(8,128)(2,1)S(1)} %pad_maximum_fusion.5), channel_id=1, source_target_pairs={{488,0},{496,8},{504,16},{0,24},{8,32},{16,40},{24,48},{32,56},{40... | collective-permute-start | bytes 442376 | tf_op jit(solution)/shard_map/ppermute | solution.py:22
  27.3 12.2 %collective-permute-start.1 = (bf16[288,256]{1,0:T(8,128)(2,1)S(1)}, bf16[288,256]{1,0:T(8,128)(2,1)S(1)}, u32[]{:S(2)}, u32[]{:S(2)}) collective-permute-start(bf16[288,256]{1,0:T(8,128)(2,1)S(1)} %pad_maximum_fusion.5), channel_id=1, source_target_pairs={{496,0},{504,8},{0,16},{8,24},{16,32},{24,40},{32,48},{40,56},{48,... | collective-permute-start | bytes 442376 | tf_op jit(solution)/shard_map/ppermute | solution.py:22
  41.5 11.0 %collective-permute-start = (bf16[288,256]{1,0:T(8,128)(2,1)S(1)}, bf16[288,256]{1,0:T(8,128)(2,1)S(1)}, u32[]{:S(2)}, u32[]{:S(2)}) collective-permute-start(bf16[288,256]{1,0:T(8,128)(2,1)S(1)} %pad_maximum_fusion.5), channel_id=1, source_target_pairs={{504,0},{0,8},{8,16},{16,24},{24,32},{32,40},{40,48},{48,56},{56,6... | collective-permute-start | bytes 442376 | tf_op jit(solution)/shard_map/ppermute | solution.py:22
  55.2 3.0 %collective-permute-start.13 = (bf16[640,4,80]{0,2,1:T(8,128)(2,1)}, bf16[640,4,80]{0,2,1:T(8,128)(2,1)}, u32[]{:S(2)}, u32[]{:S(2)}) collective-permute-start(bf16[640,4,80]{0,2,1:T(8,128)(2,1)} %get-tuple-element.11), channel_id=1, source_target_pairs={{0,16},{16,0},{1,17},{17,1},{2,18},{18,2},{3,19},{19,3},{4,20},{20... | collective-permute-start | bytes 1228808 | tf_op jit(solution)/shard_map/ppermute | solution.py:158
  58.3 13.8 %collective-permute-done = bf16[288,256]{1,0:T(8,128)(2,1)S(1)} collective-permute-done((bf16[288,256]{1,0:T(8,128)(2,1)S(1)}, bf16[288,256]{1,0:T(8,128)(2,1)S(1)}, u32[]{:S(2)}, u32[]{:S(2)}) %collective-permute-start) | collective-permute-done | bytes 147488 | tf_op jit(solution)/shard_map/ppermute | solution.py:22
  75.1 4.8 %collective-permute-start.3 = (bf16[1152,256]{1,0:T(8,128)(2,1)}, bf16[1152,256]{1,0:T(8,128)(2,1)S(1)}, u32[]{:S(2)}, u32[]{:S(2)}) collective-permute-start(bf16[1152,256]{1,0:T(8,128)(2,1)} %pad_maximum_fusion.1), channel_id=1, source_target_pairs={{480,0},{488,8},{496,16},{504,24},{0,32},{8,40},{16,48},{24,56},{3... | collective-permute-start | bytes 1769480 | tf_op jit(solution)/shard_map/ppermute | solution.py:22
  79.9 4.8 %and_and_fusion = pred[256,4096]{0,1:T(8,128)(4,1)} fusion(s32[256]{0:T(256)S(1)} %iota_add_fusion.1, s32[256]{0:T(256)S(1)} %get-tuple-element.6, s32[4096]{0:T(1024)S(1)} %bitcast.173, s32[4096]{0:T(1024)S(1)} %convert_reduce_fusion, pred[4096]{0:T(1024)(128)(4,1)S(1)} %broadcast_compare_fusion), kind=kLoop, calls=%fused_computation.13 | loop fusion | flops 4194304 | bytes 1087488 | tf_op jit(solution)/shard_map/and | solution.py:93
  88.5 10.2 %collective-permute-done.13 = bf16[640,4,80]{0,2,1:T(8,128)(2,1)} collective-permute-done((bf16[640,4,80]{0,2,1:T(8,128)(2,1)}, bf16[640,4,80]{0,2,1:T(8,128)(2,1)}, u32[]{:S(2)}, u32[]{:S(2)}) %collective-permute-start.13) | collective-permute-done | bytes 409632 | tf_op jit(solution)/shard_map/ppermute | solution.py:158
  98.7 2.2 maximum_select_fusion
  100.9 14.9 %collective-permute-done.3 = bf16[1152,256]{1,0:T(8,128)(2,1)S(1)} collective-permute-done((bf16[1152,256]{1,0:T(8,128)(2,1)}, bf16[1152,256]{1,0:T(8,128)(2,1)S(1)}, u32[]{:S(2)}, u32[]{:S(2)}) %collective-permute-start.3) | collective-permute-done | bytes 589856 | tf_op jit(solution)/shard_map/ppermute | solution.py:22
  118.0 2.1 collective-permute-start.8
  120.2 2.9 %collective-permute-start.7 = (bf16[16,32,256]{2,1,0:T(8,128)(2,1)S(1)}, bf16[16,32,256]{2,1,0:T(8,128)(2,1)}, u32[]{:S(2)}, u32[]{:S(2)}) collective-permute-start(bf16[16,32,256]{2,1,0:T(8,128)(2,1)S(1)} %constant_dynamic-update-slice_fusion.4), channel_id=1, source_target_pairs={{256,0},{264,8},{272,16},{280,24},{288,32},{296,40},{304,48},{312,... | collective-permute-start | bytes 786440 | tf_op jit(solution)/shard_map/ppermute | solution.py:22
  123.9 2.4 collective-permute-start.6
  128.1 3.6 %fusion = (f32[5,256]{1,0:T(8,128)S(1)}, f32[4096,256,5]{1,0,2:T(8,128)S(1)}) fusion(pred[256,4096]{0,1:T(8,128)(4,1)S(1)} %copy-done, bf16[256,5,128]{0,2,1:T(8,128)(2,1)S(1)} %bitcast.153, bf16[4096,256]{1,0:T(8,128)(2,1)S(1)} %bitcast.179), kind=kOutput, calls=%fused_computation.2 | convolution fusion | flops 1357904640 | bytes 23401472 | tf_op jit(solution)/shard_map/qgd,kd->gqk/dot_general | solution.py:105
  132.4 8.3 %fusion.3 = f32[5,256,128]{1,2,0:T(8,128)} fusion(f32[4096,256,5]{1,0,2:T(8,128)S(1)} %get-tuple-element.17, f32[5,256]{1,0:T(8,128)} %max.45, pred[256,4096]{0,1:T(8,128)(4,1)} %and_and_fusion, bf16[4096,256]{1,0:T(8,128)(2,1)} %bitcast.180), kind=kOutput, calls=%fused_computation.5 | convolution fusion | flops 1368391680 | bytes 23732224 | tf_op jit(solution)/shard_map/gqk,kd->gqd/dot_general | solution.py:109
  140.7 6.2 %fusion.1 = f32[5,256]{1,0:T(8,128)S(1)} fusion(f32[4096,256,5]{1,0,2:T(8,128)S(1)} %get-tuple-element.17, f32[5,256]{1,0:T(8,128)} %max.45, pred[256,4096]{0,1:T(8,128)(4,1)} %and_and_fusion), kind=kLoop, calls=%fused_computation.3 | loop fusion | flops 26213120 | bytes 22030336 | tf_op jit(solution)/shard_map/reduce_sum | solution.py:119
  147.3 3.2 %collective-permute-done.6 = bf16[768,256]{1,0:T(8,128)(2,1)} collective-permute-done((bf16[768,256]{1,0:T(8,128)(2,1)}, bf16[768,256]{1,0:T(8,128)(2,1)}, u32[]{:S(2)}, u32[]{:S(2)}) %collective-permute-start.6) | collective-permute-done | bytes 393248 | tf_op jit(solution)/shard_map/ppermute | solution.py:22
  160.1 4.7 %collective-permute-start.9 = (bf16[256,640]{0,1:T(8,128)(2,1)S(1)}, bf16[256,640]{0,1:T(8,128)(2,1)S(1)}, u32[]{:S(2)}, u32[]{:S(2)}) collective-permute-start(bf16[256,640]{0,1:T(8,128)(2,1)S(1)} %bitcast.182), channel_id=1, source_target_pairs={{0,8},{8,0},{1,9},{9,1},{2,10},{10,2},{3,11},{11,3},{4,12},{12,4},... | collective-permute-start | bytes 983048 | tf_op jit(solution)/shard_map/ppermute | solution.py:150
  166.9 5.7 %convolution_convert_fusion = bf16[512,2560]{0,1:T(8,128)(2,1)} fusion(bf16[640,2560]{0,1:T(8,128)(2,1)} %all-gather.2.cloned.1.call-done, bf16[256,640]{0,1:T(8,128)(2,1)S(1)} %collective-permute-done.9, bf16[256,640]{0,1:T(8,128)(2,1)S(1)} %bitcast.183), kind=kOutput, calls=%fused_computation.12 | convolution fusion | flops 1680343040 | bytes 6553600 | tf_op jit(solution)/shard_map/dot_general | solution.py:165
  172.6 69.9 %reduce-scatter.2.cloned.1.call-done = bf16[512,320]{0,1:T(8,128)(2,1)} async-done(((bf16[512,2560]{0,1:T(8,128)(2,1)}), bf16[512,320]{0,1:T(8,128)(2,1)}) %reduce-scatter.2.cloned.1.call-update) | async-done | bytes 327696 | tf_op jit(solution)/shard_map/reduce_scatter | solution.py:166
  243.4 5.5 %collective-permute-start.14 = (bf16[256,320]{0,1:T(8,128)(2,1)S(1)}, bf16[256,320]{0,1:T(8,128)(2,1)S(1)}, u32[]{:S(2)}, u32[]{:S(2)}) collective-permute-start(bf16[256,320]{0,1:T(8,128)(2,1)S(1)} %slice.117), channel_id=1, source_target_pairs={{0,8},{8,0},{1,9},{9,1},{2,10},{10,2},{3,11},{11,3},{4,12},{12,4},... | collective-permute-start | bytes 491528 | tf_op jit(solution)/shard_map/ppermute | solution.py:167
  (104 shorter events, 35.7 us)
Async XLA Ops:
  6.5 160.4 %all-gather.2.cloned.1.call-start = ((), (), s32[]{:S(2)}) async-start(), calls=%async_computation.1 | async-start | bytes 4096000 | tf_op jit(solution)/shard_map/all_gather | solution.py:164
  6.5 45.9 %collective-permute-start.11 = (bf16[640,80]{0,1:T(8,128)(2,1)}, bf16[640,80]{0,1:T(8,128)(2,1)S(1)}, u32[]{:S(2)}, u32[]{:S(2)}) collective-permute-start(bf16[640,80]{0,1:T(8,128)(2,1)} %param.14), channel_id=1, source_target_pairs={{64,0},{96,32},{0,64},{32,96},{65,1},{97,33},{1,65},{33,97},{66,2}... | collective-permute-start | bytes 307208 | tf_op jit(solution)/shard_map/ppermute | solution.py:153
  12.0 29.4 %collective-permute-start.10 = (bf16[640,80]{0,1:T(8,128)(2,1)}, bf16[640,80]{0,1:T(8,128)(2,1)S(1)}, u32[]{:S(2)}, u32[]{:S(2)}) collective-permute-start(bf16[640,80]{0,1:T(8,128)(2,1)} %param.14), channel_id=1, source_target_pairs={{32,0},{64,32},{96,64},{0,96},{33,1},{65,33},{97,65},{1,97},{34,2}... | collective-permute-start | bytes 307208 | tf_op jit(solution)/shard_map/ppermute | solution.py:153
  14.8 37.7 %collective-permute-start.12 = (bf16[640,80]{0,1:T(8,128)(2,1)}, bf16[640,80]{0,1:T(8,128)(2,1)S(1)}, u32[]{:S(2)}, u32[]{:S(2)}) collective-permute-start(bf16[640,80]{0,1:T(8,128)(2,1)} %param.14), channel_id=1, source_target_pairs={{96,0},{0,32},{32,64},{64,96},{97,1},{1,33},{33,65},{65,97},{98,2}... | collective-permute-start | bytes 307208 | tf_op jit(solution)/shard_map/ppermute | solution.py:153
  20.5 37.8 %collective-permute-start.2 = (bf16[288,256]{1,0:T(8,128)(2,1)S(1)}, bf16[288,256]{1,0:T(8,128)(2,1)S(1)}, u32[]{:S(2)}, u32[]{:S(2)}) collective-permute-start(bf16[288,256]{1,0:T(8,128)(2,1)S(1)} %pad_maximum_fusion.5), channel_id=1, source_target_pairs={{488,0},{496,8},{504,16},{0,24},{8,32},{16,40},{24,48},{32,56},{40... | collective-permute-start | bytes 442376 | tf_op jit(solution)/shard_map/ppermute | solution.py:22
  27.3 31.0 %collective-permute-start.1 = (bf16[288,256]{1,0:T(8,128)(2,1)S(1)}, bf16[288,256]{1,0:T(8,128)(2,1)S(1)}, u32[]{:S(2)}, u32[]{:S(2)}) collective-permute-start(bf16[288,256]{1,0:T(8,128)(2,1)S(1)} %pad_maximum_fusion.5), channel_id=1, source_target_pairs={{496,0},{504,8},{0,16},{8,24},{16,32},{24,40},{32,48},{40,56},{48,... | collective-permute-start | bytes 442376 | tf_op jit(solution)/shard_map/ppermute | solution.py:22
  41.5 30.7 %collective-permute-start = (bf16[288,256]{1,0:T(8,128)(2,1)S(1)}, bf16[288,256]{1,0:T(8,128)(2,1)S(1)}, u32[]{:S(2)}, u32[]{:S(2)}) collective-permute-start(bf16[288,256]{1,0:T(8,128)(2,1)S(1)} %pad_maximum_fusion.5), channel_id=1, source_target_pairs={{504,0},{0,8},{8,16},{16,24},{24,32},{32,40},{40,48},{48,56},{56,6... | collective-permute-start | bytes 442376 | tf_op jit(solution)/shard_map/ppermute | solution.py:22
  55.2 43.5 %collective-permute-start.13 = (bf16[640,4,80]{0,2,1:T(8,128)(2,1)}, bf16[640,4,80]{0,2,1:T(8,128)(2,1)}, u32[]{:S(2)}, u32[]{:S(2)}) collective-permute-start(bf16[640,4,80]{0,2,1:T(8,128)(2,1)} %get-tuple-element.11), channel_id=1, source_target_pairs={{0,16},{16,0},{1,17},{17,1},{2,18},{18,2},{3,19},{19,3},{4,20},{20... | collective-permute-start | bytes 1228808 | tf_op jit(solution)/shard_map/ppermute | solution.py:158
  73.1 27.8 %collective-permute-start.4 = (bf16[1152,256]{1,0:T(8,128)(2,1)}, bf16[1152,256]{1,0:T(8,128)(2,1)S(1)}, u32[]{:S(2)}, u32[]{:S(2)}) collective-permute-start(bf16[1152,256]{1,0:T(8,128)(2,1)} %pad_maximum_fusion.1), channel_id=1, source_target_pairs={{448,0},{456,8},{464,16},{472,24},{480,32},{488,40},{496,48},{504,... | collective-permute-start | bytes 1769480 | tf_op jit(solution)/shard_map/ppermute | solution.py:22
  75.1 40.8 %collective-permute-start.3 = (bf16[1152,256]{1,0:T(8,128)(2,1)}, bf16[1152,256]{1,0:T(8,128)(2,1)S(1)}, u32[]{:S(2)}, u32[]{:S(2)}) collective-permute-start(bf16[1152,256]{1,0:T(8,128)(2,1)} %pad_maximum_fusion.1), channel_id=1, source_target_pairs={{480,0},{488,8},{496,16},{504,24},{0,32},{8,40},{16,48},{24,56},{3... | collective-permute-start | bytes 1769480 | tf_op jit(solution)/shard_map/ppermute | solution.py:22
  84.7 33.3 %collective-permute-start.5 = (bf16[1152,256]{1,0:T(8,128)(2,1)}, bf16[1152,256]{1,0:T(8,128)(2,1)S(1)}, u32[]{:S(2)}, u32[]{:S(2)}) collective-permute-start(bf16[1152,256]{1,0:T(8,128)(2,1)} %pad_maximum_fusion.1), channel_id=1, source_target_pairs={{416,0},{424,8},{432,16},{440,24},{448,32},{456,40},{464,48},{472,... | collective-permute-start | bytes 1769480 | tf_op jit(solution)/shard_map/ppermute | solution.py:22
  100.9 141.6 %reduce-scatter.2.cloned.1.call-start = ((), (), s32[]{:S(2)}) async-start(), calls=%async_computation.2 | async-start | bytes 2949120 | tf_op jit(solution)/shard_map/reduce_scatter | solution.py:166
  118.0 33.5 %collective-permute-start.8 = (bf16[16,32,256]{2,1,0:T(8,128)(2,1)S(1)}, bf16[16,32,256]{2,1,0:T(8,128)(2,1)}, u32[]{:S(2)}, u32[]{:S(2)}) collective-permute-start(bf16[16,32,256]{2,1,0:T(8,128)(2,1)S(1)} %constant_dynamic-update-slice_fusion.4), channel_id=1, source_target_pairs={{128,0},{136,8},{144,16},{152,24},{160,32},{168,40},{176,48},{184,... | collective-permute-start | bytes 786440 | tf_op jit(solution)/shard_map/ppermute | solution.py:22
  120.2 31.4 %collective-permute-start.7 = (bf16[16,32,256]{2,1,0:T(8,128)(2,1)S(1)}, bf16[16,32,256]{2,1,0:T(8,128)(2,1)}, u32[]{:S(2)}, u32[]{:S(2)}) collective-permute-start(bf16[16,32,256]{2,1,0:T(8,128)(2,1)S(1)} %constant_dynamic-update-slice_fusion.4), channel_id=1, source_target_pairs={{256,0},{264,8},{272,16},{280,24},{288,32},{296,40},{304,48},{312,... | collective-permute-start | bytes 786440 | tf_op jit(solution)/shard_map/ppermute | solution.py:22
  123.9 26.7 %collective-permute-start.6 = (bf16[768,256]{1,0:T(8,128)(2,1)}, bf16[768,256]{1,0:T(8,128)(2,1)}, u32[]{:S(2)}, u32[]{:S(2)}) collective-permute-start(bf16[768,256]{1,0:T(8,128)(2,1)} %pad_maximum_fusion.3), channel_id=1, source_target_pairs={{384,0},{392,8},{400,16},{408,24},{416,32},{424,40},{432,48},{440,... | collective-permute-start | bytes 1179656 | tf_op jit(solution)/shard_map/ppermute | solution.py:22
  126.5 1.7 copy-start
  126.6 5.1 %copy-start.4 = (bf16[16,256,256]{2,1,0:T(8,128)(2,1)}, bf16[16,256,256]{2,1,0:T(8,128)(2,1)S(1)}, u32[]{:S(2)}) copy-start(bf16[16,256,256]{2,1,0:T(8,128)(2,1)S(1)} %constant_dynamic-update-slice_fusion.11) | copy-start | bytes 6291460
  140.7 6.2 %copy-start.3 = (f32[5,256]{1,0:T(8,128)S(1)}, f32[5,256]{1,0:T(8,128)}, u32[]{:S(2)}) copy-start(f32[5,256]{1,0:T(8,128)} %max.45) | copy-start | bytes 15364
  146.9 5.8 %copy-start.2 = (pred[256,256]{0,1:T(8,128)(4,1)S(1)}, pred[256,256]{0,1:T(8,128)(4,1)}, u32[]{:S(2)}) copy-start(pred[256,256]{0,1:T(8,128)(4,1)} %and_and_fusion.1) | copy-start | bytes 196612
  155.3 1.3 copy-start.1
  160.1 6.0 %collective-permute-start.9 = (bf16[256,640]{0,1:T(8,128)(2,1)S(1)}, bf16[256,640]{0,1:T(8,128)(2,1)S(1)}, u32[]{:S(2)}, u32[]{:S(2)}) collective-permute-start(bf16[256,640]{0,1:T(8,128)(2,1)S(1)} %bitcast.182), channel_id=1, source_target_pairs={{0,8},{8,0},{1,9},{9,1},{2,10},{10,2},{3,11},{11,3},{4,12},{12,4},... | collective-permute-start | bytes 983048 | tf_op jit(solution)/shard_map/ppermute | solution.py:150
  243.4 6.5 %collective-permute-start.14 = (bf16[256,320]{0,1:T(8,128)(2,1)S(1)}, bf16[256,320]{0,1:T(8,128)(2,1)S(1)}, u32[]{:S(2)}, u32[]{:S(2)}) collective-permute-start(bf16[256,320]{0,1:T(8,128)(2,1)S(1)} %slice.117), channel_id=1, source_target_pairs={{0,8},{8,0},{1,9},{9,1},{2,10},{10,2},{3,11},{11,3},{4,12},{12,4},... | collective-permute-start | bytes 491528 | tf_op jit(solution)/shard_map/ppermute | solution.py:167
Sparse Core Ops, SparseCore 0:
  101.0 65.8 all-gather.1
  172.7 69.7 reduce-scatter.1

commit v10 on v7

--- a/solution.py
+++ b/solution.py
@@ -57,9 +57,11 @@
     suffix = own_kv
     reach = blocks // 4
     distances = [0]
-    last_block = shifted(own_kv, BLK, reach)
     step = 1
     while step < reach:
+        if step > 1:
+            own_kv, suffix, prefix = lax.optimization_barrier((own_kv, suffix, prefix))
+            last_block = shifted(own_kv, BLK, reach)
         got = [shifted_pair(suffix, prefix, BLK, step * k) for k in (1, 2, 3)]
         suffix = jnp.concatenate([pair[0] for pair in got] + [suffix], axis=0)
         prefix = jnp.concatenate([pair[1] for pair in got] + [prefix], axis=0)
@@ -149,21 +151,20 @@
     swap = [(0, 1), (1, 0)]
     core = lax.axis_index("core")
     both = jnp.concatenate((attn, lax.ppermute(attn, "core", swap)), axis=0)
-    z_hi = lax.axis_index(BLK[2])
-    partner = lax.ppermute(out_weight, BLK[2], swap)
-    pair = jnp.where(
-        z_hi == 0,
-        jnp.concatenate((out_weight, partner), axis=1),
-        jnp.concatenate((partner, out_weight), axis=1),
-    )
     across = dict(BLK_PARTS)[BLK[1]]
-    from_behind = [pair] + [
-        lax.ppermute(pair, BLK[1], [((i - k) % across, i) for i in range(across)])
+    from_behind = [out_weight] + [
+        lax.ppermute(out_weight, BLK[1], [((i - k) % across, i) for i in range(across)])
         for k in range(1, across)
     ]
     in_order = jnp.roll(jnp.stack(from_behind[::-1]), lax.axis_index(BLK[1]) + 1, axis=0)
-    row = jnp.moveaxis(in_order, 0, 1).reshape(out_weight.shape[0], -1)
-    weight = lax.all_gather(row, BLK[0], axis=1, tiled=True)
+    row = jnp.moveaxis(in_order, 0, 1)
+    partner = lax.ppermute(row, BLK[2], swap)
+    pair = jnp.where(
+        lax.axis_index(BLK[2]) == 0,
+        jnp.stack((row, partner), axis=2),
+        jnp.stack((partner, row), axis=2),
+    )
+    weight = lax.all_gather(pair.reshape(out_weight.shape[0], -1), BLK[0], axis=1, tiled=True)
     product = jnp.dot(both, weight, preferred_element_type=jnp.float32)
     reduced = lax.psum_scatter(product.astype(jnp.bfloat16), "mp", scatter_dimension=1, tiled=True)
     other = lax.ppermute(reduced[tok_rows:], "core", swap)

time: 272 us -> 265 us (0.974)
  waiting for transfers between devices: 116 us -> 105 us
    ppermute x4, waiting for transfers between devices: 10.9 us -> 4.57 us  [the longest x3 4.56 us: per_device(): lax.ppermute(out_weight, BLK[1], [((i - k) % across, i) for i in range(ac...]
    unnamed x40 -> x18, local copies, waits for them, and re-layouts: 11.3 us -> 6.85 us
  transfers between devices with their start and end apart: 18 -> 18, of which waited for: 7 -> 6; matrix products, arithmetic and copies ran while one was open for 20% -> 22% of each run, Pallas kernels for 0% -> 0%
where the time goes in v10:
time: 265 us; the launch traced here: 264 us
  waiting for transfers between devices  105 us (40%)
  starting transfers between devices  75.7 us (29%)
  matrix products  30.9 us (12%)
  other arithmetic  21.1 us (8%)
  local copies, waits for them, and re-layouts  17.5 us (7%)
  between operations  13.9 us (5%)
    reduce_scatter x1, waiting for transfers between devices, per_device(): lax.psum_scatter(product.astype(jnp.bfloat16), 'mp', scatter_dimension=1,...  65.8 us
    ppermute x10, starting transfers between devices, shifted(): return lax.ppermute(block, axis, route)  54.4 us
    ppermute x10, waiting for transfers between devices, shifted(): return lax.ppermute(block, axis, route)  32 us
    dot_general x3, matrix products, weighted(): jnp.einsum('gqk,kd->gqd', weights.astype(jnp.bfloat16), values, preferred...  12.7 us
    dot_general x3, matrix products, scores_of(): jnp.einsum('qgd,kd->gqk', q, keys, preferred_element_type=jnp.float32)  12.6 us
    reduce_sum x1, other arithmetic, piece(): total = total + jnp.sum(suf_weights, axis=-1)  10.3 us
    ppermute x3, starting transfers between devices, per_device(): lax.ppermute(out_weight, BLK[1], [((i - k) % across, i) for i in range(ac...  9.04 us
    unnamed x18, local copies, waits for them, and re-layouts  6.85 us
  transfers between devices with their start and end apart: 18, of which 6 were waited for; matrix products, arithmetic and copies ran while one was open for 22% of the time, Pallas kernels for 0%

profile of v10, /device:TPU:1, one launch (start us, length us, event | category | flops | bytes accessed | tf_op | source)
XLA Modules:
  0.0 263.6 jit_solution(1667528905829924601)
XLA Ops:
  9.7 4.5 %collective-permute-start.2 = (bf16[288,256]{1,0:T(8,128)(2,1)S(1)}, bf16[288,256]{1,0:T(8,128)(2,1)S(1)}, u32[]{:S(2)}, u32[]{:S(2)}) collective-permute-start(bf16[288,256]{1,0:T(8,128)(2,1)S(1)} %pad_maximum_fusion.5), channel_id=1, source_target_pairs={{488,0},{496,8},{504,16},{0,24},{8,32},{16,40},{24,48},{32,56},{40... | collective-permute-start | bytes 442376 | tf_op jit(solution)/shard_map/ppermute | solution.py:22
  14.2 15.4 %collective-permute-start.1 = (bf16[288,256]{1,0:T(8,128)(2,1)S(1)}, bf16[288,256]{1,0:T(8,128)(2,1)S(1)}, u32[]{:S(2)}, u32[]{:S(2)}) collective-permute-start(bf16[288,256]{1,0:T(8,128)(2,1)S(1)} %pad_maximum_fusion.5), channel_id=1, source_target_pairs={{496,0},{504,8},{0,16},{8,24},{16,32},{24,40},{32,48},{40,56},{48,... | collective-permute-start | bytes 442376 | tf_op jit(solution)/shard_map/ppermute | solution.py:22
  29.6 11.8 %collective-permute-start = (bf16[288,256]{1,0:T(8,128)(2,1)S(1)}, bf16[288,256]{1,0:T(8,128)(2,1)S(1)}, u32[]{:S(2)}, u32[]{:S(2)}) collective-permute-start(bf16[288,256]{1,0:T(8,128)(2,1)S(1)} %pad_maximum_fusion.5), channel_id=1, source_target_pairs={{504,0},{0,8},{8,16},{16,24},{24,32},{32,40},{40,48},{48,56},{56,6... | collective-permute-start | bytes 442376 | tf_op jit(solution)/shard_map/ppermute | solution.py:22
  41.5 4.4 %collective-permute-start.11 = (bf16[640,80]{0,1:T(8,128)(2,1)}, bf16[640,80]{0,1:T(8,128)(2,1)S(1)}, u32[]{:S(2)}, u32[]{:S(2)}) collective-permute-start(bf16[640,80]{0,1:T(8,128)(2,1)} %param.13), channel_id=1, source_target_pairs={{32,0},{64,32},{96,64},{0,96},{33,1},{65,33},{97,65},{1,97},{34,2}... | collective-permute-start | bytes 307208 | tf_op jit(solution)/shard_map/ppermute | solution.py:156
  45.9 2.4 collective-permute-start.12
  50.2 2.2 collective-permute-start.13
  53.3 3.7 %collective-permute-done.13 = bf16[640,80]{0,1:T(8,128)(2,1)S(1)} collective-permute-done((bf16[640,80]{0,1:T(8,128)(2,1)}, bf16[640,80]{0,1:T(8,128)(2,1)S(1)}, u32[]{:S(2)}, u32[]{:S(2)}) %collective-permute-start.13) | collective-permute-done | bytes 102432 | tf_op jit(solution)/shard_map/ppermute | solution.py:156
  59.8 2.8 %collective-permute-start.14 = (bf16[640,4,80]{0,2,1:T(8,128)(2,1)}, bf16[640,4,80]{0,2,1:T(8,128)(2,1)}, u32[]{:S(2)}, u32[]{:S(2)}) collective-permute-start(bf16[640,4,80]{0,2,1:T(8,128)(2,1)} %get-tuple-element.15), channel_id=1, source_target_pairs={{0,16},{16,0},{1,17},{17,1},{2,18},{18,2},{3,19},{19,3},{4,20},{20... | collective-permute-start | bytes 1228808 | tf_op jit(solution)/shard_map/ppermute | solution.py:161
  65.6 3.2 %collective-permute-start.4 = (bf16[1152,256]{1,0:T(8,128)(2,1)}, bf16[1152,256]{1,0:T(8,128)(2,1)}, u32[]{:S(2)}, u32[]{:S(2)}) collective-permute-start(bf16[1152,256]{1,0:T(8,128)(2,1)} %pad_maximum_fusion.1), channel_id=1, source_target_pairs={{448,0},{456,8},{464,16},{472,24},{480,32},{488,40},{496,48},{504,... | collective-permute-start | bytes 1769480 | tf_op jit(solution)/shard_map/ppermute | solution.py:22
  68.8 4.9 %collective-permute-start.5 = (bf16[1152,256]{1,0:T(8,128)(2,1)}, bf16[1152,256]{1,0:T(8,128)(2,1)S(1)}, u32[]{:S(2)}, u32[]{:S(2)}) collective-permute-start(bf16[1152,256]{1,0:T(8,128)(2,1)} %pad_maximum_fusion.1), channel_id=1, source_target_pairs={{416,0},{424,8},{432,16},{440,24},{448,32},{456,40},{464,48},{472,... | collective-permute-start | bytes 1769480 | tf_op jit(solution)/shard_map/ppermute | solution.py:22
  73.8 2.9 %collective-permute-start.6 = (bf16[1,256,256]{2,1,0:T(8,128)(2,1)S(1)}, bf16[1,256,256]{2,1,0:T(8,128)(2,1)}, u32[]{:S(2)}, u32[]{:S(2)}) collective-permute-start(bf16[1,256,256]{2,1,0:T(8,128)(2,1)S(1)} %bitcast.141), channel_id=1, source_target_pairs={{384,0},{392,8},{400,16},{408,24},{416,32},{424,40},{432,48},{440,... | collective-permute-start | bytes 393224 | tf_op jit(solution)/shard_map/ppermute | solution.py:22
  76.7 3.7 %and_and_fusion = pred[256,4352]{0,1:T(8,128)(4,1)S(1)} fusion(s32[256]{0:T(256)S(1)} %iota_add_fusion.1, s32[256]{0:T(256)S(1)} %convert_reduce_fusion.1, s32[4352]{0:T(1024)S(1)} %add.75, s32[4352]{0:T(1024)S(1)} %convert_reduce_fusion, pred[4352]{0:T(1024)(128)(4,1)S(1)} %broadcast_compare_fusion), kind=kLoop, calls=%fused_computation.13 | loop fusion | flops 4456448 | bytes 1155328 | tf_op jit(solution)/shard_map/and | solution.py:94
  80.6 32.0 %collective-permute-done.6 = bf16[1,256,256]{2,1,0:T(8,128)(2,1)} collective-permute-done((bf16[1,256,256]{2,1,0:T(8,128)(2,1)S(1)}, bf16[1,256,256]{2,1,0:T(8,128)(2,1)}, u32[]{:S(2)}, u32[]{:S(2)}) %collective-permute-start.6) | collective-permute-done | bytes 131104 | tf_op jit(solution)/shard_map/ppermute | solution.py:22
  114.1 2.2 maximum_select_fusion
  118.1 2.0 collective-permute-start.7
  120.1 4.5 %collective-permute-start.8 = (bf16[16,32,256]{2,1,0:T(8,128)(2,1)S(1)}, bf16[16,32,256]{2,1,0:T(8,128)(2,1)S(1)}, u32[]{:S(2)}, u32[]{:S(2)}) collective-permute-start(bf16[16,32,256]{2,1,0:T(8,128)(2,1)S(1)} %pad_maximum_fusion.4), channel_id=1, source_target_pairs={{256,0},{264,8},{272,16},{280,24},{288,32},{296,40},{304,48},{312,... | collective-permute-start | bytes 786440 | tf_op jit(solution)/shard_map/ppermute | solution.py:22
  124.6 3.2 %collective-permute-start.9 = (bf16[16,32,256]{2,1,0:T(8,128)(2,1)S(1)}, bf16[16,32,256]{2,1,0:T(8,128)(2,1)S(1)}, u32[]{:S(2)}, u32[]{:S(2)}) collective-permute-start(bf16[16,32,256]{2,1,0:T(8,128)(2,1)S(1)} %pad_maximum_fusion.4), channel_id=1, source_target_pairs={{128,0},{136,8},{144,16},{152,24},{160,32},{168,40},{176,48},{184,... | collective-permute-start | bytes 786440 | tf_op jit(solution)/shard_map/ppermute | solution.py:22
  133.9 10.9 %fusion = (f32[5,256]{1,0:T(8,128)S(1)}, f32[4352,256,5]{1,0,2:T(8,128)}) fusion(pred[256,4352]{0,1:T(8,128)(4,1)S(1)} %and_and_fusion, bf16[256,5,128]{0,2,1:T(8,128)(2,1)S(1)} %bitcast.131, bf16[4352,256]{1,0:T(8,128)(2,1)} %bitcast.151), kind=kOutput, calls=%fused_computation.2 | convolution fusion | flops 1442773760 | bytes 24843264 | tf_op jit(solution)/shard_map/qgd,kd->gqk/dot_general | solution.py:105
  144.8 10.4 %fusion.3 = f32[5,256,128]{1,2,0:T(8,128)S(1)} fusion(f32[4352,256,5]{1,0,2:T(8,128)} %get-tuple-element.23, f32[5,256]{1,0:T(8,128)S(1)} %max.29, pred[256,4352]{0,1:T(8,128)(4,1)S(1)} %and_and_fusion, bf16[4352,256]{1,0:T(8,128)(2,1)S(1)} %bitcast.152), kind=kOutput, calls=%fused_computation.5 | convolution fusion | flops 1453916160 | bytes 25174016 | tf_op jit(solution)/shard_map/gqk,kd->gqd/dot_general | solution.py:109
  155.3 10.3 %fusion.1 = f32[5,256]{1,0:T(8,128)S(1)} fusion(f32[4352,256,5]{1,0,2:T(8,128)} %get-tuple-element.23, f32[5,256]{1,0:T(8,128)S(1)} %max.29, pred[256,4352]{0,1:T(8,128)(4,1)S(1)} %and_and_fusion), kind=kLoop, calls=%fused_computation.3 | loop fusion | flops 27851520 | bytes 23406592 | tf_op jit(solution)/shard_map/reduce_sum | solution.py:126
  170.9 3.3 %collective-permute-start.10 = (bf16[256,640]{0,1:T(8,128)(2,1)S(1)}, bf16[256,640]{0,1:T(8,128)(2,1)S(1)}, u32[]{:S(2)}, u32[]{:S(2)}) collective-permute-start(bf16[256,640]{0,1:T(8,128)(2,1)S(1)} %bitcast.154), channel_id=1, source_target_pairs={{0,8},{8,0},{1,9},{9,1},{2,10},{10,2},{3,11},{11,3},{4,12},{12,4},... | collective-permute-start | bytes 983048 | tf_op jit(solution)/shard_map/ppermute | solution.py:153
  175.5 5.6 %convolution_convert_fusion = bf16[512,2560]{0,1:T(8,128)(2,1)} fusion(bf16[640,2560]{0,1:T(8,128)(2,1)} %all-gather.2.cloned.1.call-done, bf16[256,640]{0,1:T(8,128)(2,1)S(1)} %collective-permute-done.10, bf16[256,640]{0,1:T(8,128)(2,1)S(1)} %bitcast.155), kind=kOutput, calls=%fused_computation.12 | convolution fusion | flops 1680343040 | bytes 6553600 | tf_op jit(solution)/shard_map/dot_general | solution.py:168
  181.1 65.8 %reduce-scatter.2.cloned.1.call-done = bf16[512,320]{0,1:T(8,128)(2,1)} async-done(((bf16[512,2560]{0,1:T(8,128)(2,1)}), bf16[512,320]{0,1:T(8,128)(2,1)}) %reduce-scatter.2.cloned.1.call-update) | async-done | bytes 327696 | tf_op jit(solution)/shard_map/reduce_scatter | solution.py:169
  247.8 6.1 %collective-permute-start.15 = (bf16[256,320]{0,1:T(8,128)(2,1)S(1)}, bf16[256,320]{0,1:T(8,128)(2,1)S(1)}, u32[]{:S(2)}, u32[]{:S(2)}) collective-permute-start(bf16[256,320]{0,1:T(8,128)(2,1)S(1)} %slice.99), channel_id=1, source_target_pairs={{0,8},{8,0},{1,9},{9,1},{2,10},{10,2},{3,11},{11,3},{4,12},{12,4},... | collective-permute-start | bytes 491528 | tf_op jit(solution)/shard_map/ppermute | solution.py:170
  (83 shorter events, 31.4 us)
Async XLA Ops:
  6.5 168.9 %all-gather.2.cloned.1.call-start = ((), (), s32[]{:S(2)}) async-start(), calls=%async_computation.1 | async-start | bytes 4096000 | tf_op jit(solution)/shard_map/all_gather | solution.py:167
  9.7 53.0 %collective-permute-start.2 = (bf16[288,256]{1,0:T(8,128)(2,1)S(1)}, bf16[288,256]{1,0:T(8,128)(2,1)S(1)}, u32[]{:S(2)}, u32[]{:S(2)}) collective-permute-start(bf16[288,256]{1,0:T(8,128)(2,1)S(1)} %pad_maximum_fusion.5), channel_id=1, source_target_pairs={{488,0},{496,8},{504,16},{0,24},{8,32},{16,40},{24,48},{32,56},{40... | collective-permute-start | bytes 442376 | tf_op jit(solution)/shard_map/ppermute | solution.py:22
  14.2 48.5 %collective-permute-start.1 = (bf16[288,256]{1,0:T(8,128)(2,1)S(1)}, bf16[288,256]{1,0:T(8,128)(2,1)S(1)}, u32[]{:S(2)}, u32[]{:S(2)}) collective-permute-start(bf16[288,256]{1,0:T(8,128)(2,1)S(1)} %pad_maximum_fusion.5), channel_id=1, source_target_pairs={{496,0},{504,8},{0,16},{8,24},{16,32},{24,40},{32,48},{40,56},{48,... | collective-permute-start | bytes 442376 | tf_op jit(solution)/shard_map/ppermute | solution.py:22
  29.6 33.0 %collective-permute-start = (bf16[288,256]{1,0:T(8,128)(2,1)S(1)}, bf16[288,256]{1,0:T(8,128)(2,1)S(1)}, u32[]{:S(2)}, u32[]{:S(2)}) collective-permute-start(bf16[288,256]{1,0:T(8,128)(2,1)S(1)} %pad_maximum_fusion.5), channel_id=1, source_target_pairs={{504,0},{0,8},{8,16},{16,24},{24,32},{32,40},{40,48},{48,56},{56,6... | collective-permute-start | bytes 442376 | tf_op jit(solution)/shard_map/ppermute | solution.py:22
  41.5 8.8 %collective-permute-start.11 = (bf16[640,80]{0,1:T(8,128)(2,1)}, bf16[640,80]{0,1:T(8,128)(2,1)S(1)}, u32[]{:S(2)}, u32[]{:S(2)}) collective-permute-start(bf16[640,80]{0,1:T(8,128)(2,1)} %param.13), channel_id=1, source_target_pairs={{32,0},{64,32},{96,64},{0,96},{33,1},{65,33},{97,65},{1,97},{34,2}... | collective-permute-start | bytes 307208 | tf_op jit(solution)/shard_map/ppermute | solution.py:156
  45.9 7.4 %collective-permute-start.12 = (bf16[640,80]{0,1:T(8,128)(2,1)}, bf16[640,80]{0,1:T(8,128)(2,1)S(1)}, u32[]{:S(2)}, u32[]{:S(2)}) collective-permute-start(bf16[640,80]{0,1:T(8,128)(2,1)} %param.13), channel_id=1, source_target_pairs={{64,0},{96,32},{0,64},{32,96},{65,1},{97,33},{1,65},{33,97},{66,2}... | collective-permute-start | bytes 307208 | tf_op jit(solution)/shard_map/ppermute | solution.py:156
  50.2 6.8 %collective-permute-start.13 = (bf16[640,80]{0,1:T(8,128)(2,1)}, bf16[640,80]{0,1:T(8,128)(2,1)S(1)}, u32[]{:S(2)}, u32[]{:S(2)}) collective-permute-start(bf16[640,80]{0,1:T(8,128)(2,1)} %param.13), channel_id=1, source_target_pairs={{96,0},{0,32},{32,64},{64,96},{97,1},{1,33},{33,65},{65,97},{98,2}... | collective-permute-start | bytes 307208 | tf_op jit(solution)/shard_map/ppermute | solution.py:156
  58.0 22.4 %copy-start = (bf16[256,640]{1,0:T(8,128)(2,1)S(1)}, bf16[256,640]{1,0:T(8,128)(2,1)}, u32[]{:S(2)}) copy-start(bf16[256,640]{1,0:T(8,128)(2,1)} %param.8) | copy-start | bytes 983044
  59.8 54.3 %collective-permute-start.14 = (bf16[640,4,80]{0,2,1:T(8,128)(2,1)}, bf16[640,4,80]{0,2,1:T(8,128)(2,1)}, u32[]{:S(2)}, u32[]{:S(2)}) collective-permute-start(bf16[640,4,80]{0,2,1:T(8,128)(2,1)} %get-tuple-element.15), channel_id=1, source_target_pairs={{0,16},{16,0},{1,17},{17,1},{2,18},{18,2},{3,19},{19,3},{4,20},{20... | collective-permute-start | bytes 1228808 | tf_op jit(solution)/shard_map/ppermute | solution.py:161
  63.7 52.6 %collective-permute-start.3 = (bf16[1152,256]{1,0:T(8,128)(2,1)}, bf16[1152,256]{1,0:T(8,128)(2,1)}, u32[]{:S(2)}, u32[]{:S(2)}) collective-permute-start(bf16[1152,256]{1,0:T(8,128)(2,1)} %pad_maximum_fusion.1), channel_id=1, source_target_pairs={{480,0},{488,8},{496,16},{504,24},{0,32},{8,40},{16,48},{24,56},{3... | collective-permute-start | bytes 1769480 | tf_op jit(solution)/shard_map/ppermute | solution.py:22
  65.6 51.6 %collective-permute-start.4 = (bf16[1152,256]{1,0:T(8,128)(2,1)}, bf16[1152,256]{1,0:T(8,128)(2,1)}, u32[]{:S(2)}, u32[]{:S(2)}) collective-permute-start(bf16[1152,256]{1,0:T(8,128)(2,1)} %pad_maximum_fusion.1), channel_id=1, source_target_pairs={{448,0},{456,8},{464,16},{472,24},{480,32},{488,40},{496,48},{504,... | collective-permute-start | bytes 1769480 | tf_op jit(solution)/shard_map/ppermute | solution.py:22
  68.8 49.2 %collective-permute-start.5 = (bf16[1152,256]{1,0:T(8,128)(2,1)}, bf16[1152,256]{1,0:T(8,128)(2,1)S(1)}, u32[]{:S(2)}, u32[]{:S(2)}) collective-permute-start(bf16[1152,256]{1,0:T(8,128)(2,1)} %pad_maximum_fusion.1), channel_id=1, source_target_pairs={{416,0},{424,8},{432,16},{440,24},{448,32},{456,40},{464,48},{472,... | collective-permute-start | bytes 1769480 | tf_op jit(solution)/shard_map/ppermute | solution.py:22
  73.8 38.8 %collective-permute-start.6 = (bf16[1,256,256]{2,1,0:T(8,128)(2,1)S(1)}, bf16[1,256,256]{2,1,0:T(8,128)(2,1)}, u32[]{:S(2)}, u32[]{:S(2)}) collective-permute-start(bf16[1,256,256]{2,1,0:T(8,128)(2,1)S(1)} %bitcast.141), channel_id=1, source_target_pairs={{384,0},{392,8},{400,16},{408,24},{416,32},{424,40},{432,48},{440,... | collective-permute-start | bytes 393224 | tf_op jit(solution)/shard_map/ppermute | solution.py:22
  116.3 130.6 %reduce-scatter.2.cloned.1.call-start = ((), (), s32[]{:S(2)}) async-start(), calls=%async_computation.2 | async-start | bytes 2949120 | tf_op jit(solution)/shard_map/reduce_scatter | solution.py:169
  118.1 48.0 %collective-permute-start.7 = (bf16[16,32,256]{2,1,0:T(8,128)(2,1)S(1)}, bf16[16,32,256]{2,1,0:T(8,128)(2,1)S(1)}, u32[]{:S(2)}, u32[]{:S(2)}) collective-permute-start(bf16[16,32,256]{2,1,0:T(8,128)(2,1)S(1)} %pad_maximum_fusion.4), channel_id=1, source_target_pairs={{384,0},{392,8},{400,16},{408,24},{416,32},{424,40},{432,48},{440,... | collective-permute-start | bytes 786440 | tf_op jit(solution)/shard_map/ppermute | solution.py:22
  120.1 46.0 %collective-permute-start.8 = (bf16[16,32,256]{2,1,0:T(8,128)(2,1)S(1)}, bf16[16,32,256]{2,1,0:T(8,128)(2,1)S(1)}, u32[]{:S(2)}, u32[]{:S(2)}) collective-permute-start(bf16[16,32,256]{2,1,0:T(8,128)(2,1)S(1)} %pad_maximum_fusion.4), channel_id=1, source_target_pairs={{256,0},{264,8},{272,16},{280,24},{288,32},{296,40},{304,48},{312,... | collective-permute-start | bytes 786440 | tf_op jit(solution)/shard_map/ppermute | solution.py:22
  124.6 41.4 %collective-permute-start.9 = (bf16[16,32,256]{2,1,0:T(8,128)(2,1)S(1)}, bf16[16,32,256]{2,1,0:T(8,128)(2,1)S(1)}, u32[]{:S(2)}, u32[]{:S(2)}) collective-permute-start(bf16[16,32,256]{2,1,0:T(8,128)(2,1)S(1)} %pad_maximum_fusion.4), channel_id=1, source_target_pairs={{128,0},{136,8},{144,16},{152,24},{160,32},{168,40},{176,48},{184,... | collective-permute-start | bytes 786440 | tf_op jit(solution)/shard_map/ppermute | solution.py:22
  133.9 10.9 %copy-start.1 = (bf16[17,256,256]{2,1,0:T(8,128)(2,1)S(1)}, bf16[17,256,256]{2,1,0:T(8,128)(2,1)}, u32[]{:S(2)}) copy-start(bf16[17,256,256]{2,1,0:T(8,128)(2,1)} %constant_dynamic-update-slice_fusion.4) | copy-start | bytes 6684676
  170.9 4.5 %collective-permute-start.10 = (bf16[256,640]{0,1:T(8,128)(2,1)S(1)}, bf16[256,640]{0,1:T(8,128)(2,1)S(1)}, u32[]{:S(2)}, u32[]{:S(2)}) collective-permute-start(bf16[256,640]{0,1:T(8,128)(2,1)S(1)} %bitcast.154), channel_id=1, source_target_pairs={{0,8},{8,0},{1,9},{9,1},{2,10},{10,2},{3,11},{11,3},{4,12},{12,4},... | collective-permute-start | bytes 983048 | tf_op jit(solution)/shard_map/ppermute | solution.py:153
  247.8 7.1 %collective-permute-start.15 = (bf16[256,320]{0,1:T(8,128)(2,1)S(1)}, bf16[256,320]{0,1:T(8,128)(2,1)S(1)}, u32[]{:S(2)}, u32[]{:S(2)}) collective-permute-start(bf16[256,320]{0,1:T(8,128)(2,1)S(1)} %slice.99), channel_id=1, source_target_pairs={{0,8},{8,0},{1,9},{9,1},{2,10},{10,2},{3,11},{11,3},{4,12},{12,4},... | collective-permute-start | bytes 491528 | tf_op jit(solution)/shard_map/ppermute | solution.py:170
Sparse Core Ops, SparseCore 0:
  116.4 47.8 all-gather.1
  181.2 65.5 reduce-scatter.1

commit v11 on v9

--- a/solution.py
+++ b/solution.py
@@ -164,7 +164,7 @@
     weight = lax.all_gather(pair.reshape(out_weight.shape[0], -1), BLK[0], axis=1, tiled=True)
     product = jnp.dot(both, weight, preferred_element_type=jnp.float32)
     reduced = lax.psum_scatter(product.astype(jnp.bfloat16), "mp", scatter_dimension=1, tiled=True)
-    other = lax.ppermute(reduced[tok_rows:], "core", swap)
+    other = lax.ppermute(reduced, "core", swap)[tok_rows:]
     mine = reduced[:tok_rows]
     per_block = out_weight.shape[1]
     mine = mine.reshape(tok_rows, -1, per_block)

time: 260 us -> 259 us (level)
  no operation moved by 1% of the time
where the time goes in v11:
time: 259 us; the launch traced here: 258 us
  waiting for transfers between devices  118 us (46%)
  starting transfers between devices  70.1 us (27%)
  matrix products  23.9 us (9%)
  other arithmetic  21.5 us (8%)
  between operations  14.1 us (5%)
  local copies, waits for them, and re-layouts  11 us (4%)
    reduce_scatter x1, waiting for transfers between devices, per_device(): lax.psum_scatter(product.astype(jnp.bfloat16), 'mp', scatter_dimension=1,...  69.9 us
    ppermute x9, starting transfers between devices, shifted(): return lax.ppermute(block, axis, route)  46 us
    ppermute x9, waiting for transfers between devices, shifted(): return lax.ppermute(block, axis, route)  34 us
    dot_general x4, matrix products, weighted(): jnp.einsum('gqk,kd->gqd', weights.astype(jnp.bfloat16), values, preferred...  11.8 us
    ppermute x3, starting transfers between devices, per_device(): lax.ppermute(out_weight, BLK[1], [((i - k) % across, i) for i in range(ac...  10.8 us
    ppermute x1, waiting for transfers between devices, per_device(): partner = lax.ppermute(row, BLK[2], swap)  10.2 us
    reduce_sum x4, other arithmetic, piece(): total = jnp.sum(pre_weights, axis=-1) + jnp.sum(suf_weights, axis=-1)  8.14 us
    dot_general x4, matrix products, scores_of(): jnp.einsum('qgd,kd->gqk', q, keys, preferred_element_type=jnp.float32)  6.48 us
  transfers between devices with their start and end apart: 17, of which 9 were waited for; matrix products, arithmetic and copies ran while one was open for 19% of the time, Pallas kernels for 0%

profile of v11, /device:TPU:1, one launch (start us, length us, event | category | flops | bytes accessed | tf_op | source)
XLA Modules:
  0.0 258.2 jit_solution(913104174961638457)
XLA Ops:
  6.5 5.5 %collective-permute-start.11 = (bf16[640,80]{0,1:T(8,128)(2,1)}, bf16[640,80]{0,1:T(8,128)(2,1)S(1)}, u32[]{:S(2)}, u32[]{:S(2)}) collective-permute-start(bf16[640,80]{0,1:T(8,128)(2,1)} %param.14), channel_id=1, source_target_pairs={{64,0},{96,32},{0,64},{32,96},{65,1},{97,33},{1,65},{33,97},{66,2}... | collective-permute-start | bytes 307208 | tf_op jit(solution)/shard_map/ppermute | solution.py:153
  12.0 2.8 %collective-permute-start.10 = (bf16[640,80]{0,1:T(8,128)(2,1)}, bf16[640,80]{0,1:T(8,128)(2,1)S(1)}, u32[]{:S(2)}, u32[]{:S(2)}) collective-permute-start(bf16[640,80]{0,1:T(8,128)(2,1)} %param.14), channel_id=1, source_target_pairs={{32,0},{64,32},{96,64},{0,96},{33,1},{65,33},{97,65},{1,97},{34,2}... | collective-permute-start | bytes 307208 | tf_op jit(solution)/shard_map/ppermute | solution.py:153
  14.8 2.5 collective-permute-start.12
  20.5 6.9 %collective-permute-start.2 = (bf16[288,256]{1,0:T(8,128)(2,1)S(1)}, bf16[288,256]{1,0:T(8,128)(2,1)S(1)}, u32[]{:S(2)}, u32[]{:S(2)}) collective-permute-start(bf16[288,256]{1,0:T(8,128)(2,1)S(1)} %pad_maximum_fusion.5), channel_id=1, source_target_pairs={{488,0},{496,8},{504,16},{0,24},{8,32},{16,40},{24,48},{32,56},{40... | collective-permute-start | bytes 442376 | tf_op jit(solution)/shard_map/ppermute | solution.py:22
  27.3 12.2 %collective-permute-start.1 = (bf16[288,256]{1,0:T(8,128)(2,1)S(1)}, bf16[288,256]{1,0:T(8,128)(2,1)S(1)}, u32[]{:S(2)}, u32[]{:S(2)}) collective-permute-start(bf16[288,256]{1,0:T(8,128)(2,1)S(1)} %pad_maximum_fusion.5), channel_id=1, source_target_pairs={{496,0},{504,8},{0,16},{8,24},{16,32},{24,40},{32,48},{40,56},{48,... | collective-permute-start | bytes 442376 | tf_op jit(solution)/shard_map/ppermute | solution.py:22
  41.5 11.0 %collective-permute-start = (bf16[288,256]{1,0:T(8,128)(2,1)S(1)}, bf16[288,256]{1,0:T(8,128)(2,1)S(1)}, u32[]{:S(2)}, u32[]{:S(2)}) collective-permute-start(bf16[288,256]{1,0:T(8,128)(2,1)S(1)} %pad_maximum_fusion.5), channel_id=1, source_target_pairs={{504,0},{0,8},{8,16},{16,24},{24,32},{32,40},{40,48},{48,56},{56,6... | collective-permute-start | bytes 442376 | tf_op jit(solution)/shard_map/ppermute | solution.py:22
  55.2 3.0 %collective-permute-start.13 = (bf16[640,4,80]{0,2,1:T(8,128)(2,1)}, bf16[640,4,80]{0,2,1:T(8,128)(2,1)}, u32[]{:S(2)}, u32[]{:S(2)}) collective-permute-start(bf16[640,4,80]{0,2,1:T(8,128)(2,1)} %get-tuple-element.11), channel_id=1, source_target_pairs={{0,16},{16,0},{1,17},{17,1},{2,18},{18,2},{3,19},{19,3},{4,20},{20... | collective-permute-start | bytes 1228808 | tf_op jit(solution)/shard_map/ppermute | solution.py:158
  58.3 13.8 %collective-permute-done = bf16[288,256]{1,0:T(8,128)(2,1)S(1)} collective-permute-done((bf16[288,256]{1,0:T(8,128)(2,1)S(1)}, bf16[288,256]{1,0:T(8,128)(2,1)S(1)}, u32[]{:S(2)}, u32[]{:S(2)}) %collective-permute-start) | collective-permute-done | bytes 147488 | tf_op jit(solution)/shard_map/ppermute | solution.py:22
  75.1 4.8 %collective-permute-start.3 = (bf16[1152,256]{1,0:T(8,128)(2,1)}, bf16[1152,256]{1,0:T(8,128)(2,1)S(1)}, u32[]{:S(2)}, u32[]{:S(2)}) collective-permute-start(bf16[1152,256]{1,0:T(8,128)(2,1)} %pad_maximum_fusion.1), channel_id=1, source_target_pairs={{480,0},{488,8},{496,16},{504,24},{0,32},{8,40},{16,48},{24,56},{3... | collective-permute-start | bytes 1769480 | tf_op jit(solution)/shard_map/ppermute | solution.py:22
  79.9 4.8 %and_and_fusion = pred[256,4096]{0,1:T(8,128)(4,1)} fusion(s32[256]{0:T(256)S(1)} %iota_add_fusion.1, s32[256]{0:T(256)S(1)} %get-tuple-element.6, s32[4096]{0:T(1024)S(1)} %bitcast.173, s32[4096]{0:T(1024)S(1)} %convert_reduce_fusion, pred[4096]{0:T(1024)(128)(4,1)S(1)} %broadcast_compare_fusion), kind=kLoop, calls=%fused_computation.13 | loop fusion | flops 4194304 | bytes 1087488 | tf_op jit(solution)/shard_map/and | solution.py:93
  88.5 10.2 %collective-permute-done.13 = bf16[640,4,80]{0,2,1:T(8,128)(2,1)} collective-permute-done((bf16[640,4,80]{0,2,1:T(8,128)(2,1)}, bf16[640,4,80]{0,2,1:T(8,128)(2,1)}, u32[]{:S(2)}, u32[]{:S(2)}) %collective-permute-start.13) | collective-permute-done | bytes 409632 | tf_op jit(solution)/shard_map/ppermute | solution.py:158
  98.7 2.2 maximum_select_fusion
  100.9 14.9 %collective-permute-done.3 = bf16[1152,256]{1,0:T(8,128)(2,1)S(1)} collective-permute-done((bf16[1152,256]{1,0:T(8,128)(2,1)}, bf16[1152,256]{1,0:T(8,128)(2,1)S(1)}, u32[]{:S(2)}, u32[]{:S(2)}) %collective-permute-start.3) | collective-permute-done | bytes 589856 | tf_op jit(solution)/shard_map/ppermute | solution.py:22
  118.0 2.1 collective-permute-start.8
  120.2 2.9 %collective-permute-start.7 = (bf16[16,32,256]{2,1,0:T(8,128)(2,1)S(1)}, bf16[16,32,256]{2,1,0:T(8,128)(2,1)}, u32[]{:S(2)}, u32[]{:S(2)}) collective-permute-start(bf16[16,32,256]{2,1,0:T(8,128)(2,1)S(1)} %constant_dynamic-update-slice_fusion.4), channel_id=1, source_target_pairs={{256,0},{264,8},{272,16},{280,24},{288,32},{296,40},{304,48},{312,... | collective-permute-start | bytes 786440 | tf_op jit(solution)/shard_map/ppermute | solution.py:22
  123.9 2.4 collective-permute-start.6
  128.1 3.6 %fusion = (f32[5,256]{1,0:T(8,128)S(1)}, f32[4096,256,5]{1,0,2:T(8,128)S(1)}) fusion(pred[256,4096]{0,1:T(8,128)(4,1)S(1)} %copy-done, bf16[256,5,128]{0,2,1:T(8,128)(2,1)S(1)} %bitcast.153, bf16[4096,256]{1,0:T(8,128)(2,1)S(1)} %bitcast.179), kind=kOutput, calls=%fused_computation.2 | convolution fusion | flops 1357904640 | bytes 23401472 | tf_op jit(solution)/shard_map/qgd,kd->gqk/dot_general | solution.py:105
  132.4 8.3 %fusion.3 = f32[5,256,128]{1,2,0:T(8,128)} fusion(f32[4096,256,5]{1,0,2:T(8,128)S(1)} %get-tuple-element.17, f32[5,256]{1,0:T(8,128)} %max.45, pred[256,4096]{0,1:T(8,128)(4,1)} %and_and_fusion, bf16[4096,256]{1,0:T(8,128)(2,1)} %bitcast.180), kind=kOutput, calls=%fused_computation.5 | convolution fusion | flops 1368391680 | bytes 23732224 | tf_op jit(solution)/shard_map/gqk,kd->gqd/dot_general | solution.py:109
  140.7 6.2 %fusion.1 = f32[5,256]{1,0:T(8,128)S(1)} fusion(f32[4096,256,5]{1,0,2:T(8,128)S(1)} %get-tuple-element.17, f32[5,256]{1,0:T(8,128)} %max.45, pred[256,4096]{0,1:T(8,128)(4,1)} %and_and_fusion), kind=kLoop, calls=%fused_computation.3 | loop fusion | flops 26213120 | bytes 22030336 | tf_op jit(solution)/shard_map/reduce_sum | solution.py:119
  147.3 3.2 %collective-permute-done.6 = bf16[768,256]{1,0:T(8,128)(2,1)} collective-permute-done((bf16[768,256]{1,0:T(8,128)(2,1)}, bf16[768,256]{1,0:T(8,128)(2,1)}, u32[]{:S(2)}, u32[]{:S(2)}) %collective-permute-start.6) | collective-permute-done | bytes 393248 | tf_op jit(solution)/shard_map/ppermute | solution.py:22
  160.1 4.7 %collective-permute-start.9 = (bf16[256,640]{0,1:T(8,128)(2,1)S(1)}, bf16[256,640]{0,1:T(8,128)(2,1)S(1)}, u32[]{:S(2)}, u32[]{:S(2)}) collective-permute-start(bf16[256,640]{0,1:T(8,128)(2,1)S(1)} %bitcast.182), channel_id=1, source_target_pairs={{0,8},{8,0},{1,9},{9,1},{2,10},{10,2},{3,11},{11,3},{4,12},{12,4},... | collective-permute-start | bytes 983048 | tf_op jit(solution)/shard_map/ppermute | solution.py:150
  166.9 5.7 %convolution_convert_fusion = bf16[512,2560]{0,1:T(8,128)(2,1)} fusion(bf16[640,2560]{0,1:T(8,128)(2,1)} %all-gather.2.cloned.1.call-done, bf16[256,640]{0,1:T(8,128)(2,1)S(1)} %collective-permute-done.9, bf16[256,640]{0,1:T(8,128)(2,1)S(1)} %bitcast.183), kind=kOutput, calls=%fused_computation.12 | convolution fusion | flops 1680343040 | bytes 6553600 | tf_op jit(solution)/shard_map/dot_general | solution.py:165
  172.6 69.9 %reduce-scatter.2.cloned.1.call-done = bf16[512,320]{0,1:T(8,128)(2,1)} async-done(((bf16[512,2560]{0,1:T(8,128)(2,1)}), bf16[512,320]{0,1:T(8,128)(2,1)}) %reduce-scatter.2.cloned.1.call-update) | async-done | bytes 327696 | tf_op jit(solution)/shard_map/reduce_scatter | solution.py:166
  242.5 5.5 %collective-permute-start.14 = (bf16[512,320]{0,1:T(8,128)(2,1)}, bf16[512,320]{0,1:T(8,128)(2,1)S(1)}, u32[]{:S(2)}, u32[]{:S(2)}) collective-permute-start(bf16[512,320]{0,1:T(8,128)(2,1)} %reduce-scatter.2.cloned.1.call-done), channel_id=1, source_target_pairs={{0,8},{8,0},{1,9},{9,1},{2,10},{10,2},{3,11},{11,3},{4,12},{12,4},... | collective-permute-start | bytes 983048 | tf_op jit(solution)/shard_map/ppermute | solution.py:167
  (103 shorter events, 35.2 us)
Async XLA Ops:
  6.5 160.4 %all-gather.2.cloned.1.call-start = ((), (), s32[]{:S(2)}) async-start(), calls=%async_computation.1 | async-start | bytes 4096000 | tf_op jit(solution)/shard_map/all_gather | solution.py:164
  6.5 45.9 %collective-permute-start.11 = (bf16[640,80]{0,1:T(8,128)(2,1)}, bf16[640,80]{0,1:T(8,128)(2,1)S(1)}, u32[]{:S(2)}, u32[]{:S(2)}) collective-permute-start(bf16[640,80]{0,1:T(8,128)(2,1)} %param.14), channel_id=1, source_target_pairs={{64,0},{96,32},{0,64},{32,96},{65,1},{97,33},{1,65},{33,97},{66,2}... | collective-permute-start | bytes 307208 | tf_op jit(solution)/shard_map/ppermute | solution.py:153
  12.0 29.4 %collective-permute-start.10 = (bf16[640,80]{0,1:T(8,128)(2,1)}, bf16[640,80]{0,1:T(8,128)(2,1)S(1)}, u32[]{:S(2)}, u32[]{:S(2)}) collective-permute-start(bf16[640,80]{0,1:T(8,128)(2,1)} %param.14), channel_id=1, source_target_pairs={{32,0},{64,32},{96,64},{0,96},{33,1},{65,33},{97,65},{1,97},{34,2}... | collective-permute-start | bytes 307208 | tf_op jit(solution)/shard_map/ppermute | solution.py:153
  14.8 37.7 %collective-permute-start.12 = (bf16[640,80]{0,1:T(8,128)(2,1)}, bf16[640,80]{0,1:T(8,128)(2,1)S(1)}, u32[]{:S(2)}, u32[]{:S(2)}) collective-permute-start(bf16[640,80]{0,1:T(8,128)(2,1)} %param.14), channel_id=1, source_target_pairs={{96,0},{0,32},{32,64},{64,96},{97,1},{1,33},{33,65},{65,97},{98,2}... | collective-permute-start | bytes 307208 | tf_op jit(solution)/shard_map/ppermute | solution.py:153
  20.5 37.8 %collective-permute-start.2 = (bf16[288,256]{1,0:T(8,128)(2,1)S(1)}, bf16[288,256]{1,0:T(8,128)(2,1)S(1)}, u32[]{:S(2)}, u32[]{:S(2)}) collective-permute-start(bf16[288,256]{1,0:T(8,128)(2,1)S(1)} %pad_maximum_fusion.5), channel_id=1, source_target_pairs={{488,0},{496,8},{504,16},{0,24},{8,32},{16,40},{24,48},{32,56},{40... | collective-permute-start | bytes 442376 | tf_op jit(solution)/shard_map/ppermute | solution.py:22
  27.3 31.0 %collective-permute-start.1 = (bf16[288,256]{1,0:T(8,128)(2,1)S(1)}, bf16[288,256]{1,0:T(8,128)(2,1)S(1)}, u32[]{:S(2)}, u32[]{:S(2)}) collective-permute-start(bf16[288,256]{1,0:T(8,128)(2,1)S(1)} %pad_maximum_fusion.5), channel_id=1, source_target_pairs={{496,0},{504,8},{0,16},{8,24},{16,32},{24,40},{32,48},{40,56},{48,... | collective-permute-start | bytes 442376 | tf_op jit(solution)/shard_map/ppermute | solution.py:22
  41.5 30.7 %collective-permute-start = (bf16[288,256]{1,0:T(8,128)(2,1)S(1)}, bf16[288,256]{1,0:T(8,128)(2,1)S(1)}, u32[]{:S(2)}, u32[]{:S(2)}) collective-permute-start(bf16[288,256]{1,0:T(8,128)(2,1)S(1)} %pad_maximum_fusion.5), channel_id=1, source_target_pairs={{504,0},{0,8},{8,16},{16,24},{24,32},{32,40},{40,48},{48,56},{56,6... | collective-permute-start | bytes 442376 | tf_op jit(solution)/shard_map/ppermute | solution.py:22
  55.2 43.5 %collective-permute-start.13 = (bf16[640,4,80]{0,2,1:T(8,128)(2,1)}, bf16[640,4,80]{0,2,1:T(8,128)(2,1)}, u32[]{:S(2)}, u32[]{:S(2)}) collective-permute-start(bf16[640,4,80]{0,2,1:T(8,128)(2,1)} %get-tuple-element.11), channel_id=1, source_target_pairs={{0,16},{16,0},{1,17},{17,1},{2,18},{18,2},{3,19},{19,3},{4,20},{20... | collective-permute-start | bytes 1228808 | tf_op jit(solution)/shard_map/ppermute | solution.py:158
  73.1 27.8 %collective-permute-start.4 = (bf16[1152,256]{1,0:T(8,128)(2,1)}, bf16[1152,256]{1,0:T(8,128)(2,1)S(1)}, u32[]{:S(2)}, u32[]{:S(2)}) collective-permute-start(bf16[1152,256]{1,0:T(8,128)(2,1)} %pad_maximum_fusion.1), channel_id=1, source_target_pairs={{448,0},{456,8},{464,16},{472,24},{480,32},{488,40},{496,48},{504,... | collective-permute-start | bytes 1769480 | tf_op jit(solution)/shard_map/ppermute | solution.py:22
  75.1 40.8 %collective-permute-start.3 = (bf16[1152,256]{1,0:T(8,128)(2,1)}, bf16[1152,256]{1,0:T(8,128)(2,1)S(1)}, u32[]{:S(2)}, u32[]{:S(2)}) collective-permute-start(bf16[1152,256]{1,0:T(8,128)(2,1)} %pad_maximum_fusion.1), channel_id=1, source_target_pairs={{480,0},{488,8},{496,16},{504,24},{0,32},{8,40},{16,48},{24,56},{3... | collective-permute-start | bytes 1769480 | tf_op jit(solution)/shard_map/ppermute | solution.py:22
  84.7 33.3 %collective-permute-start.5 = (bf16[1152,256]{1,0:T(8,128)(2,1)}, bf16[1152,256]{1,0:T(8,128)(2,1)S(1)}, u32[]{:S(2)}, u32[]{:S(2)}) collective-permute-start(bf16[1152,256]{1,0:T(8,128)(2,1)} %pad_maximum_fusion.1), channel_id=1, source_target_pairs={{416,0},{424,8},{432,16},{440,24},{448,32},{456,40},{464,48},{472,... | collective-permute-start | bytes 1769480 | tf_op jit(solution)/shard_map/ppermute | solution.py:22
  100.9 141.6 %reduce-scatter.2.cloned.1.call-start = ((), (), s32[]{:S(2)}) async-start(), calls=%async_computation.2 | async-start | bytes 2949120 | tf_op jit(solution)/shard_map/reduce_scatter | solution.py:166
  118.0 33.5 %collective-permute-start.8 = (bf16[16,32,256]{2,1,0:T(8,128)(2,1)S(1)}, bf16[16,32,256]{2,1,0:T(8,128)(2,1)}, u32[]{:S(2)}, u32[]{:S(2)}) collective-permute-start(bf16[16,32,256]{2,1,0:T(8,128)(2,1)S(1)} %constant_dynamic-update-slice_fusion.4), channel_id=1, source_target_pairs={{128,0},{136,8},{144,16},{152,24},{160,32},{168,40},{176,48},{184,... | collective-permute-start | bytes 786440 | tf_op jit(solution)/shard_map/ppermute | solution.py:22
  120.2 31.4 %collective-permute-start.7 = (bf16[16,32,256]{2,1,0:T(8,128)(2,1)S(1)}, bf16[16,32,256]{2,1,0:T(8,128)(2,1)}, u32[]{:S(2)}, u32[]{:S(2)}) collective-permute-start(bf16[16,32,256]{2,1,0:T(8,128)(2,1)S(1)} %constant_dynamic-update-slice_fusion.4), channel_id=1, source_target_pairs={{256,0},{264,8},{272,16},{280,24},{288,32},{296,40},{304,48},{312,... | collective-permute-start | bytes 786440 | tf_op jit(solution)/shard_map/ppermute | solution.py:22
  123.9 26.7 %collective-permute-start.6 = (bf16[768,256]{1,0:T(8,128)(2,1)}, bf16[768,256]{1,0:T(8,128)(2,1)}, u32[]{:S(2)}, u32[]{:S(2)}) collective-permute-start(bf16[768,256]{1,0:T(8,128)(2,1)} %pad_maximum_fusion.3), channel_id=1, source_target_pairs={{384,0},{392,8},{400,16},{408,24},{416,32},{424,40},{432,48},{440,... | collective-permute-start | bytes 1179656 | tf_op jit(solution)/shard_map/ppermute | solution.py:22
  126.5 1.7 copy-start
  126.6 5.1 %copy-start.4 = (bf16[16,256,256]{2,1,0:T(8,128)(2,1)}, bf16[16,256,256]{2,1,0:T(8,128)(2,1)S(1)}, u32[]{:S(2)}) copy-start(bf16[16,256,256]{2,1,0:T(8,128)(2,1)S(1)} %constant_dynamic-update-slice_fusion.11) | copy-start | bytes 6291460
  140.7 6.2 %copy-start.3 = (f32[5,256]{1,0:T(8,128)S(1)}, f32[5,256]{1,0:T(8,128)}, u32[]{:S(2)}) copy-start(f32[5,256]{1,0:T(8,128)} %max.45) | copy-start | bytes 15364
  146.9 5.8 %copy-start.2 = (pred[256,256]{0,1:T(8,128)(4,1)S(1)}, pred[256,256]{0,1:T(8,128)(4,1)}, u32[]{:S(2)}) copy-start(pred[256,256]{0,1:T(8,128)(4,1)} %and_and_fusion.1) | copy-start | bytes 196612
  155.3 1.3 copy-start.1
  160.1 6.0 %collective-permute-start.9 = (bf16[256,640]{0,1:T(8,128)(2,1)S(1)}, bf16[256,640]{0,1:T(8,128)(2,1)S(1)}, u32[]{:S(2)}, u32[]{:S(2)}) collective-permute-start(bf16[256,640]{0,1:T(8,128)(2,1)S(1)} %bitcast.182), channel_id=1, source_target_pairs={{0,8},{8,0},{1,9},{9,1},{2,10},{10,2},{3,11},{11,3},{4,12},{12,4},... | collective-permute-start | bytes 983048 | tf_op jit(solution)/shard_map/ppermute | solution.py:150
  242.5 7.0 %collective-permute-start.14 = (bf16[512,320]{0,1:T(8,128)(2,1)}, bf16[512,320]{0,1:T(8,128)(2,1)S(1)}, u32[]{:S(2)}, u32[]{:S(2)}) collective-permute-start(bf16[512,320]{0,1:T(8,128)(2,1)} %reduce-scatter.2.cloned.1.call-done), channel_id=1, source_target_pairs={{0,8},{8,0},{1,9},{9,1},{2,10},{10,2},{3,11},{11,3},{4,12},{12,4},... | collective-permute-start | bytes 983048 | tf_op jit(solution)/shard_map/ppermute | solution.py:167
Sparse Core Ops, SparseCore 0:
  101.0 65.8 all-gather.1
  172.7 69.7 reduce-scatter.1
